TPU v7x, 512 devices: a whole 4x4x16 slice. The times are simulated.
512 devices in a mesh: gx: 8 (over x, core), gy: 4 (over y), gz: 16 (over z).
Axes of the slice: x: 4, y: 4, z: 16, core: 2. Of those that a mesh axis runs over, the one named last changes fastest.
Arguments:
- multipoles: bfloat16 [289, 262144], P(None, ('gx', 'gy', 'gz')), may hold values from -6 to 6
- up_shift: bfloat16 [8, 289, 289], replicated, may hold values from -0.125 to 0.125
- down_shift: bfloat16 [8, 289, 289], replicated, may hold values from -0.375 to 0.375
- far_shift: bfloat16 [8, 289, 289], replicated, may hold values from -0.09375 to 0.09375
- send_list: int32 [8, 64, 64, 16], P('gx', ('gy', 'gz')), may hold values from 0 to 511
- leaf_src: int32 [16, 262144], P(None, ('gx', 'gy', 'gz')), may hold values from 0 to 1535
- leaf_kind: int32 [16, 262144], P(None, ('gx', 'gy', 'gz')), may hold values from 0 to 7
- coarse_src: int32 [8, 64], replicated, may hold values from 0 to 63
- coarse_kind: int32 [8, 64], replicated, may hold values from 0 to 7
Outputs:
- leaf_local: bfloat16 [289, 262144], P(None, ('gx', 'gy', 'gz'))
All inputs are finite; a program needn't handle non-finite values.
Results may differ from a plain program's by a relative error of at most 0.014.
Values may be sent and summed in bfloat16 or wider, within the bound.
No kernel may reach another device: no remote copies, remote signals or barrier semaphores. Data moves between devices by JAX's collectives and lax.ppermute only.
A program may use at most 128 MiB of HBM per device.

v0:
```python
import jax
import jax.numpy as jnp
from jax import lax
from jax.sharding import PartitionSpec as P

LOCAL_LEVELS = 3


def lift_level(children, up_shift):
    coefs = children.shape[0]
    count = children.shape[1] // 8
    child_stack = children.reshape(coefs, count, 8).transpose(2, 0, 1).reshape(8 * coefs, count)
    shift_table = up_shift.transpose(1, 0, 2).reshape(coefs, 8 * coefs)
    return jnp.dot(shift_table, child_stack, preferred_element_type=jnp.float32)


def lower_level(parent, down_shift):
    coefs = parent.shape[0]
    count = parent.shape[1]
    spread = jnp.dot(
        down_shift.reshape(8 * coefs, coefs), parent, preferred_element_type=jnp.float32
    )
    return spread.reshape(8, coefs, count).transpose(1, 2, 0).reshape(coefs, 8 * count)


def on_device(
    multipoles,
    up_shift,
    down_shift,
    far_shift,
    send_list,
    leaf_src,
    leaf_kind,
    coarse_src,
    coarse_kind,
):
    coefs = multipoles.shape[0]
    kind_count = far_shift.shape[0]
    flat_index = lax.axis_index(("gx", "gy", "gz"))
    coarse_box = flat_index // 8
    octant = flat_index % 8
    peer_count = lax.axis_size(("gy", "gz"))
    slot_count = send_list.shape[3]
    send_order = send_list.reshape(peer_count * slot_count)
    outgoing = jnp.take(multipoles, send_order, axis=1)
    arrived = lax.all_to_all(outgoing, ("gy", "gz"), split_axis=1, concat_axis=1, tiled=True)
    upward = multipoles
    for level in range(LOCAL_LEVELS):
        upward = lift_level(upward, up_shift).astype(jnp.bfloat16)
    every_box = lax.all_gather(upward, ("gx", "gy", "gz"), axis=1, tiled=True)
    coarse_multi = lift_level(every_box, up_shift).astype(jnp.bfloat16)
    coarse_cols = coarse_src[:, coarse_box]
    coarse_kinds = coarse_kind[:, coarse_box]
    list_len = coarse_cols.shape[0]
    coarse_picked = jnp.take(coarse_multi, coarse_cols, axis=1)
    stacked = (
        jnp.take(far_shift, coarse_kinds, axis=0)
        .transpose(1, 0, 2)
        .reshape(coefs, list_len * coefs)
    )
    column_vec = coarse_picked.transpose(1, 0).reshape(list_len * coefs, 1)
    coarse_local = jnp.dot(stacked, column_vec, preferred_element_type=jnp.float32).astype(
        jnp.bfloat16
    )
    downward = jnp.dot(down_shift[octant], coarse_local, preferred_element_type=jnp.float32).astype(
        jnp.bfloat16
    )
    for level in range(LOCAL_LEVELS - 1):
        downward = lower_level(downward, down_shift).astype(jnp.bfloat16)
    chain_part = lower_level(downward, down_shift)
    buffer = jnp.concatenate([multipoles, arrived], axis=1)
    leaf_count = leaf_src.shape[1]
    picked = jnp.take(buffer, leaf_src, axis=1)
    kind_range = jnp.arange(kind_count, dtype=jnp.int32)
    kind_hot = (leaf_kind[None, :, :] == kind_range[:, None, None]).astype(jnp.bfloat16)
    grouped = jnp.einsum("plt,klt->kpt", picked, kind_hot, preferred_element_type=jnp.float32)
    grouped = grouped.reshape(kind_count * coefs, leaf_count)
    upper_part = grouped.astype(jnp.bfloat16)
    lower_part = (grouped - upper_part.astype(jnp.float32)).astype(jnp.bfloat16)
    shift_table = far_shift.transpose(1, 0, 2).reshape(coefs, kind_count * coefs)
    far_total = jnp.dot(shift_table, upper_part, preferred_element_type=jnp.float32)
    far_total = far_total + jnp.dot(shift_table, lower_part, preferred_element_type=jnp.float32)
    return (chain_part + far_total).astype(jnp.bfloat16)


def solution(mesh):
    in_specs = (
        P(None, ("gx", "gy", "gz")),
        P(),
        P(),
        P(),
        P("gx", ("gy", "gz"), None, None),
        P(None, ("gx", "gy", "gz")),
        P(None, ("gx", "gy", "gz")),
        P(),
        P(),
    )
    out_specs = P(None, ("gx", "gy", "gz"))
    return jax.shard_map(
        on_device, mesh=mesh, in_specs=in_specs, out_specs=out_specs, check_vma=False
    )
```

profile of v0, /device:TPU:32, one launch (start us, length us, event | category | flops | bytes accessed | tf_op | source)
XLA Modules:
  0.0 275.0 jit_solution(4691575993083344755)
XLA Ops:
  0.0 0.8 copy.104
  0.8 0.7 compare_and_fusion.1
  1.5 1.2 copy.91
  2.7 0.1 reshape.143
  2.8 0.1 copy.103
  2.9 3.9 %gather_fusion.2 = bf16[1024,289]{1,0:T(8,128)(2,1)S(1)} fusion(bf16[289,512]{0,1:T(8,128)(2,1)S(1)} %copy.91, s32[1024]{0:T(1024)S(1)} %broadcast_clamp_fusion.1), kind=kCustom, calls=%fused_computation.2 | custom fusion | bytes 1187840 | tf_op jit(solution)/shard_map/jit(_take)/gather | solution.py:45
  6.8 0.0 copy-start.9
  6.8 0.0 copy-start.10
  6.8 0.0 copy-start.3
  6.8 1.1 broadcast_select_fusion
  7.9 18.4 %all-to-all-start = ((bf16[289,64,16]{0,2,1:T(8,128)(2,1)}), bf16[289,64,16]{0,2,1:T(8,128)(2,1)S(1)}, u32[]{:S(2)}, u32[]{:S(2)}) async-start(bf16[289,64,16]{0,2,1:T(8,128)(2,1)} %broadcast_select_fusion), calls=%async_computation | async-start | bytes 1572864 | tf_op jit(solution)/shard_map/all_to_all | solution.py:46
  26.3 0.0 copy-done.9
  26.3 0.2 fusion.74
  26.5 0.0 copy-done.10
  26.5 0.2 and_reduce_fusion
  26.8 0.2 fusion.75
  27.0 0.0 copy-done.3
  27.0 3.0 %reshape.137 = bf16[289,2312]{1,0:T(8,128)(2,1)} reshape(bf16[289,8,289]{2,1,0:T(8,128)(2,1)S(1)} %bitcast.160) | data formatting | bytes 2672672 | tf_op jit(solution)/shard_map/reshape | solution.py:13
  29.9 0.7 fusion.45
  30.7 0.6 fusion.57
  31.3 0.1 reshape.185
  31.4 0.0 copy-start.4
  31.4 2.0 convolution_reduce_fusion.1
  33.4 151.1 %all-gather = bf16[512,1,289]{2,1,0:T(2,128)(2,1)S(1)} all-gather(bf16[1,1,289]{2,1,0:T(2,128)(2,1)S(1)} %reshape.178), channel_id=1, replica_groups=mesh['gx'=8,'gy'=4,'gz'=16] {'gx','gy','gz'}, dimensions={0}, use_global_device_ids=true | all-gather | bytes 296514 | tf_op jit(solution)/shard_map/all_gather | solution.py:50
  184.5 0.1 copy.180
  184.6 0.0 copy-start
  184.6 0.0 copy-done.4
  184.6 0.7 fusion.48
  185.4 0.6 gather_fusion.1
  185.9 0.1 select_bitcast_fusion.1
  186.0 0.1 copy-done
  186.1 6.8 %gather_fusion = bf16[8,289,289]{2,0,1:T(8,128)(2,1)} fusion(bf16[8,289,289]{2,0,1:T(8,128)(2,1)S(1)} %copy-done, s32[1024]{0:T(1024)S(1)} %pad_clamp_fusion.1), kind=kCustom, calls=%fused_computation | custom fusion | bytes 2672704 | tf_op jit(solution)/shard_map/jit(_take)/gather | solution.py:57
  192.9 1.8 select_bitcast_fusion
  194.7 0.6 fusion.60
  195.3 4.5 %copy.100 = bf16[8,289,289]{1,0,2:T(8,128)(2,1)} copy(bf16[8,289,289]{2,0,1:T(8,128)(2,1)} %param.11) | data formatting | bytes 2672672 | tf_op args[2]
  199.8 1.9 constant_dynamic-slice_fusion
  201.7 0.2 convolution_reduce_fusion
  202.0 4.1 %reshape.139 = bf16[2312,289]{0,1:T(8,128)(2,1)} reshape(bf16[8,289,289]{1,0,2:T(8,128)(2,1)} %copy.100) | data formatting | bytes 2672672 | tf_op jit(solution)/shard_map/reshape | solution.py:21
  206.0 0.0 copy-start.2
  206.0 2.3 fusion.8
  208.3 0.0 copy-done.2
  208.3 0.3 fusion.4
  208.7 0.1 convert_element_type.88
  208.8 2.6 convolution_bitcast_fusion
  211.4 0.0 copy-start.7
  211.4 0.0 copy-start.8
  211.4 2.4 reshape.140
  213.8 2.2 copy.113
  216.0 0.0 copy-done.7
  216.0 0.0 copy-done.8
  216.0 0.1 copy.101
  216.2 0.2 copy.102
  216.4 3.2 %copy.119 = bf16[289,8,289]{0,1,2:T(8,128)(2,1)} copy(bf16[289,8,289]{2,1,0:T(8,128)(2,1)S(1)} %bitcast.158) | data formatting | bytes 2672672 | tf_op jit(solution)/shard_map/transpose | solution.py:80
  219.5 0.0 all-to-all-done
  219.5 0.1 pad_maximum_fusion
  219.7 33.2 %gather_fusion.3 = bf16[8192,289]{1,0:T(8,128)(2,1)} fusion(bf16[289,1536]{0,1:T(8,128)(2,1)S(1)} %pad_maximum_fusion, s32[8192]{0:T(1024)S(1)} %broadcast_clamp_fusion), kind=kCustom, calls=%fused_computation.3 | custom fusion | bytes 9502720 | tf_op jit(solution)/shard_map/jit(_take)/gather | solution.py:73
  252.9 10.0 %fusion = f32[512,8,289]{2,1,0:T(8,128)} fusion(bf16[16,512,289]{2,1,0:T(8,128)(2,1)} %bitcast.164, pred[16,512]{0,1:T(8,128)(4,1)S(1)} %copy.102, s32[16,512]{0,1:T(8,128)S(1)} %copy.101), kind=kOutput, calls=%fused_computation.4 | convolution fusion | flops 40312832 | bytes 9510912 | tf_op jit(solution)/shard_map/plt,klt->kpt/dot_general | solution.py:76
  262.8 0.0 copy-start.5
  262.8 6.5 %copy.108 = f32[512,8,289]{0,1,2:T(8,128)} copy(f32[512,8,289]{2,1,0:T(8,128)} %fusion) | data formatting | bytes 9469952 | tf_op jit(solution)/shard_map/plt,klt->kpt/dot_general | solution.py:76
  269.3 0.0 copy-done.5
  269.3 3.5 %convolution_bitcast_fusion.1 = f32[512,289]{0,1:T(8,128)S(1)} fusion(bf16[289,8,289]{0,1,2:T(8,128)(2,1)S(1)} %copy-done.5, f32[512,8,289]{0,1,2:T(8,128)} %copy.108), kind=kOutput, calls=%fused_computation.29 | convolution fusion | flops 684204032 | bytes 6663184 | tf_op jit(solution)/shard_map/dot_general | solution.py:81
  272.9 0.2 copy-done.1
  273.1 0.2 copy-done.6
  273.2 1.7 fusion.30
  (13 shorter events, 0.1 us)
Async XLA Ops:
  6.8 19.5 %copy-start.9 = (s32[8,64]{1,0:T(8,128)S(1)}, s32[8,64]{1,0:T(8,128)}, u32[]{:S(2)}) copy-start(s32[8,64]{1,0:T(8,128)} %param.17) | copy-start | bytes 6148
  6.8 19.7 %copy-start.10 = (s32[8,64]{1,0:T(8,128)S(1)}, s32[8,64]{1,0:T(8,128)}, u32[]{:S(2)}) copy-start(s32[8,64]{1,0:T(8,128)} %param.16) | copy-start | bytes 6148
  6.8 20.2 %copy-start.3 = (bf16[8,289,289]{2,0,1:T(8,128)(2,1)S(1)}, bf16[8,289,289]{2,0,1:T(8,128)(2,1)}, u32[]{:S(2)}) copy-start(bf16[8,289,289]{2,0,1:T(8,128)(2,1)} %param.10) | copy-start | bytes 4009012
  7.9 211.6 %all-to-all-start = ((bf16[289,64,16]{0,2,1:T(8,128)(2,1)}), bf16[289,64,16]{0,2,1:T(8,128)(2,1)S(1)}, u32[]{:S(2)}, u32[]{:S(2)}) async-start(bf16[289,64,16]{0,2,1:T(8,128)(2,1)} %broadcast_select_fusion), calls=%async_computation | async-start | bytes 1572864 | tf_op jit(solution)/shard_map/all_to_all | solution.py:46
  31.4 153.2 %copy-start.4 = (bf16[8,289,289]{2,0,1:T(8,128)(2,1)S(1)}, bf16[8,289,289]{2,0,1:T(8,128)(2,1)}, u32[]{:S(2)}) copy-start(bf16[8,289,289]{2,0,1:T(8,128)(2,1)} %param.10) | copy-start | bytes 4009012
  184.6 1.5 copy-start
  206.0 2.3 copy-start.2
  211.4 4.6 %copy-start.7 = (s32[16,512]{1,0:T(8,128)S(1)}, s32[16,512]{1,0:T(8,128)}, u32[]{:S(2)}) copy-start(s32[16,512]{1,0:T(8,128)} %param.14) | copy-start | bytes 98308
  211.4 4.6 %copy-start.8 = (s32[16,512]{1,0:T(8,128)S(1)}, s32[16,512]{1,0:T(8,128)}, u32[]{:S(2)}) copy-start(s32[16,512]{1,0:T(8,128)} %param.15) | copy-start | bytes 98308
  262.8 6.5 %copy-start.5 = (bf16[289,8,289]{0,1,2:T(8,128)(2,1)S(1)}, bf16[289,8,289]{0,1,2:T(8,128)(2,1)}, u32[]{:S(2)}) copy-start(bf16[289,8,289]{0,1,2:T(8,128)(2,1)} %copy.119) | copy-start | bytes 4009012
  269.3 3.8 %copy-start.1 = (f32[512,8,289]{0,1,2:T(8,128)S(1)}, f32[512,8,289]{0,1,2:T(8,128)}, u32[]{:S(2)}) copy-start(f32[512,8,289]{0,1,2:T(8,128)} %copy.108) | copy-start | bytes 14204932
  269.3 3.9 %copy-start.6 = (f32[289,512]{1,0:T(8,128)S(1)}, f32[289,512]{1,0:T(8,128)}, u32[]{:S(2)}) copy-start(f32[289,512]{1,0:T(8,128)} %copy.113) | copy-start | bytes 1775620
where the time goes:
time: 276 us; the launch traced here: 275 us
  blocking collectives  151 us (55%)
  local copies, waits for them, and re-layouts  75.5 us (27%)
  matrix products  25.2 us (9%)
  starting transfers between devices  18.4 us (7%)
  other arithmetic  4.45 us (2%)
    all_gather x1, blocking collectives, on_device(): every_box = lax.all_gather(upward, ('gx', 'gy', 'gz'), axis=1, tiled=True)  151 us
    gather x1, local copies, waits for them, and re-layouts, on_device(): picked = jnp.take(buffer, leaf_src, axis=1)  33.2 us
    all_to_all x1, starting transfers between devices, on_device(): lax.all_to_all(outgoing, ('gy', 'gz'), split_axis=1, concat_axis=1, tiled...  18.4 us
    dot_general x1, matrix products, on_device(): jnp.einsum('plt,klt->kpt', picked, kind_hot, preferred_element_type=jnp.f...  9.96 us
    unnamed x29, local copies, waits for them, and re-layouts  7.11 us
    gather x1, local copies, waits for them, and re-layouts, on_device(): jnp.take(far_shift, coarse_kinds, axis=0).transpose(1, 0, 2)  6.81 us
    dot_general x1, local copies, waits for them, and re-layouts, on_device(): jnp.einsum('plt,klt->kpt', picked, kind_hot, preferred_element_type=jnp.f...  6.5 us
  transfers between devices with their start and end apart: 1, of which 0 were waited for; matrix products, arithmetic and copies ran while one was open for 15% of the time, Pallas kernels for 0%

commit v1 on v0

--- a/solution.py
+++ b/solution.py
@@ -21,6 +21,14 @@
         down_shift.reshape(8 * coefs, coefs), parent, preferred_element_type=jnp.float32
     )
     return spread.reshape(8, coefs, count).transpose(1, 2, 0).reshape(coefs, 8 * count)
+
+
+def gather_columns(column_block, axes):
+    group = lax.axis_size(axes)
+    width = column_block.shape[1]
+    spread = jnp.broadcast_to(column_block[:, None, :], (column_block.shape[0], group, width))
+    spread = spread.reshape(column_block.shape[0], group * width)
+    return lax.all_to_all(spread, axes, split_axis=1, concat_axis=1, tiled=True)
 
 
 def on_device(
@@ -47,8 +55,9 @@
     upward = multipoles
     for level in range(LOCAL_LEVELS):
         upward = lift_level(upward, up_shift).astype(jnp.bfloat16)
-    every_box = lax.all_gather(upward, ("gx", "gy", "gz"), axis=1, tiled=True)
-    coarse_multi = lift_level(every_box, up_shift).astype(jnp.bfloat16)
+    row_boxes = gather_columns(upward, "gz")
+    row_multi = lift_level(row_boxes, up_shift).astype(jnp.bfloat16)
+    coarse_multi = gather_columns(row_multi, ("gx", "gy"))
     coarse_cols = coarse_src[:, coarse_box]
     coarse_kinds = coarse_kind[:, coarse_box]
     list_len = coarse_cols.shape[0]

time: 276 us -> 160 us (0.58)
  the two profiles are of different devices: /device:TPU:32 before, /device:TPU:8 now
where the time goes in v1:
time: 160 us; the launch traced here: 159 us
  local copies, waits for them, and re-layouts  74.7 us (47%)
  starting transfers between devices  30.2 us (19%)
  matrix products  26.7 us (17%)
  waiting for transfers between devices  22.3 us (14%)
  other arithmetic  4.96 us (3%)
    gather x1, local copies, waits for them, and re-layouts, on_device(): picked = jnp.take(buffer, leaf_src, axis=1)  33.2 us
    all_to_all x2, starting transfers between devices, gather_columns(): return lax.all_to_all(spread, axes, split_axis=1, concat_axis=1, tiled=True)  22.7 us
    all_to_all x2, waiting for transfers between devices, gather_columns(): return lax.all_to_all(spread, axes, split_axis=1, concat_axis=1, tiled=True)  13.4 us
    dot_general x1, matrix products, on_device(): jnp.einsum('plt,klt->kpt', picked, kind_hot, preferred_element_type=jnp.f...  9.96 us
    all_to_all x1, waiting for transfers between devices, on_device(): lax.all_to_all(outgoing, ('gy', 'gz'), split_axis=1, concat_axis=1, tiled...  8.93 us
    all_to_all x1, starting transfers between devices, on_device(): lax.all_to_all(outgoing, ('gy', 'gz'), split_axis=1, concat_axis=1, tiled...  7.45 us
    gather x1, local copies, waits for them, and re-layouts, on_device(): jnp.take(far_shift, coarse_kinds, axis=0).transpose(1, 0, 2)  6.81 us
    dot_general x1, local copies, waits for them, and re-layouts, on_device(): jnp.einsum('plt,klt->kpt', picked, kind_hot, preferred_element_type=jnp.f...  6.5 us
  transfers between devices with their start and end apart: 3, of which 3 were waited for; matrix products, arithmetic and copies ran while one was open for 24% of the time, Pallas kernels for 0%

profile of v1, /device:TPU:8, one launch (start us, length us, event | category | flops | bytes accessed | tf_op | source)
XLA Modules:
  0.0 159.2 jit_solution(3946871346502079837)
XLA Ops:
  0.0 1.2 copy.69
  1.2 0.0 copy-start.4
  1.2 4.2 %reshape.156 = bf16[289,2312]{1,0:T(8,128)(2,1)} reshape(bf16[289,8,289]{2,1,0:T(8,128)(2,1)} %bitcast.158) | data formatting | bytes 2672672 | tf_op jit(solution)/shard_map/reshape | solution.py:13
  5.4 0.0 copy-done.4
  5.4 0.7 fusion.39
  6.1 0.0 copy-start.10
  6.2 0.6 fusion.48
  6.7 0.1 reshape.200
  6.9 1.9 %convolution_reduce_fusion.1 = bf16[289]{0:T(512)(128)(2,1)S(1)} fusion(bf16[2312,1]{0,1:T(2,128)(2,1)S(1)} %reshape.200, bf16[289,2312]{1,0:T(8,128)(2,1)} %reshape.156), kind=kOutput, calls=%fused_computation.45 | convolution fusion | flops 1336336 | bytes 1341538 | tf_op jit(solution)/shard_map/dot_general | solution.py:14
  8.7 0.6 reshape.157
  9.4 15.2 %all-to-all-start = ((bf16[289,16,1]{0,2,1:T(2,128)(2,1)}), bf16[289,16,1]{0,2,1:T(2,128)(2,1)S(1)}, u32[]{:S(2)}, u32[]{:S(2)}) async-start(bf16[289,16,1]{0,2,1:T(2,128)(2,1)} %reshape.157), calls=%async_computation | async-start | bytes 49152 | tf_op jit(solution)/shard_map/all_to_all | solution.py:31
  24.6 0.0 copy-done.10
  24.6 0.1 copy.80
  24.7 0.1 reshape.163
  24.8 3.9 %gather_fusion.2 = bf16[1024,289]{1,0:T(8,128)(2,1)S(1)} fusion(bf16[289,512]{0,1:T(8,128)(2,1)S(1)} %copy.69, s32[1024]{0:T(1024)S(1)} %broadcast_clamp_fusion.1), kind=kCustom, calls=%fused_computation.2 | custom fusion | bytes 1187840 | tf_op jit(solution)/shard_map/jit(_take)/gather | solution.py:53
  28.7 0.1 copy.79
  28.8 0.0 copy-start.8
  28.8 1.1 broadcast_select_fusion
  29.9 7.2 %all-to-all-done = bf16[289,16,1]{0,2,1:T(2,128)(2,1)S(1)} async-done(((bf16[289,16,1]{0,2,1:T(2,128)(2,1)}), bf16[289,16,1]{0,2,1:T(2,128)(2,1)S(1)}, u32[]{:S(2)}, u32[]{:S(2)}) %all-to-all-start) | async-done | bytes 9280 | tf_op jit(solution)/shard_map/all_to_all | solution.py:31
  37.1 2.2 %fusion.60 = bf16[289,2]{0,1:T(2,128)(2,1)S(1)} fusion(bf16[289,8,289]{2,1,0:T(8,128)(2,1)} %bitcast.159, bf16[289,2,8]{0,2,1:T(8,128)(2,1)S(1)} %bitcast.168), kind=kOutput, calls=%fused_computation.46 | convolution fusion | flops 2673250 | bytes 1346740 | tf_op jit(solution)/shard_map/dot_general | solution.py:14
  39.3 0.7 broadcast_in_dim.57
  40.0 7.5 %all-to-all-start.1 = ((bf16[289,32,2]{0,2,1:T(2,128)(2,1)}), bf16[289,32,2]{0,2,1:T(2,128)(2,1)S(1)}, u32[]{:S(2)}, u32[]{:S(2)}) async-start(bf16[289,32,2]{0,2,1:T(2,128)(2,1)} %broadcast_in_dim.57), calls=%async_computation.1 | async-start | bytes 98304 | tf_op jit(solution)/shard_map/all_to_all | solution.py:31
  47.5 0.0 copy-done.8
  47.6 6.2 %all-to-all-done.1 = bf16[289,32,2]{0,2,1:T(2,128)(2,1)S(1)} async-done(((bf16[289,32,2]{0,2,1:T(2,128)(2,1)}), bf16[289,32,2]{0,2,1:T(2,128)(2,1)S(1)}, u32[]{:S(2)}, u32[]{:S(2)}) %all-to-all-start.1) | async-done | bytes 37024 | tf_op jit(solution)/shard_map/all_to_all | solution.py:31
  53.7 7.5 %all-to-all-start.2 = ((bf16[289,64,16]{0,2,1:T(8,128)(2,1)}), bf16[289,64,16]{0,2,1:T(8,128)(2,1)S(1)}, u32[]{:S(2)}, u32[]{:S(2)}) async-start(bf16[289,64,16]{0,2,1:T(8,128)(2,1)} %broadcast_select_fusion), calls=%async_computation.2 | async-start | bytes 1572864 | tf_op jit(solution)/shard_map/all_to_all | solution.py:54
  61.2 0.0 copy-done.3
  61.2 3.1 %copy.76 = bf16[8,289,289]{1,0,2:T(8,128)(2,1)} copy(bf16[8,289,289]{2,0,1:T(8,128)(2,1)S(1)} %copy-done.3) | data formatting | bytes 2672672 | tf_op args[2]
  64.4 4.2 %reshape.159 = bf16[2312,289]{0,1:T(8,128)(2,1)} reshape(bf16[8,289,289]{1,0,2:T(8,128)(2,1)} %copy.76) | data formatting | bytes 2672672 | tf_op jit(solution)/shard_map/reshape | solution.py:21
  68.6 0.0 copy-done.9
  68.6 0.8 copy.77
  69.5 0.2 copy.78
  69.7 0.0 copy-done.11
  69.7 0.2 fusion.74
  69.9 0.0 copy-done
  69.9 6.8 %gather_fusion = bf16[8,289,289]{2,0,1:T(8,128)(2,1)} fusion(bf16[8,289,289]{2,0,1:T(8,128)(2,1)S(1)} %copy-done, s32[1024]{0:T(1024)S(1)} %pad_clamp_fusion.1), kind=kCustom, calls=%fused_computation | custom fusion | bytes 2672704 | tf_op jit(solution)/shard_map/jit(_take)/gather | solution.py:66
  76.7 3.2 %copy.95 = bf16[289,8,289]{0,1,2:T(8,128)(2,1)} copy(bf16[289,8,289]{2,1,0:T(8,128)(2,1)S(1)} %bitcast.156) | data formatting | bytes 2672672 | tf_op jit(solution)/shard_map/transpose | solution.py:89
  79.8 0.0 copy-done.12
  79.8 0.2 fusion.75
  80.0 0.2 and_reduce_fusion
  80.3 1.9 %constant_dynamic-slice_fusion = bf16[1,289,289]{2,0,1:T(2,128)(2,1)S(1)} fusion(bf16[8,289,289]{2,0,1:T(8,128)(2,1)} %param.11, s32[]{:T(128)S(6)} %select_n.79), kind=kLoop, calls=%fused_computation.77 | loop fusion | bytes 334088 | tf_op jit(solution)/shard_map/dynamic_slice | solution.py:74
  82.2 3.0 %select_bitcast_fusion = bf16[289,8,289]{2,1,0:T(8,128)(2,1)} fusion(bf16[8,289,289]{2,0,1:T(8,128)(2,1)} %gather_fusion, pred[8]{0:T(512)(128)(4,1)S(1)} %get-tuple-element.6), kind=kLoop, calls=%fused_computation.21 | loop fusion | flops 668168 | bytes 2672680 | tf_op jit(solution)/shard_map/jit(_take)/select_n | solution.py:66
  85.3 0.6 gather_fusion.1
  85.9 0.1 select_bitcast_fusion.1
  85.9 2.2 %fusion.57 = bf16[289]{0:T(512)(128)(2,1)S(1)} fusion(bf16[289,8,289]{2,1,0:T(8,128)(2,1)} %select_bitcast_fusion, bf16[8,289,1]{1,0,2:T(8,128)(2,1)S(1)} %select_bitcast_fusion.1), kind=kOutput, calls=%fused_computation.43 | convolution fusion | flops 1336336 | bytes 1341538 | tf_op jit(solution)/shard_map/dot_general | solution.py:71
  88.2 0.2 convolution_reduce_fusion
  88.4 2.2 %fusion.8 = bf16[1,8,289]{2,0,1:T(2,128)(2,1)S(1)} fusion(bf16[289,1,1]{0,1,2:T(2,128)(2,1)S(1)} %reshape.207, bf16[8,289,289]{2,0,1:T(8,128)(2,1)} %param.11), kind=kOutput, calls=%fused_computation.17 | convolution fusion | flops 1336336 | bytes 1341538 | tf_op jit(solution)/shard_map/dot_general | solution.py:20
  90.5 0.0 copy-done.2
  90.5 0.3 fusion.4
  90.9 0.1 convert_element_type.85
  91.0 1.2 convolution_bitcast_fusion
  92.2 1.5 reshape.160
  93.7 1.1 copy.89
  94.8 8.9 %all-to-all-done.2 = bf16[289,64,16]{0,2,1:T(8,128)(2,1)S(1)} async-done(((bf16[289,64,16]{0,2,1:T(8,128)(2,1)}), bf16[289,64,16]{0,2,1:T(8,128)(2,1)S(1)}, u32[]{:S(2)}, u32[]{:S(2)}) %all-to-all-start.2) | async-done | bytes 591904 | tf_op jit(solution)/shard_map/all_to_all | solution.py:54
  103.8 0.1 pad_maximum_fusion
  103.9 0.0 copy-start.7
  103.9 33.2 %gather_fusion.3 = bf16[8192,289]{1,0:T(8,128)(2,1)} fusion(bf16[289,1536]{0,1:T(8,128)(2,1)S(1)} %pad_maximum_fusion, s32[8192]{0:T(1024)S(1)} %broadcast_clamp_fusion), kind=kCustom, calls=%fused_computation.3 | custom fusion | bytes 9502720 | tf_op jit(solution)/shard_map/jit(_take)/gather | solution.py:82
  137.1 0.0 copy-done.7
  137.1 10.0 %fusion = f32[512,8,289]{2,1,0:T(8,128)} fusion(bf16[16,512,289]{2,1,0:T(8,128)(2,1)} %bitcast.162, pred[16,512]{0,1:T(8,128)(4,1)S(1)} %copy.78, s32[16,512]{0,1:T(8,128)S(1)} %copy-done.7), kind=kOutput, calls=%fused_computation.4 | convolution fusion | flops 40312832 | bytes 9510912 | tf_op jit(solution)/shard_map/plt,klt->kpt/dot_general | solution.py:85
  147.1 6.5 %copy.84 = f32[512,8,289]{0,1,2:T(8,128)} copy(f32[512,8,289]{2,1,0:T(8,128)} %fusion) | data formatting | bytes 9469952 | tf_op jit(solution)/shard_map/plt,klt->kpt/dot_general | solution.py:85
  153.6 0.0 copy-done.5
  153.6 3.5 %convolution_bitcast_fusion.1 = f32[512,289]{0,1:T(8,128)S(1)} fusion(bf16[289,8,289]{0,1,2:T(8,128)(2,1)S(1)} %copy-done.5, f32[512,8,289]{0,1,2:T(8,128)} %copy.84), kind=kOutput, calls=%fused_computation.29 | convolution fusion | flops 684204032 | bytes 6663184 | tf_op jit(solution)/shard_map/dot_general | solution.py:90
  157.1 0.2 copy-done.1
  157.3 0.2 copy-done.6
  157.5 1.7 %fusion.30 = bf16[289,512]{1,0:T(8,128)(2,1)} fusion(f32[289,512]{1,0:T(8,128)S(1)} %copy-done.6, f32[512,289]{0,1:T(8,128)S(1)} %convolution_bitcast_fusion.1, bf16[289,8,289]{0,1,2:T(8,128)(2,1)S(1)} %copy-done.5, f32[512,8,289]{0,1,2:T(8,128)S(1)} %copy-done.1), kind=kOutput, calls=%fused_computation.33 | convolution fusion | flops 689382912 | bytes 7550992 | tf_op jit(solution)/shard_map/dot_general | solution.py:91
  (22 shorter events, 0.1 us)
Async XLA Ops:
  1.2 4.2 %copy-start.4 = (bf16[8,289,289]{2,0,1:T(8,128)(2,1)S(1)}, bf16[8,289,289]{2,0,1:T(8,128)(2,1)}, u32[]{:S(2)}) copy-start(bf16[8,289,289]{2,0,1:T(8,128)(2,1)} %param.10) | copy-start | bytes 4009012
  6.1 18.4 %copy-start.10 = (s32[1,1,64,16]{2,3,1,0:T(8,128)S(1)}, s32[1,1,64,16]{2,3,1,0:T(8,128)}, u32[]{:S(2)}) copy-start(s32[1,1,64,16]{2,3,1,0:T(8,128)} %param.13) | copy-start | bytes 12292
  9.4 27.8 %all-to-all-start = ((bf16[289,16,1]{0,2,1:T(2,128)(2,1)}), bf16[289,16,1]{0,2,1:T(2,128)(2,1)S(1)}, u32[]{:S(2)}, u32[]{:S(2)}) async-start(bf16[289,16,1]{0,2,1:T(2,128)(2,1)} %reshape.157), calls=%async_computation | async-start | bytes 49152 | tf_op jit(solution)/shard_map/all_to_all | solution.py:31
  28.8 18.7 %copy-start.8 = (s32[16,512]{1,0:T(8,128)S(1)}, s32[16,512]{1,0:T(8,128)}, u32[]{:S(2)}) copy-start(s32[16,512]{1,0:T(8,128)} %param.14) | copy-start | bytes 98308
  37.1 24.1 %copy-start.3 = (bf16[8,289,289]{2,0,1:T(8,128)(2,1)S(1)}, bf16[8,289,289]{2,0,1:T(8,128)(2,1)}, u32[]{:S(2)}) copy-start(bf16[8,289,289]{2,0,1:T(8,128)(2,1)} %param.11) | copy-start | bytes 4009012
  40.0 13.7 %all-to-all-start.1 = ((bf16[289,32,2]{0,2,1:T(2,128)(2,1)}), bf16[289,32,2]{0,2,1:T(2,128)(2,1)S(1)}, u32[]{:S(2)}, u32[]{:S(2)}) async-start(bf16[289,32,2]{0,2,1:T(2,128)(2,1)} %broadcast_in_dim.57), calls=%async_computation.1 | async-start | bytes 98304 | tf_op jit(solution)/shard_map/all_to_all | solution.py:31
  53.7 50.0 %all-to-all-start.2 = ((bf16[289,64,16]{0,2,1:T(8,128)(2,1)}), bf16[289,64,16]{0,2,1:T(8,128)(2,1)S(1)}, u32[]{:S(2)}, u32[]{:S(2)}) async-start(bf16[289,64,16]{0,2,1:T(8,128)(2,1)} %broadcast_select_fusion), calls=%async_computation.2 | async-start | bytes 1572864 | tf_op jit(solution)/shard_map/all_to_all | solution.py:54
  64.4 4.2 %copy-start.9 = (s32[16,512]{1,0:T(8,128)S(1)}, s32[16,512]{1,0:T(8,128)}, u32[]{:S(2)}) copy-start(s32[16,512]{1,0:T(8,128)} %param.15) | copy-start | bytes 98308
  64.4 5.3 %copy-start.11 = (s32[8,64]{1,0:T(8,128)S(1)}, s32[8,64]{1,0:T(8,128)}, u32[]{:S(2)}) copy-start(s32[8,64]{1,0:T(8,128)} %param.17) | copy-start | bytes 6148
  64.4 5.5 %copy-start = (bf16[8,289,289]{2,0,1:T(8,128)(2,1)S(1)}, bf16[8,289,289]{2,0,1:T(8,128)(2,1)}, u32[]{:S(2)}) copy-start(bf16[8,289,289]{2,0,1:T(8,128)(2,1)} %param.12) | copy-start | bytes 4009012
  76.7 3.2 %copy-start.12 = (s32[8,64]{1,0:T(8,128)S(1)}, s32[8,64]{1,0:T(8,128)}, u32[]{:S(2)}) copy-start(s32[8,64]{1,0:T(8,128)} %param.16) | copy-start | bytes 6148
  85.9 4.6 %copy-start.2 = (bf16[2312,289]{0,1:T(8,128)(2,1)S(1)}, bf16[2312,289]{0,1:T(8,128)(2,1)}, u32[]{:S(2)}) copy-start(bf16[2312,289]{0,1:T(8,128)(2,1)} %reshape.159) | copy-start | bytes 4009012
  103.9 33.2 %copy-start.7 = (s32[16,512]{0,1:T(8,128)S(1)}, s32[16,512]{0,1:T(8,128)}, u32[]{:S(2)}) copy-start(s32[16,512]{0,1:T(8,128)} %copy.77) | copy-start | bytes 98308
  147.0 6.5 %copy-start.5 = (bf16[289,8,289]{0,1,2:T(8,128)(2,1)S(1)}, bf16[289,8,289]{0,1,2:T(8,128)(2,1)}, u32[]{:S(2)}) copy-start(bf16[289,8,289]{0,1,2:T(8,128)(2,1)} %copy.95) | copy-start | bytes 4009012
  153.6 3.8 %copy-start.1 = (f32[512,8,289]{0,1,2:T(8,128)S(1)}, f32[512,8,289]{0,1,2:T(8,128)}, u32[]{:S(2)}) copy-start(f32[512,8,289]{0,1,2:T(8,128)} %copy.84) | copy-start | bytes 14204932
  153.6 3.9 %copy-start.6 = (f32[289,512]{1,0:T(8,128)S(1)}, f32[289,512]{1,0:T(8,128)}, u32[]{:S(2)}) copy-start(f32[289,512]{1,0:T(8,128)} %copy.89) | copy-start | bytes 1775620

commit v2 on v1

--- a/solution.py
+++ b/solution.py
@@ -1,9 +1,12 @@
 import jax
 import jax.numpy as jnp
 from jax import lax
+from jax.experimental import pallas as pl
+from jax.experimental.pallas import tpu as pltpu
 from jax.sharding import PartitionSpec as P
 
 LOCAL_LEVELS = 3
+LANES = 384
 
 
 def lift_level(children, up_shift):
@@ -21,6 +24,49 @@
         down_shift.reshape(8 * coefs, coefs), parent, preferred_element_type=jnp.float32
     )
     return spread.reshape(8, coefs, count).transpose(1, 2, 0).reshape(coefs, 8 * count)
+
+
+def far_kernel(idx_ref, buf_ref, fs_ref, out_ref, table_ref):
+    kinds = fs_ref.shape[0]
+    rows = buf_ref.shape[0]
+    for k in range(kinds):
+        table_ref[pl.ds(k * rows, rows), :] = jnp.dot(
+            buf_ref[...], fs_ref[k], preferred_element_type=jnp.float32
+        )
+    targets = out_ref.shape[0]
+    lists = idx_ref.shape[0] // targets
+
+    def body(t, carry):
+        base = t * lists
+        acc = table_ref[pl.ds(idx_ref[base], 1), :]
+        for l in range(1, lists):
+            acc = acc + table_ref[pl.ds(idx_ref[base + l], 1), :]
+        out_ref[pl.ds(t, 1), :] = acc
+        return carry
+
+    lax.fori_loop(0, targets, body, 0)
+
+
+def far_field(buffer, far_shift, leaf_src, leaf_kind):
+    coefs, rows = buffer.shape
+    kinds = far_shift.shape[0]
+    lists, targets = leaf_src.shape
+    pad = LANES - coefs
+    buf_t = jnp.pad(buffer.T, ((0, 0), (0, pad)))
+    fs_t = jnp.pad(far_shift.transpose(0, 2, 1), ((0, 0), (0, pad), (0, pad)))
+    idx = (leaf_kind * rows + leaf_src).T.reshape(lists * targets)
+    out = pl.pallas_call(
+        far_kernel,
+        out_shape=jax.ShapeDtypeStruct((targets, LANES), jnp.float32),
+        in_specs=[
+            pl.BlockSpec(memory_space=pltpu.SMEM),
+            pl.BlockSpec(memory_space=pltpu.VMEM),
+            pl.BlockSpec(memory_space=pltpu.VMEM),
+        ],
+        out_specs=pl.BlockSpec(memory_space=pltpu.VMEM),
+        scratch_shapes=[pltpu.VMEM((kinds * rows, LANES), jnp.float32)],
+    )(idx, buf_t, fs_t)
+    return out[:, :coefs].T
 
 
 def gather_columns(column_block, axes):
@@ -43,7 +89,6 @@
     coarse_kind,
 ):
     coefs = multipoles.shape[0]
-    kind_count = far_shift.shape[0]
     flat_index = lax.axis_index(("gx", "gy", "gz"))
     coarse_box = flat_index // 8
     octant = flat_index % 8
@@ -78,17 +123,7 @@
         downward = lower_level(downward, down_shift).astype(jnp.bfloat16)
     chain_part = lower_level(downward, down_shift)
     buffer = jnp.concatenate([multipoles, arrived], axis=1)
-    leaf_count = leaf_src.shape[1]
-    picked = jnp.take(buffer, leaf_src, axis=1)
-    kind_range = jnp.arange(kind_count, dtype=jnp.int32)
-    kind_hot = (leaf_kind[None, :, :] == kind_range[:, None, None]).astype(jnp.bfloat16)
-    grouped = jnp.einsum("plt,klt->kpt", picked, kind_hot, preferred_element_type=jnp.float32)
-    grouped = grouped.reshape(kind_count * coefs, leaf_count)
-    upper_part = grouped.astype(jnp.bfloat16)
-    lower_part = (grouped - upper_part.astype(jnp.float32)).astype(jnp.bfloat16)
-    shift_table = far_shift.transpose(1, 0, 2).reshape(coefs, kind_count * coefs)
-    far_total = jnp.dot(shift_table, upper_part, preferred_element_type=jnp.float32)
-    far_total = far_total + jnp.dot(shift_table, lower_part, preferred_element_type=jnp.float32)
+    far_total = far_field(buffer, far_shift, leaf_src, leaf_kind)
     return (chain_part + far_total).astype(jnp.bfloat16)
 
 

time: 160 us -> 132 us (0.82)
  local copies, waits for them, and re-layouts: 74.7 us -> 39.4 us
  Pallas kernels: 0 us -> 26.8 us
  matrix products: 26.7 us -> 9.87 us
    gather x1 -> x0, local copies, waits for them, and re-layouts: 33.2 us -> none  [on_device(): picked = jnp.take(buffer, leaf_src, axis=1)]
    pallas_call x0 -> x1, Pallas kernels: none -> 26.8 us  [far_field(): pl.pallas_call(far_kernel, out_shape=jax.ShapeDtypeStruct((targets, LANES...]
    dot_general x3 -> x0, matrix products: 15.2 us -> none  [the longest x1 9.96 us: on_device(): jnp.einsum('plt,klt->kpt', picked, kind_hot, preferred_element_type=jnp.f...]
    dot_general x1 -> x0, local copies, waits for them, and re-layouts: 6.5 us -> none  [on_device(): jnp.einsum('plt,klt->kpt', picked, kind_hot, preferred_element_type=jnp.f...]
    pad x0 -> x2, local copies, waits for them, and re-layouts: none -> 4.47 us  [the longest x1 3.32 us: far_field(): fs_t = jnp.pad(far_shift.transpose(0, 2, 1), ((0, 0), (0, pad), (0, pad)))]
    transpose x1, local copies, waits for them, and re-layouts: 3.16 us -> 0.12 us  [far_field(): idx = (leaf_kind * rows + leaf_src).T.reshape(lists * targets)]
    unnamed x32 -> x23, local copies, waits for them, and re-layouts: 5.69 us -> 8.28 us
    dot_general x4, matrix products: 5.36 us -> 3.76 us  [lift_level(): return jnp.dot(shift_table, child_stack, preferred_element_type=jnp.float32)]
  transfers between devices with their start and end apart: 3 -> 3, of which waited for: 3 -> 3; matrix products, arithmetic and copies ran while one was open for 24% -> 30% of each run, Pallas kernels for 0% -> 0%
where the time goes in v2:
time: 132 us; the launch traced here: 131 us
  local copies, waits for them, and re-layouts  39.4 us (30%)
  starting transfers between devices  29.1 us (22%)
  Pallas kernels  26.8 us (20%)
  waiting for transfers between devices  21.2 us (16%)
  matrix products  9.87 us (7%)
  other arithmetic  4.69 us (4%)
    pallas_call x1, Pallas kernels, far_field(): pl.pallas_call(far_kernel, out_shape=jax.ShapeDtypeStruct((targets, LANES...  26.8 us
    all_to_all x2, starting transfers between devices, gather_columns(): return lax.all_to_all(spread, axes, split_axis=1, concat_axis=1, tiled=True)  22.7 us
    all_to_all x2, waiting for transfers between devices, gather_columns(): return lax.all_to_all(spread, axes, split_axis=1, concat_axis=1, tiled=True)  13.4 us
    unnamed x23, local copies, waits for them, and re-layouts  8.28 us
    all_to_all x1, waiting for transfers between devices, on_device(): lax.all_to_all(outgoing, ('gy', 'gz'), split_axis=1, concat_axis=1, tiled...  7.78 us
    gather x1, local copies, waits for them, and re-layouts, on_device(): jnp.take(far_shift, coarse_kinds, axis=0).transpose(1, 0, 2)  6.81 us
    all_to_all x1, starting transfers between devices, on_device(): lax.all_to_all(outgoing, ('gy', 'gz'), split_axis=1, concat_axis=1, tiled...  6.35 us
    reshape x1, local copies, waits for them, and re-layouts, lift_level(): shift_table = up_shift.transpose(1, 0, 2).reshape(coefs, 8 * coefs)  4.21 us
  transfers between devices with their start and end apart: 3, of which 3 were waited for; matrix products, arithmetic and copies ran while one was open for 30% of the time, Pallas kernels for 0%

profile of v2, /device:TPU:8, one launch (start us, length us, event | category | flops | bytes accessed | tf_op | source)
XLA Modules:
  0.0 131.3 jit_solution(12314280043472063000)
XLA Ops:
  0.0 1.2 copy.37
  1.2 0.0 copy-start.2
  1.2 4.2 %reshape.149 = bf16[289,2312]{1,0:T(8,128)(2,1)} reshape(bf16[289,8,289]{2,1,0:T(8,128)(2,1)} %bitcast.112) | data formatting | bytes 2672672 | tf_op jit(solution)/shard_map/reshape | solution.py:16
  5.4 0.0 copy-done.2
  5.4 0.7 fusion.17
  6.1 0.0 copy-start.6
  6.2 0.6 fusion.26
  6.7 0.1 reshape.184
  6.9 1.9 %convolution_reduce_fusion.1 = bf16[289]{0:T(512)(128)(2,1)S(1)} fusion(bf16[2312,1]{0,1:T(2,128)(2,1)S(1)} %reshape.184, bf16[289,2312]{1,0:T(8,128)(2,1)} %reshape.149), kind=kOutput, calls=%fused_computation.28 | convolution fusion | flops 1336336 | bytes 1341538 | tf_op jit(solution)/shard_map/dot_general | solution.py:17
  8.7 0.6 reshape.150
  9.4 15.2 %all-to-all-start = ((bf16[289,16,1]{0,2,1:T(2,128)(2,1)}), bf16[289,16,1]{0,2,1:T(2,128)(2,1)S(1)}, u32[]{:S(2)}, u32[]{:S(2)}) async-start(bf16[289,16,1]{0,2,1:T(2,128)(2,1)} %reshape.150), calls=%async_computation | async-start | bytes 49152 | tf_op jit(solution)/shard_map/all_to_all | solution.py:77
  24.6 0.0 copy-done.6
  24.6 0.1 copy.47
  24.7 0.1 reshape.157
  24.8 3.9 %gather_fusion.2 = bf16[1024,289]{1,0:T(8,128)(2,1)S(1)} fusion(bf16[289,512]{0,1:T(8,128)(2,1)S(1)} %copy.37, s32[1024]{0:T(1024)S(1)} %broadcast_clamp_fusion), kind=kCustom, calls=%fused_computation.2 | custom fusion | bytes 1187840 | tf_op jit(solution)/shard_map/jit(_take)/gather | solution.py:98
  28.7 0.1 copy.46
  28.8 8.3 %all-to-all-done = bf16[289,16,1]{0,2,1:T(2,128)(2,1)S(1)} async-done(((bf16[289,16,1]{0,2,1:T(2,128)(2,1)}), bf16[289,16,1]{0,2,1:T(2,128)(2,1)S(1)}, u32[]{:S(2)}, u32[]{:S(2)}) %all-to-all-start) | async-done | bytes 9280 | tf_op jit(solution)/shard_map/all_to_all | solution.py:77
  37.1 0.6 fusion.38
  37.7 0.0 copy-start.4
  37.7 0.0 copy-start.5
  37.7 0.7 broadcast_in_dim.43
  38.4 7.5 %all-to-all-start.1 = ((bf16[289,32,2]{0,2,1:T(2,128)(2,1)}), bf16[289,32,2]{0,2,1:T(2,128)(2,1)S(1)}, u32[]{:S(2)}, u32[]{:S(2)}) async-start(bf16[289,32,2]{0,2,1:T(2,128)(2,1)} %broadcast_in_dim.43), calls=%async_computation.1 | async-start | bytes 98304 | tf_op jit(solution)/shard_map/all_to_all | solution.py:77
  45.9 0.0 copy-start
  45.9 1.1 broadcast_select_fusion
  47.0 5.1 %all-to-all-done.1 = bf16[289,32,2]{0,2,1:T(2,128)(2,1)S(1)} async-done(((bf16[289,32,2]{0,2,1:T(2,128)(2,1)}), bf16[289,32,2]{0,2,1:T(2,128)(2,1)S(1)}, u32[]{:S(2)}, u32[]{:S(2)}) %all-to-all-start.1) | async-done | bytes 37024 | tf_op jit(solution)/shard_map/all_to_all | solution.py:77
  52.1 6.3 %all-to-all-start.2 = ((bf16[289,64,16]{0,2,1:T(8,128)(2,1)}), bf16[289,64,16]{0,2,1:T(8,128)(2,1)S(1)}, u32[]{:S(2)}, u32[]{:S(2)}) async-start(bf16[289,64,16]{0,2,1:T(8,128)(2,1)} %broadcast_select_fusion), calls=%async_computation.2 | async-start | bytes 1572864 | tf_op jit(solution)/shard_map/all_to_all | solution.py:99
  58.5 0.0 copy-done.4
  58.5 0.0 copy-done.5
  58.5 0.1 copy.45
  58.7 0.8 reshape.155.idx_ref
  59.4 0.0 copy-done
  59.4 2.8 %copy.50 = bf16[8,289,289]{1,2,0:T(8,128)(2,1)} copy(bf16[8,289,289]{2,0,1:T(8,128)(2,1)S(1)} %copy-done) | data formatting | bytes 2672672 | tf_op args[3]
  62.2 4.2 %copy.44 = bf16[8,289,289]{1,0,2:T(8,128)(2,1)} copy(bf16[8,289,289]{2,0,1:T(8,128)(2,1)} %param.11) | data formatting | bytes 2672672 | tf_op args[2]
  66.4 0.0 copy-start.7
  66.4 4.1 %reshape.152 = bf16[2312,289]{0,1:T(8,128)(2,1)} reshape(bf16[8,289,289]{1,0,2:T(8,128)(2,1)} %copy.44) | data formatting | bytes 2672672 | tf_op jit(solution)/shard_map/reshape | solution.py:24
  70.5 0.0 copy-done.7
  70.5 0.2 fusion.52
  70.7 6.8 %gather_fusion = bf16[8,289,289]{2,0,1:T(8,128)(2,1)} fusion(bf16[8,289,289]{2,0,1:T(8,128)(2,1)S(1)} %copy-done, s32[1024]{0:T(1024)S(1)} %pad_clamp_fusion.1), kind=kCustom, calls=%fused_computation | custom fusion | bytes 2672704 | tf_op jit(solution)/shard_map/jit(_take)/gather | solution.py:111
  77.5 0.0 copy-start.8
  77.5 0.0 copy-start.3
  77.5 3.3 %pad.9.fs_ref = bf16[8,384,384]{2,1,0:T(8,128)(2,1)} pad(bf16[8,289,289]{2,1,0:T(8,128)(2,1)} %bitcast.116, bf16[]{:T(256)} %constant.89.clone.1), padding=0_0x0_95x0_95 | pad | bytes 3695634 | tf_op jit(solution)/shard_map/jit(_pad)/pad | solution.py:56
  80.8 0.0 copy-done.8
  80.8 0.2 fusion.53
  81.0 0.2 and_reduce_fusion
  81.2 1.9 %constant_dynamic-slice_fusion = bf16[1,289,289]{2,0,1:T(2,128)(2,1)S(1)} fusion(bf16[8,289,289]{2,0,1:T(8,128)(2,1)} %param.11, s32[]{:T(128)S(6)} %select_n.70), kind=kLoop, calls=%fused_computation.59 | loop fusion | bytes 334088 | tf_op jit(solution)/shard_map/dynamic_slice | solution.py:119
  83.2 0.0 copy-done.3
  83.2 1.6 %select_bitcast_fusion = bf16[289,8,289]{2,1,0:T(8,128)(2,1)} fusion(bf16[8,289,289]{2,0,1:T(8,128)(2,1)S(1)} %copy-done.3, pred[8]{0:T(512)(128)(4,1)S(1)} %get-tuple-element.6), kind=kLoop, calls=%fused_computation.10 | loop fusion | flops 668168 | bytes 2672680 | tf_op jit(solution)/shard_map/jit(_take)/select_n | solution.py:111
  84.8 0.6 gather_fusion.1
  85.4 0.1 select_bitcast_fusion.1
  85.4 0.0 copy-start.1
  85.5 2.2 %fusion.35 = bf16[289]{0:T(512)(128)(2,1)S(1)} fusion(bf16[289,8,289]{2,1,0:T(8,128)(2,1)} %select_bitcast_fusion, bf16[8,289,1]{1,0,2:T(8,128)(2,1)S(1)} %select_bitcast_fusion.1), kind=kOutput, calls=%fused_computation.26 | convolution fusion | flops 1336336 | bytes 1341538 | tf_op jit(solution)/shard_map/dot_general | solution.py:116
  87.7 0.2 convolution_reduce_fusion
  87.9 2.2 %fusion.1 = bf16[1,8,289]{2,0,1:T(2,128)(2,1)S(1)} fusion(bf16[289,1,1]{0,1,2:T(2,128)(2,1)S(1)} %reshape.191, bf16[8,289,289]{2,0,1:T(8,128)(2,1)} %param.11), kind=kOutput, calls=%fused_computation.6 | convolution fusion | flops 1336336 | bytes 1341538 | tf_op jit(solution)/shard_map/dot_general | solution.py:23
  90.0 0.0 copy-done.1
  90.0 0.3 fusion
  90.4 0.1 convert_element_type.75
  90.5 1.2 convolution_bitcast_fusion
  91.7 1.5 %reshape.153 = f32[8,289,64]{1,0,2:T(8,128)S(1)} reshape(f32[2312,64]{0,1:T(8,128)} %convolution_bitcast_fusion) | data formatting | bytes 1183744 | tf_op jit(solution)/shard_map/reshape | solution.py:26
  93.3 7.8 %all-to-all-done.2 = bf16[289,64,16]{0,2,1:T(8,128)(2,1)S(1)} async-done(((bf16[289,64,16]{0,2,1:T(8,128)(2,1)}), bf16[289,64,16]{0,2,1:T(8,128)(2,1)S(1)}, u32[]{:S(2)}, u32[]{:S(2)}) %all-to-all-start.2) | async-done | bytes 591904 | tf_op jit(solution)/shard_map/all_to_all | solution.py:99
  101.0 0.1 maximum_bitcast_fusion
  101.2 1.2 pad.8.buf_ref
  102.3 26.8 %shard_map.91 = f32[512,384]{1,0:T(8,128)} custom-call(s32[8192]{0:T(1024)} %reshape.155.idx_ref, bf16[1536,384]{1,0:T(8,128)(2,1)} %pad.8.buf_ref, bf16[8,384,384]{2,1,0:T(8,128)(2,1)} %pad.9.fs_ref), custom_call_target="tpu_custom_call" | custom-call | tf_op jit(solution)/shard_map/pallas_call | solution.py:58
  129.2 1.2 fusion.42
  130.4 0.9 copy.51
  (10 shorter events, 0.1 us)
Async XLA Ops:
  1.2 4.2 %copy-start.2 = (bf16[8,289,289]{2,0,1:T(8,128)(2,1)S(1)}, bf16[8,289,289]{2,0,1:T(8,128)(2,1)}, u32[]{:S(2)}) copy-start(bf16[8,289,289]{2,0,1:T(8,128)(2,1)} %param.10) | copy-start | bytes 4009012
  6.1 18.4 %copy-start.6 = (s32[1,1,64,16]{2,3,1,0:T(8,128)S(1)}, s32[1,1,64,16]{2,3,1,0:T(8,128)}, u32[]{:S(2)}) copy-start(s32[1,1,64,16]{2,3,1,0:T(8,128)} %param.13) | copy-start | bytes 12292
  9.4 27.8 %all-to-all-start = ((bf16[289,16,1]{0,2,1:T(2,128)(2,1)}), bf16[289,16,1]{0,2,1:T(2,128)(2,1)S(1)}, u32[]{:S(2)}, u32[]{:S(2)}) async-start(bf16[289,16,1]{0,2,1:T(2,128)(2,1)} %reshape.150), calls=%async_computation | async-start | bytes 49152 | tf_op jit(solution)/shard_map/all_to_all | solution.py:77
  37.7 20.8 %copy-start.4 = (s32[16,512]{1,0:T(8,128)S(1)}, s32[16,512]{1,0:T(8,128)}, u32[]{:S(2)}) copy-start(s32[16,512]{1,0:T(8,128)} %param.14) | copy-start | bytes 98308
  37.7 20.8 %copy-start.5 = (s32[16,512]{1,0:T(8,128)S(1)}, s32[16,512]{1,0:T(8,128)}, u32[]{:S(2)}) copy-start(s32[16,512]{1,0:T(8,128)} %param.15) | copy-start | bytes 98308
  38.4 13.7 %all-to-all-start.1 = ((bf16[289,32,2]{0,2,1:T(2,128)(2,1)}), bf16[289,32,2]{0,2,1:T(2,128)(2,1)S(1)}, u32[]{:S(2)}, u32[]{:S(2)}) async-start(bf16[289,32,2]{0,2,1:T(2,128)(2,1)} %broadcast_in_dim.43), calls=%async_computation.1 | async-start | bytes 98304 | tf_op jit(solution)/shard_map/all_to_all | solution.py:77
  45.9 13.5 %copy-start = (bf16[8,289,289]{2,0,1:T(8,128)(2,1)S(1)}, bf16[8,289,289]{2,0,1:T(8,128)(2,1)}, u32[]{:S(2)}) copy-start(bf16[8,289,289]{2,0,1:T(8,128)(2,1)} %param.12) | copy-start | bytes 4009012
  52.1 48.9 %all-to-all-start.2 = ((bf16[289,64,16]{0,2,1:T(8,128)(2,1)}), bf16[289,64,16]{0,2,1:T(8,128)(2,1)S(1)}, u32[]{:S(2)}, u32[]{:S(2)}) async-start(bf16[289,64,16]{0,2,1:T(8,128)(2,1)} %broadcast_select_fusion), calls=%async_computation.2 | async-start | bytes 1572864 | tf_op jit(solution)/shard_map/all_to_all | solution.py:99
  66.4 4.1 %copy-start.7 = (s32[8,64]{1,0:T(8,128)S(1)}, s32[8,64]{1,0:T(8,128)}, u32[]{:S(2)}) copy-start(s32[8,64]{1,0:T(8,128)} %param.17) | copy-start | bytes 6148
  77.5 3.3 %copy-start.8 = (s32[8,64]{1,0:T(8,128)S(1)}, s32[8,64]{1,0:T(8,128)}, u32[]{:S(2)}) copy-start(s32[8,64]{1,0:T(8,128)} %param.16) | copy-start | bytes 6148
  77.5 5.7 %copy-start.3 = (bf16[8,289,289]{2,0,1:T(8,128)(2,1)S(1)}, bf16[8,289,289]{2,0,1:T(8,128)(2,1)}, u32[]{:S(2)}) copy-start(bf16[8,289,289]{2,0,1:T(8,128)(2,1)} %gather_fusion) | copy-start | bytes 4009012
  85.4 4.6 %copy-start.1 = (bf16[2312,289]{0,1:T(8,128)(2,1)S(1)}, bf16[2312,289]{0,1:T(8,128)(2,1)}, u32[]{:S(2)}) copy-start(bf16[2312,289]{0,1:T(8,128)(2,1)} %reshape.152) | copy-start | bytes 4009012

commit v3 on v2

--- a/solution.py
+++ b/solution.py
@@ -70,11 +70,7 @@
 
 
 def gather_columns(column_block, axes):
-    group = lax.axis_size(axes)
-    width = column_block.shape[1]
-    spread = jnp.broadcast_to(column_block[:, None, :], (column_block.shape[0], group, width))
-    spread = spread.reshape(column_block.shape[0], group * width)
-    return lax.all_to_all(spread, axes, split_axis=1, concat_axis=1, tiled=True)
+    return lax.all_gather(column_block, axes, axis=1, tiled=True)
 
 
 def on_device(

time: 132 us -> 171 us (1.30)
  the two profiles are of different devices: /device:TPU:8 before, /device:TPU:1 now
where the time goes in v3:
time: 171 us
  blocking collectives  71.7 us (42%)
  local copies, waits for them, and re-layouts  38.7 us (23%)
  Pallas kernels  26.6 us (16%)
  starting transfers between devices  19.3 us (11%)
  matrix products  9.9 us (6%)
  other arithmetic  4.17 us (2%)
    all_gather x2, blocking collectives, gather_columns(): return lax.all_gather(column_block, axes, axis=1, tiled=True)  71.7 us
    pallas_call x1, Pallas kernels, far_field(): pl.pallas_call(far_kernel, out_shape=jax.ShapeDtypeStruct((targets, LANES...  26.6 us
    all_to_all x1, starting transfers between devices, on_device(): lax.all_to_all(outgoing, ('gy', 'gz'), split_axis=1, concat_axis=1, tiled...  19.3 us
    unnamed x23, local copies, waits for them, and re-layouts  9.09 us
    gather x1, local copies, waits for them, and re-layouts, on_device(): jnp.take(far_shift, coarse_kinds, axis=0).transpose(1, 0, 2)  6.84 us
    dot_general x4, matrix products, lift_level(): return jnp.dot(shift_table, child_stack, preferred_element_type=jnp.float32)  5.36 us
    reshape x1, local copies, waits for them, and re-layouts, lift_level(): shift_table = up_shift.transpose(1, 0, 2).reshape(coefs, 8 * coefs)  4.19 us
    reshape x1, local copies, waits for them, and re-layouts, lower_level(): down_shift.reshape(8 * coefs, coefs)  4.07 us
  transfers between devices with their start and end apart: 1, of which 0 were waited for; matrix products, arithmetic and copies ran while one was open for 24% of the time, Pallas kernels for 0%

profile of v3, /device:TPU:1, one launch (start us, length us, event | category | flops | bytes accessed | tf_op | source)
XLA Modules:
  0.0 170.7 jit_solution(18225643984334134982)
XLA Ops:
  0.0 0.8 copy.47
  0.8 0.7 compare_and_fusion
  1.5 1.2 copy.37
  2.7 0.1 reshape.137
  2.8 0.1 copy.46
  2.9 3.9 %gather_fusion.2 = bf16[1024,289]{1,0:T(8,128)(2,1)S(1)} fusion(bf16[289,512]{0,1:T(8,128)(2,1)S(1)} %copy.37, s32[1024]{0:T(1024)S(1)} %broadcast_clamp_fusion), kind=kCustom, calls=%fused_computation.2 | custom fusion | bytes 1187840 | tf_op jit(solution)/shard_map/jit(_take)/gather | solution.py:94
  6.8 0.0 copy-start.2
  6.8 1.1 broadcast_select_fusion
  7.9 19.3 %all-to-all-start = ((bf16[289,64,16]{0,2,1:T(8,128)(2,1)}), bf16[289,64,16]{0,2,1:T(8,128)(2,1)S(1)}, u32[]{:S(2)}, u32[]{:S(2)}) async-start(bf16[289,64,16]{0,2,1:T(8,128)(2,1)} %broadcast_select_fusion), calls=%async_computation | async-start | bytes 1572864 | tf_op jit(solution)/shard_map/all_to_all | solution.py:95
  27.2 0.0 copy-done.2
  27.2 0.0 copy-start.4
  27.2 0.0 copy-start.5
  27.2 0.0 copy-start.6
  27.3 0.7 fusion.17
  28.0 0.6 fusion.26
  28.6 0.0 copy-done.4
  28.6 0.0 copy-done.5
  28.6 0.0 copy-done.6
  28.6 0.2 fusion.52
  28.8 0.0 copy-start
  28.8 4.2 %reshape.130 = bf16[289,2312]{1,0:T(8,128)(2,1)} reshape(bf16[289,8,289]{2,1,0:T(8,128)(2,1)} %bitcast.116) | data formatting | bytes 2672672 | tf_op jit(solution)/shard_map/reshape | solution.py:16
  33.0 0.1 copy.45
  33.2 0.8 reshape.135.idx_ref
  33.9 0.0 copy-done
  33.9 2.8 %copy.50 = bf16[8,289,289]{1,2,0:T(8,128)(2,1)} copy(bf16[8,289,289]{2,0,1:T(8,128)(2,1)S(1)} %copy-done) | data formatting | bytes 2672672 | tf_op args[3]
  36.7 4.2 %copy.44 = bf16[8,289,289]{1,0,2:T(8,128)(2,1)} copy(bf16[8,289,289]{2,0,1:T(8,128)(2,1)} %param.11) | data formatting | bytes 2672672 | tf_op args[2]
  41.0 4.1 %reshape.132 = bf16[2312,289]{0,1:T(8,128)(2,1)} reshape(bf16[8,289,289]{1,0,2:T(8,128)(2,1)} %copy.44) | data formatting | bytes 2672672 | tf_op jit(solution)/shard_map/reshape | solution.py:24
  45.0 6.8 %gather_fusion = bf16[8,289,289]{2,0,1:T(8,128)(2,1)} fusion(bf16[8,289,289]{2,0,1:T(8,128)(2,1)S(1)} %copy-done, s32[1024]{0:T(1024)S(1)} %pad_clamp_fusion.1), kind=kCustom, calls=%fused_computation | custom fusion | bytes 2672704 | tf_op jit(solution)/shard_map/jit(_take)/gather | solution.py:107
  51.9 0.0 copy-start.7
  51.9 0.1 reshape.171
  52.0 0.0 copy-start.3
  52.0 2.0 %convolution_reduce_fusion.1 = bf16[289]{0:T(512)(128)(2,1)S(1)} fusion(bf16[2312,1]{0,1:T(2,128)(2,1)S(1)} %reshape.171, bf16[289,2312]{1,0:T(8,128)(2,1)} %reshape.130), kind=kOutput, calls=%fused_computation.28 | convolution fusion | flops 1336336 | bytes 1341538 | tf_op jit(solution)/shard_map/dot_general | solution.py:17
  54.0 25.6 %all-gather = bf16[16,1,289]{2,1,0:T(2,128)(2,1)S(1)} all-gather(bf16[1,1,289]{2,1,0:T(2,128)(2,1)S(1)} %reshape.162), channel_id=1, replica_groups=mesh['gx'=8,'gy'=4,'gz'=16] {'gz'}, dimensions={0}, use_global_device_ids=true | all-gather | bytes 9826 | tf_op jit(solution)/shard_map/all_gather | solution.py:73
  79.6 2.1 %fusion.38 = bf16[1,2,289]{2,1,0:T(2,128)(2,1)S(1)} fusion(bf16[289,8,289]{2,1,0:T(8,128)(2,1)} %bitcast.117, bf16[289,2,8]{0,2,1:T(8,128)(2,1)S(1)} %bitcast.124), kind=kOutput, calls=%fused_computation.29 | convolution fusion | flops 2673250 | bytes 1346740 | tf_op jit(solution)/shard_map/dot_general | solution.py:17
  81.7 46.0 %all-gather.1 = bf16[32,2,289]{2,1,0:T(2,128)(2,1)S(1)} all-gather(bf16[1,2,289]{2,1,0:T(2,128)(2,1)S(1)} %fusion.38), channel_id=1, replica_groups=mesh['gx'=8,'gy'=4,'gz'=16] {'gx','gy'}, dimensions={0}, use_global_device_ids=true | all-gather | bytes 38148 | tf_op jit(solution)/shard_map/all_gather | solution.py:73
  127.8 0.0 copy-done.7
  127.8 0.2 fusion.53
  128.0 0.6 gather_fusion.1
  128.5 0.2 and_reduce_fusion
  128.8 0.1 select_bitcast_fusion.1
  128.8 0.0 copy-done.3
  128.8 0.3 select_bitcast_fusion
  129.2 0.6 fusion.35
  129.8 0.0 copy-start.1
  129.8 2.0 %constant_dynamic-slice_fusion = bf16[1,289,289]{2,0,1:T(2,128)(2,1)S(1)} fusion(bf16[8,289,289]{2,0,1:T(8,128)(2,1)} %param.11, s32[]{:T(128)S(6)} %select_n.70), kind=kLoop, calls=%fused_computation.59 | loop fusion | bytes 334088 | tf_op jit(solution)/shard_map/dynamic_slice | solution.py:115
  131.9 0.2 convolution_reduce_fusion
  132.1 2.2 %fusion.1 = bf16[1,8,289]{2,0,1:T(2,128)(2,1)S(1)} fusion(bf16[289,1,1]{0,1,2:T(2,128)(2,1)S(1)} %reshape.178, bf16[8,289,289]{2,0,1:T(8,128)(2,1)} %param.11), kind=kOutput, calls=%fused_computation.6 | convolution fusion | flops 1336336 | bytes 1341538 | tf_op jit(solution)/shard_map/dot_general | solution.py:23
  134.3 0.0 copy-done.1
  134.3 0.3 fusion
  134.6 0.1 convert_element_type.78
  134.7 1.2 convolution_bitcast_fusion
  136.0 1.5 reshape.133
  137.5 3.2 %pad.9.fs_ref = bf16[8,384,384]{2,1,0:T(8,128)(2,1)} pad(bf16[8,289,289]{2,1,0:T(8,128)(2,1)} %bitcast.120, bf16[]{:T(256)} %constant.89.clone.1), padding=0_0x0_95x0_95 | pad | bytes 3695634 | tf_op jit(solution)/shard_map/jit(_pad)/pad | solution.py:56
  140.7 0.0 all-to-all-done
  140.7 0.1 maximum_bitcast_fusion
  140.8 1.1 pad.8.buf_ref
  141.9 26.6 %shard_map.91 = f32[512,384]{1,0:T(8,128)} custom-call(s32[8192]{0:T(1024)} %reshape.135.idx_ref, bf16[1536,384]{1,0:T(8,128)(2,1)} %pad.8.buf_ref, bf16[8,384,384]{2,1,0:T(8,128)(2,1)} %pad.9.fs_ref), custom_call_target="tpu_custom_call" | custom-call | tf_op jit(solution)/shard_map/pallas_call | solution.py:58
  168.6 1.2 fusion.42
  169.8 0.9 copy.51
  (10 shorter events, 0.1 us)
Async XLA Ops:
  6.8 20.4 %copy-start.2 = (bf16[8,289,289]{2,0,1:T(8,128)(2,1)S(1)}, bf16[8,289,289]{2,0,1:T(8,128)(2,1)}, u32[]{:S(2)}) copy-start(bf16[8,289,289]{2,0,1:T(8,128)(2,1)} %param.10) | copy-start | bytes 4009012
  7.9 132.8 %all-to-all-start = ((bf16[289,64,16]{0,2,1:T(8,128)(2,1)}), bf16[289,64,16]{0,2,1:T(8,128)(2,1)S(1)}, u32[]{:S(2)}, u32[]{:S(2)}) async-start(bf16[289,64,16]{0,2,1:T(8,128)(2,1)} %broadcast_select_fusion), calls=%async_computation | async-start | bytes 1572864 | tf_op jit(solution)/shard_map/all_to_all | solution.py:95
  27.2 1.4 copy-start.4
  27.2 1.4 copy-start.5
  27.2 1.4 copy-start.6
  28.8 5.1 %copy-start = (bf16[8,289,289]{2,0,1:T(8,128)(2,1)S(1)}, bf16[8,289,289]{2,0,1:T(8,128)(2,1)}, u32[]{:S(2)}) copy-start(bf16[8,289,289]{2,0,1:T(8,128)(2,1)} %param.12) | copy-start | bytes 4009012
  51.9 75.9 %copy-start.7 = (s32[8,64]{1,0:T(8,128)S(1)}, s32[8,64]{1,0:T(8,128)}, u32[]{:S(2)}) copy-start(s32[8,64]{1,0:T(8,128)} %param.16) | copy-start | bytes 6148
  52.0 76.9 %copy-start.3 = (bf16[8,289,289]{2,0,1:T(8,128)(2,1)S(1)}, bf16[8,289,289]{2,0,1:T(8,128)(2,1)}, u32[]{:S(2)}) copy-start(bf16[8,289,289]{2,0,1:T(8,128)(2,1)} %gather_fusion) | copy-start | bytes 4009012
  129.8 4.5 %copy-start.1 = (bf16[2312,289]{0,1:T(8,128)(2,1)S(1)}, bf16[2312,289]{0,1:T(8,128)(2,1)}, u32[]{:S(2)}) copy-start(bf16[2312,289]{0,1:T(8,128)(2,1)} %reshape.132) | copy-start | bytes 4009012

commit v4 on v2

--- a/solution.py
+++ b/solution.py
@@ -95,14 +95,18 @@
     peer_count = lax.axis_size(("gy", "gz"))
     slot_count = send_list.shape[3]
     send_order = send_list.reshape(peer_count * slot_count)
-    outgoing = jnp.take(multipoles, send_order, axis=1)
-    arrived = lax.all_to_all(outgoing, ("gy", "gz"), split_axis=1, concat_axis=1, tiled=True)
     upward = multipoles
     for level in range(LOCAL_LEVELS):
         upward = lift_level(upward, up_shift).astype(jnp.bfloat16)
-    row_boxes = gather_columns(upward, "gz")
-    row_multi = lift_level(row_boxes, up_shift).astype(jnp.bfloat16)
-    coarse_multi = gather_columns(row_multi, ("gx", "gy"))
+    outgoing = jnp.take(multipoles, send_order, axis=1).reshape(coefs, peer_count, slot_count)
+    own_box = jnp.broadcast_to(upward[:, None, :], (coefs, peer_count, 1))
+    payload = jnp.concatenate([outgoing, own_box], axis=2).reshape(coefs, peer_count * (slot_count + 1))
+    landed = lax.all_to_all(payload, ("gy", "gz"), split_axis=1, concat_axis=1, tiled=True)
+    landed = landed.reshape(coefs, peer_count, slot_count + 1)
+    arrived = landed[:, :, :slot_count].reshape(coefs, peer_count * slot_count)
+    slice_boxes = landed[:, :, slot_count]
+    slice_multi = lift_level(slice_boxes, up_shift).astype(jnp.bfloat16)
+    coarse_multi = gather_columns(slice_multi, "gx")
     coarse_cols = coarse_src[:, coarse_box]
     coarse_kinds = coarse_kind[:, coarse_box]
     list_len = coarse_cols.shape[0]

time: 132 us -> 136 us (1.030)
  the two profiles are of different devices: /device:TPU:8 before, /device:TPU:1 now
where the time goes in v4:
time: 136 us
  local copies, waits for them, and re-layouts  39.8 us (29%)
  starting transfers between devices  28.7 us (21%)
  waiting for transfers between devices  28.1 us (21%)
  Pallas kernels  26.6 us (20%)
  matrix products  7.67 us (6%)
  other arithmetic  4.59 us (3%)
    all_to_all x1, waiting for transfers between devices, on_device(): lax.all_to_all(payload, ('gy', 'gz'), split_axis=1, concat_axis=1, tiled=...  28.1 us
    pallas_call x1, Pallas kernels, far_field(): pl.pallas_call(far_kernel, out_shape=jax.ShapeDtypeStruct((targets, LANES...  26.6 us
    all_to_all x1, starting transfers between devices, on_device(): lax.all_to_all(payload, ('gy', 'gz'), split_axis=1, concat_axis=1, tiled=...  19.5 us
    unnamed x31, local copies, waits for them, and re-layouts  9.37 us
    all_to_all x1, starting transfers between devices, gather_columns(): return lax.all_to_all(spread, axes, split_axis=1, concat_axis=1, tiled=True)  9.23 us
    gather x1, local copies, waits for them, and re-layouts, on_device(): jnp.take(far_shift, coarse_kinds, axis=0).transpose(1, 0, 2)  6.79 us
    reshape x1, local copies, waits for them, and re-layouts, lower_level(): down_shift.reshape(8 * coefs, coefs)  4.21 us
    reshape x1, local copies, waits for them, and re-layouts, lift_level(): shift_table = up_shift.transpose(1, 0, 2).reshape(coefs, 8 * coefs)  4.21 us
  transfers between devices with their start and end apart: 2, of which 1 were waited for; matrix products, arithmetic and copies ran while one was open for 21% of the time, Pallas kernels for 20%

profile of v4, /device:TPU:1, one launch (start us, length us, event | category | flops | bytes accessed | tf_op | source)
XLA Modules:
  0.0 135.7 jit_solution(11229077413090986887)
XLA Ops:
  0.0 0.8 copy.39
  0.8 0.7 compare_and_fusion
  1.5 1.2 copy.40
  2.7 0.0 copy-start.1
  2.7 4.2 %reshape.146 = bf16[289,2312]{1,0:T(8,128)(2,1)} reshape(bf16[289,8,289]{2,1,0:T(8,128)(2,1)} %bitcast.111) | data formatting | bytes 2672672 | tf_op jit(solution)/shard_map/reshape | solution.py:16
  6.9 0.0 copy-done.1
  6.9 0.7 fusion.17
  7.6 0.6 fusion.32
  8.2 0.1 reshape.178
  8.3 0.1 reshape.141
  8.4 0.0 copy-start.6
  8.5 3.9 %gather_fusion.1 = bf16[1024,289]{1,0:T(8,128)(2,1)S(1)} fusion(bf16[289,512]{0,1:T(8,128)(2,1)S(1)} %copy.40, s32[1024]{0:T(1024)S(1)} %broadcast_clamp_fusion), kind=kCustom, calls=%fused_computation.1 | custom fusion | bytes 1187840 | tf_op jit(solution)/shard_map/jit(_take)/gather | solution.py:101
  12.4 0.1 copy.38
  12.5 0.0 copy-done.6
  12.5 0.5 convolution_reduce_fusion.1
  13.0 0.2 broadcast_select_fusion
  13.2 0.1 broadcast_in_dim.47
  13.3 0.0 copy-start
  13.3 1.2 pad_maximum_fusion
  14.5 19.5 %all-to-all-start = ((bf16[289,64,17]{0,2,1:T(8,128)(2,1)}), bf16[289,64,17]{0,2,1:T(8,128)(2,1)S(1)}, u32[]{:S(2)}, u32[]{:S(2)}) async-start(bf16[289,64,17]{0,2,1:T(8,128)(2,1)} %pad_maximum_fusion), calls=%async_computation | async-start | bytes 2359296 | tf_op jit(solution)/shard_map/all_to_all | solution.py:104
  34.0 0.0 copy-done
  34.0 0.0 copy-start.11
  34.0 2.8 %copy.52 = bf16[8,289,289]{1,2,0:T(8,128)(2,1)} copy(bf16[8,289,289]{2,0,1:T(8,128)(2,1)S(1)} %copy-done) | data formatting | bytes 2672672 | tf_op args[3]
  36.9 0.0 copy-done.11
  36.9 0.2 fusion.52
  37.1 6.8 %gather_fusion = bf16[8,289,289]{2,0,1:T(8,128)(2,1)} fusion(bf16[8,289,289]{2,0,1:T(8,128)(2,1)S(1)} %copy-done, s32[1024]{0:T(1024)S(1)} %pad_clamp_fusion.1), kind=kCustom, calls=%fused_computation | custom fusion | bytes 2672704 | tf_op jit(solution)/shard_map/jit(_take)/gather | solution.py:115
  43.9 4.2 %copy.49 = bf16[8,289,289]{1,0,2:T(8,128)(2,1)} copy(bf16[8,289,289]{2,0,1:T(8,128)(2,1)} %param.11) | data formatting | bytes 2672672 | tf_op args[2]
  48.1 4.2 %reshape.147 = bf16[2312,289]{0,1:T(8,128)(2,1)} reshape(bf16[8,289,289]{1,0,2:T(8,128)(2,1)} %copy.49) | data formatting | bytes 2672672 | tf_op jit(solution)/shard_map/reshape | solution.py:24
  52.3 0.0 copy-done.9
  52.3 0.0 copy-done.10
  52.3 0.8 copy.50
  53.2 1.7 %reshape.150.idx_ref = s32[8192]{0:T(1024)} reshape(s32[512,16]{1,0:T(8,128)} %copy.50) | data formatting | bytes 65536 | tf_op jit(solution)/shard_map/reshape | solution.py:57
  54.9 0.0 copy-done.5
  54.9 1.7 %pad.9.fs_ref = bf16[8,384,384]{2,1,0:T(8,128)(2,1)} pad(bf16[8,289,289]{2,1,0:T(8,128)(2,1)S(1)} %bitcast.116, bf16[]{:T(256)} %constant.89.clone.1), padding=0_0x0_95x0_95 | pad | bytes 3695634 | tf_op jit(solution)/shard_map/jit(_pad)/pad | solution.py:56
  56.5 0.0 copy-done.12
  56.5 0.2 fusion.53
  56.7 0.2 and_reduce_fusion
  57.0 2.7 %constant_dynamic-slice_fusion = bf16[1,289,289]{2,0,1:T(2,128)(2,1)} fusion(bf16[8,289,289]{2,0,1:T(8,128)(2,1)} %param.11, s32[]{:T(128)S(6)} %select_n.70), kind=kLoop, calls=%fused_computation.60 | loop fusion | bytes 334088 | tf_op jit(solution)/shard_map/dynamic_slice | solution.py:123
  59.7 0.0 copy-done.4
  59.7 1.5 %select_bitcast_fusion = bf16[289,8,289]{2,1,0:T(8,128)(2,1)} fusion(bf16[8,289,289]{2,0,1:T(8,128)(2,1)S(1)} %copy-done.4, pred[8]{0:T(512)(128)(4,1)S(1)} %get-tuple-element.6), kind=kLoop, calls=%fused_computation.10 | loop fusion | flops 668168 | bytes 2672680 | tf_op jit(solution)/shard_map/jit(_take)/select_n | solution.py:115
  61.2 28.1 %all-to-all-done = bf16[289,64,17]{0,2,1:T(8,128)(2,1)S(1)} async-done(((bf16[289,64,17]{0,2,1:T(8,128)(2,1)}), bf16[289,64,17]{0,2,1:T(8,128)(2,1)S(1)}, u32[]{:S(2)}, u32[]{:S(2)}) %all-to-all-start) | async-done | bytes 628896 | tf_op jit(solution)/shard_map/all_to_all | solution.py:104
  89.3 0.1 slice.18
  89.4 0.0 copy-done.2
  89.4 0.6 fusion.35
  90.0 0.6 broadcast_in_dim.48
  90.6 9.2 %all-to-all-start.1 = ((bf16[289,8,8]{0,2,1:T(8,128)(2,1)}), bf16[289,8,8]{0,2,1:T(8,128)(2,1)S(1)}, u32[]{:S(2)}, u32[]{:S(2)}) async-start(bf16[289,8,8]{0,2,1:T(8,128)(2,1)} %broadcast_in_dim.48), calls=%async_computation.1 | async-start | bytes 98304 | tf_op jit(solution)/shard_map/all_to_all | solution.py:77
  99.9 0.1 slice.19
  100.0 0.1 maximum_bitcast_fusion
  100.1 1.2 pad.8.buf_ref
  101.3 26.6 %shard_map.91 = f32[512,384]{1,0:T(8,128)} custom-call(s32[8192]{0:T(1024)} %reshape.150.idx_ref, bf16[1536,384]{1,0:T(8,128)(2,1)} %pad.8.buf_ref, bf16[8,384,384]{2,1,0:T(8,128)(2,1)} %pad.9.fs_ref), custom_call_target="tpu_custom_call" | custom-call | tf_op jit(solution)/shard_map/pallas_call | solution.py:58
  127.8 0.0 all-to-all-done.1
  127.8 0.6 gather_fusion.2
  128.4 0.1 select_bitcast_fusion.1
  128.5 2.2 %fusion.38 = bf16[289]{0:T(512)(128)(2,1)S(1)} fusion(bf16[289,8,289]{2,1,0:T(8,128)(2,1)} %select_bitcast_fusion, bf16[8,289,1]{1,0,2:T(8,128)(2,1)S(1)} %select_bitcast_fusion.1), kind=kOutput, calls=%fused_computation.28 | convolution fusion | flops 1336336 | bytes 1341538 | tf_op jit(solution)/shard_map/dot_general | solution.py:120
  130.7 0.2 convolution_reduce_fusion
  130.9 2.2 %fusion.1 = bf16[1,8,289]{2,0,1:T(2,128)(2,1)S(1)} fusion(bf16[289,1,1]{0,1,2:T(2,128)(2,1)S(1)} %reshape.185, bf16[8,289,289]{2,0,1:T(8,128)(2,1)} %param.11), kind=kOutput, calls=%fused_computation.6 | convolution fusion | flops 1336336 | bytes 1341538 | tf_op jit(solution)/shard_map/dot_general | solution.py:23
  133.1 0.0 copy-done.3
  133.1 0.3 fusion
  133.4 0.1 convert_element_type.75
  133.6 0.4 convolution_bitcast_fusion
  134.0 0.4 reshape.148
  134.4 0.3 copy-done.7
  134.7 0.1 fusion.42
  134.8 0.9 copy.53
  (18 shorter events, 0.1 us)
Async XLA Ops:
  2.7 4.2 %copy-start.1 = (bf16[8,289,289]{2,0,1:T(8,128)(2,1)S(1)}, bf16[8,289,289]{2,0,1:T(8,128)(2,1)}, u32[]{:S(2)}) copy-start(bf16[8,289,289]{2,0,1:T(8,128)(2,1)} %param.10) | copy-start | bytes 4009012
  8.4 4.0 %copy-start.6 = (bf16[289,2312]{1,0:T(8,128)(2,1)S(1)}, bf16[289,2312]{1,0:T(8,128)(2,1)}, u32[]{:S(2)}) copy-start(bf16[289,2312]{1,0:T(8,128)(2,1)} %reshape.146) | copy-start | bytes 4009012
  13.3 20.8 %copy-start = (bf16[8,289,289]{2,0,1:T(8,128)(2,1)S(1)}, bf16[8,289,289]{2,0,1:T(8,128)(2,1)}, u32[]{:S(2)}) copy-start(bf16[8,289,289]{2,0,1:T(8,128)(2,1)} %param.12) | copy-start | bytes 4009012
  14.5 74.8 %all-to-all-start = ((bf16[289,64,17]{0,2,1:T(8,128)(2,1)}), bf16[289,64,17]{0,2,1:T(8,128)(2,1)S(1)}, u32[]{:S(2)}, u32[]{:S(2)}) async-start(bf16[289,64,17]{0,2,1:T(8,128)(2,1)} %pad_maximum_fusion), calls=%async_computation | async-start | bytes 2359296 | tf_op jit(solution)/shard_map/all_to_all | solution.py:104
  34.0 2.8 %copy-start.11 = (s32[8,64]{1,0:T(8,128)S(1)}, s32[8,64]{1,0:T(8,128)}, u32[]{:S(2)}) copy-start(s32[8,64]{1,0:T(8,128)} %param.17) | copy-start | bytes 6148
  48.1 4.2 %copy-start.9 = (s32[16,512]{1,0:T(8,128)S(1)}, s32[16,512]{1,0:T(8,128)}, u32[]{:S(2)}) copy-start(s32[16,512]{1,0:T(8,128)} %param.14) | copy-start | bytes 98308
  48.1 4.2 %copy-start.10 = (s32[16,512]{1,0:T(8,128)S(1)}, s32[16,512]{1,0:T(8,128)}, u32[]{:S(2)}) copy-start(s32[16,512]{1,0:T(8,128)} %param.15) | copy-start | bytes 98308
  48.1 6.8 %copy-start.5 = (bf16[8,289,289]{1,2,0:T(8,128)(2,1)S(1)}, bf16[8,289,289]{1,2,0:T(8,128)(2,1)}, u32[]{:S(2)}) copy-start(bf16[8,289,289]{1,2,0:T(8,128)(2,1)} %copy.52) | copy-start | bytes 4009012
  54.9 1.7 %copy-start.12 = (s32[8,64]{1,0:T(8,128)S(1)}, s32[8,64]{1,0:T(8,128)}, u32[]{:S(2)}) copy-start(s32[8,64]{1,0:T(8,128)} %param.16) | copy-start | bytes 6148
  54.9 4.8 %copy-start.4 = (bf16[8,289,289]{2,0,1:T(8,128)(2,1)S(1)}, bf16[8,289,289]{2,0,1:T(8,128)(2,1)}, u32[]{:S(2)}) copy-start(bf16[8,289,289]{2,0,1:T(8,128)(2,1)} %gather_fusion) | copy-start | bytes 4009012
  59.7 29.7 %copy-start.2 = (bf16[8,289,289]{2,0,1:T(8,128)(2,1)S(1)}, bf16[8,289,289]{2,0,1:T(8,128)(2,1)}, u32[]{:S(2)}) copy-start(bf16[8,289,289]{2,0,1:T(8,128)(2,1)} %param.10) | copy-start | bytes 4009012
  90.6 37.2 %all-to-all-start.1 = ((bf16[289,8,8]{0,2,1:T(8,128)(2,1)}), bf16[289,8,8]{0,2,1:T(8,128)(2,1)S(1)}, u32[]{:S(2)}, u32[]{:S(2)}) async-start(bf16[289,8,8]{0,2,1:T(8,128)(2,1)} %broadcast_in_dim.48), calls=%async_computation.1 | async-start | bytes 98304 | tf_op jit(solution)/shard_map/all_to_all | solution.py:77
  127.8 2.9 %copy-start.8 = (bf16[1,289,289]{2,0,1:T(2,128)(2,1)S(1)}, bf16[1,289,289]{2,0,1:T(2,128)(2,1)}, u32[]{:S(2)}) copy-start(bf16[1,289,289]{2,0,1:T(2,128)(2,1)} %constant_dynamic-slice_fusion) | copy-start | bytes 501130
  128.5 4.6 %copy-start.3 = (bf16[2312,289]{0,1:T(8,128)(2,1)S(1)}, bf16[2312,289]{0,1:T(8,128)(2,1)}, u32[]{:S(2)}) copy-start(bf16[2312,289]{0,1:T(8,128)(2,1)} %reshape.147) | copy-start | bytes 4009012
  133.6 1.1 copy-start.7

commit v5 on v2

--- a/solution.py
+++ b/solution.py
@@ -102,6 +102,7 @@
         upward = lift_level(upward, up_shift).astype(jnp.bfloat16)
     row_boxes = gather_columns(upward, "gz")
     row_multi = lift_level(row_boxes, up_shift).astype(jnp.bfloat16)
+    row_multi, arrived = lax.optimization_barrier((row_multi, arrived))
     coarse_multi = gather_columns(row_multi, ("gx", "gy"))
     coarse_cols = coarse_src[:, coarse_box]
     coarse_kinds = coarse_kind[:, coarse_box]

time: 132 us -> 133 us (level)
  the two profiles are of different devices: /device:TPU:8 before, /device:TPU:1 now
where the time goes in v5:
time: 133 us
  local copies, waits for them, and re-layouts  38.9 us (29%)
  starting transfers between devices  36.7 us (28%)
  Pallas kernels  26.6 us (20%)
  waiting for transfers between devices  17.4 us (13%)
  matrix products  9.03 us (7%)
  other arithmetic  3.57 us (3%)
    all_to_all x2, starting transfers between devices, gather_columns(): return lax.all_to_all(spread, axes, split_axis=1, concat_axis=1, tiled=True)  27.5 us
    pallas_call x1, Pallas kernels, far_field(): pl.pallas_call(far_kernel, out_shape=jax.ShapeDtypeStruct((targets, LANES...  26.6 us
    all_to_all x1, waiting for transfers between devices, on_device(): lax.all_to_all(outgoing, ('gy', 'gz'), split_axis=1, concat_axis=1, tiled...  11.4 us
    all_to_all x1, starting transfers between devices, on_device(): lax.all_to_all(outgoing, ('gy', 'gz'), split_axis=1, concat_axis=1, tiled...  9.13 us
    unnamed x27, local copies, waits for them, and re-layouts  8.97 us
    gather x1, local copies, waits for them, and re-layouts, on_device(): jnp.take(far_shift, coarse_kinds, axis=0).transpose(1, 0, 2)  6.82 us
    all_to_all x2, waiting for transfers between devices, gather_columns(): return lax.all_to_all(spread, axes, split_axis=1, concat_axis=1, tiled=True)  6.05 us
    reshape x1, local copies, waits for them, and re-layouts, lift_level(): shift_table = up_shift.transpose(1, 0, 2).reshape(coefs, 8 * coefs)  4.21 us
  transfers between devices with their start and end apart: 3, of which 2 were waited for; matrix products, arithmetic and copies ran while one was open for 25% of the time, Pallas kernels for 20%

profile of v5, /device:TPU:1, one launch (start us, length us, event | category | flops | bytes accessed | tf_op | source)
XLA Modules:
  0.0 132.5 jit_solution(18128354745674489469)
XLA Ops:
  0.0 1.2 copy.37
  1.2 0.0 copy-start.2
  1.2 4.2 %reshape.149 = bf16[289,2312]{1,0:T(8,128)(2,1)} reshape(bf16[289,8,289]{2,1,0:T(8,128)(2,1)} %bitcast.112) | data formatting | bytes 2672672 | tf_op jit(solution)/shard_map/reshape | solution.py:16
  5.4 0.0 copy-done.2
  5.4 0.7 fusion.17
  6.1 0.0 copy-start.8
  6.2 0.6 fusion.26
  6.7 0.1 reshape.184
  6.9 1.9 %convolution_reduce_fusion.1 = bf16[289]{0:T(512)(128)(2,1)S(1)} fusion(bf16[2312,1]{0,1:T(2,128)(2,1)S(1)} %reshape.184, bf16[289,2312]{1,0:T(8,128)(2,1)} %reshape.149), kind=kOutput, calls=%fused_computation.28 | convolution fusion | flops 1336336 | bytes 1341538 | tf_op jit(solution)/shard_map/dot_general | solution.py:17
  8.7 0.6 reshape.150
  9.4 15.7 %all-to-all-start = ((bf16[289,16,1]{0,2,1:T(2,128)(2,1)}), bf16[289,16,1]{0,2,1:T(2,128)(2,1)S(1)}, u32[]{:S(2)}, u32[]{:S(2)}) async-start(bf16[289,16,1]{0,2,1:T(2,128)(2,1)} %reshape.150), calls=%async_computation | async-start | bytes 49152 | tf_op jit(solution)/shard_map/all_to_all | solution.py:77
  25.1 0.0 copy-done.8
  25.1 0.1 copy.45
  25.2 0.1 reshape.153
  25.3 3.9 %gather_fusion.1 = bf16[1024,289]{1,0:T(8,128)(2,1)S(1)} fusion(bf16[289,512]{0,1:T(8,128)(2,1)S(1)} %copy.37, s32[1024]{0:T(1024)S(1)} %broadcast_clamp_fusion), kind=kCustom, calls=%fused_computation.1 | custom fusion | bytes 1187840 | tf_op jit(solution)/shard_map/jit(_take)/gather | solution.py:98
  29.2 0.0 copy-start.6
  29.3 0.0 copy-start.7
  29.3 0.1 copy.44
  29.4 0.0 copy-start
  29.4 1.1 broadcast_select_fusion
  30.5 6.1 %all-to-all-done = bf16[289,16,1]{0,2,1:T(2,128)(2,1)S(1)} async-done(((bf16[289,16,1]{0,2,1:T(2,128)(2,1)}), bf16[289,16,1]{0,2,1:T(2,128)(2,1)S(1)}, u32[]{:S(2)}, u32[]{:S(2)}) %all-to-all-start) | async-done | bytes 9280 | tf_op jit(solution)/shard_map/all_to_all | solution.py:77
  36.5 9.1 %all-to-all-start.1 = ((bf16[289,64,16]{0,2,1:T(8,128)(2,1)}), bf16[289,64,16]{0,2,1:T(8,128)(2,1)S(1)}, u32[]{:S(2)}, u32[]{:S(2)}) async-start(bf16[289,64,16]{0,2,1:T(8,128)(2,1)} %broadcast_select_fusion), calls=%async_computation.1 | async-start | bytes 1572864 | tf_op jit(solution)/shard_map/all_to_all | solution.py:99
  45.7 0.0 copy-done.6
  45.7 0.0 copy-done.7
  45.7 0.1 copy.48
  45.9 0.7 reshape.157.idx_ref
  46.6 0.0 copy-done
  46.6 2.8 %copy.50 = bf16[8,289,289]{1,2,0:T(8,128)(2,1)} copy(bf16[8,289,289]{2,0,1:T(8,128)(2,1)S(1)} %copy-done) | data formatting | bytes 2672672 | tf_op args[3]
  49.4 4.2 %copy.47 = bf16[8,289,289]{1,0,2:T(8,128)(2,1)} copy(bf16[8,289,289]{2,0,1:T(8,128)(2,1)} %param.11) | data formatting | bytes 2672672 | tf_op args[2]
  53.6 4.1 %reshape.154 = bf16[2312,289]{0,1:T(8,128)(2,1)} reshape(bf16[8,289,289]{1,0,2:T(8,128)(2,1)} %copy.47) | data formatting | bytes 2672672 | tf_op jit(solution)/shard_map/reshape | solution.py:24
  57.7 0.0 copy-done.9
  57.7 0.2 fusion.52
  57.9 6.8 %gather_fusion = bf16[8,289,289]{2,0,1:T(8,128)(2,1)} fusion(bf16[8,289,289]{2,0,1:T(8,128)(2,1)S(1)} %copy-done, s32[1024]{0:T(1024)S(1)} %pad_clamp_fusion.1), kind=kCustom, calls=%fused_computation | custom fusion | bytes 2672704 | tf_op jit(solution)/shard_map/jit(_take)/gather | solution.py:112
  64.7 3.3 %pad.9.fs_ref = bf16[8,384,384]{2,1,0:T(8,128)(2,1)} pad(bf16[8,289,289]{2,1,0:T(8,128)(2,1)} %bitcast.116, bf16[]{:T(256)} %constant.89.clone.1), padding=0_0x0_95x0_95 | pad | bytes 3695634 | tf_op jit(solution)/shard_map/jit(_pad)/pad | solution.py:56
  68.0 0.0 copy-done.10
  68.0 0.2 fusion.53
  68.2 0.2 and_reduce_fusion
  68.4 1.9 %constant_dynamic-slice_fusion = bf16[1,289,289]{2,0,1:T(2,128)(2,1)S(1)} fusion(bf16[8,289,289]{2,0,1:T(8,128)(2,1)} %param.11, s32[]{:T(128)S(6)} %select_n.70), kind=kLoop, calls=%fused_computation.59 | loop fusion | bytes 334088 | tf_op jit(solution)/shard_map/dynamic_slice | solution.py:120
  70.4 0.0 copy-done.4
  70.4 0.0 copy-start.3
  70.4 1.5 %select_bitcast_fusion = bf16[289,8,289]{2,1,0:T(8,128)(2,1)} fusion(bf16[8,289,289]{2,0,1:T(8,128)(2,1)S(1)} %copy-done.4, pred[8]{0:T(512)(128)(4,1)S(1)} %get-tuple-element.10), kind=kLoop, calls=%fused_computation.10 | loop fusion | flops 668168 | bytes 2672680 | tf_op jit(solution)/shard_map/jit(_take)/select_n | solution.py:112
  71.9 0.4 copy-done.3
  72.3 0.6 fusion.38
  72.9 11.4 %all-to-all-done.1 = bf16[289,64,16]{0,2,1:T(8,128)(2,1)S(1)} async-done(((bf16[289,64,16]{0,2,1:T(8,128)(2,1)}), bf16[289,64,16]{0,2,1:T(8,128)(2,1)S(1)}, u32[]{:S(2)}, u32[]{:S(2)}) %all-to-all-start.1) | async-done | bytes 591904 | tf_op jit(solution)/shard_map/all_to_all | solution.py:99
  84.3 0.6 broadcast_in_dim.45
  84.9 11.8 %all-to-all-start.2 = ((bf16[289,32,2]{0,2,1:T(2,128)(2,1)}), bf16[289,32,2]{0,2,1:T(2,128)(2,1)S(1)}, u32[]{:S(2)}, u32[]{:S(2)}) async-start(bf16[289,32,2]{0,2,1:T(2,128)(2,1)} %broadcast_in_dim.45), calls=%async_computation.2 | async-start | bytes 98304 | tf_op jit(solution)/shard_map/all_to_all | solution.py:77
  96.7 0.1 maximum_bitcast_fusion
  96.9 1.2 pad.8.buf_ref
  98.0 26.6 %shard_map.91 = f32[512,384]{1,0:T(8,128)} custom-call(s32[8192]{0:T(1024)} %reshape.157.idx_ref, bf16[1536,384]{1,0:T(8,128)(2,1)} %pad.8.buf_ref, bf16[8,384,384]{2,1,0:T(8,128)(2,1)} %pad.9.fs_ref), custom_call_target="tpu_custom_call" | custom-call | tf_op jit(solution)/shard_map/pallas_call | solution.py:58
  124.6 0.0 all-to-all-done.2
  124.7 0.6 gather_fusion.2
  125.3 0.1 select_bitcast_fusion.1
  125.4 2.2 %fusion.35 = bf16[289]{0:T(512)(128)(2,1)S(1)} fusion(bf16[289,8,289]{2,1,0:T(8,128)(2,1)} %select_bitcast_fusion, bf16[8,289,1]{1,0,2:T(8,128)(2,1)S(1)} %select_bitcast_fusion.1), kind=kOutput, calls=%fused_computation.26 | convolution fusion | flops 1336336 | bytes 1341538 | tf_op jit(solution)/shard_map/dot_general | solution.py:117
  127.6 0.2 convolution_reduce_fusion
  127.8 2.2 %fusion.1 = bf16[1,8,289]{2,0,1:T(2,128)(2,1)S(1)} fusion(bf16[289,1,1]{0,1,2:T(2,128)(2,1)S(1)} %reshape.191, bf16[8,289,289]{2,0,1:T(8,128)(2,1)} %param.11), kind=kOutput, calls=%fused_computation.6 | convolution fusion | flops 1336336 | bytes 1341538 | tf_op jit(solution)/shard_map/dot_general | solution.py:23
  129.9 0.0 copy-done.1
  129.9 0.3 fusion
  130.3 0.1 convert_element_type.75
  130.4 0.0 copy-start.5
  130.4 0.4 convolution_bitcast_fusion
  130.8 0.4 reshape.155
  131.3 0.3 copy-done.5
  131.6 0.1 fusion.42
  131.7 0.9 copy.51
  (14 shorter events, 0.1 us)
Async XLA Ops:
  1.2 4.2 %copy-start.2 = (bf16[8,289,289]{2,0,1:T(8,128)(2,1)S(1)}, bf16[8,289,289]{2,0,1:T(8,128)(2,1)}, u32[]{:S(2)}) copy-start(bf16[8,289,289]{2,0,1:T(8,128)(2,1)} %param.10) | copy-start | bytes 4009012
  6.1 19.0 %copy-start.8 = (s32[1,1,64,16]{2,3,1,0:T(8,128)S(1)}, s32[1,1,64,16]{2,3,1,0:T(8,128)}, u32[]{:S(2)}) copy-start(s32[1,1,64,16]{2,3,1,0:T(8,128)} %param.13) | copy-start | bytes 12292
  9.4 27.2 %all-to-all-start = ((bf16[289,16,1]{0,2,1:T(2,128)(2,1)}), bf16[289,16,1]{0,2,1:T(2,128)(2,1)S(1)}, u32[]{:S(2)}, u32[]{:S(2)}) async-start(bf16[289,16,1]{0,2,1:T(2,128)(2,1)} %reshape.150), calls=%async_computation | async-start | bytes 49152 | tf_op jit(solution)/shard_map/all_to_all | solution.py:77
  29.2 16.5 %copy-start.6 = (s32[16,512]{1,0:T(8,128)S(1)}, s32[16,512]{1,0:T(8,128)}, u32[]{:S(2)}) copy-start(s32[16,512]{1,0:T(8,128)} %param.14) | copy-start | bytes 98308
  29.3 16.5 %copy-start.7 = (s32[16,512]{1,0:T(8,128)S(1)}, s32[16,512]{1,0:T(8,128)}, u32[]{:S(2)}) copy-start(s32[16,512]{1,0:T(8,128)} %param.15) | copy-start | bytes 98308
  29.4 17.2 %copy-start = (bf16[8,289,289]{2,0,1:T(8,128)(2,1)S(1)}, bf16[8,289,289]{2,0,1:T(8,128)(2,1)}, u32[]{:S(2)}) copy-start(bf16[8,289,289]{2,0,1:T(8,128)(2,1)} %param.12) | copy-start | bytes 4009012
  36.5 47.7 %all-to-all-start.1 = ((bf16[289,64,16]{0,2,1:T(8,128)(2,1)}), bf16[289,64,16]{0,2,1:T(8,128)(2,1)S(1)}, u32[]{:S(2)}, u32[]{:S(2)}) async-start(bf16[289,64,16]{0,2,1:T(8,128)(2,1)} %broadcast_select_fusion), calls=%async_computation.1 | async-start | bytes 1572864 | tf_op jit(solution)/shard_map/all_to_all | solution.py:99
  53.6 4.1 %copy-start.9 = (s32[8,64]{1,0:T(8,128)S(1)}, s32[8,64]{1,0:T(8,128)}, u32[]{:S(2)}) copy-start(s32[8,64]{1,0:T(8,128)} %param.17) | copy-start | bytes 6148
  64.7 3.3 %copy-start.10 = (s32[8,64]{1,0:T(8,128)S(1)}, s32[8,64]{1,0:T(8,128)}, u32[]{:S(2)}) copy-start(s32[8,64]{1,0:T(8,128)} %param.16) | copy-start | bytes 6148
  64.7 5.7 %copy-start.4 = (bf16[8,289,289]{2,0,1:T(8,128)(2,1)S(1)}, bf16[8,289,289]{2,0,1:T(8,128)(2,1)}, u32[]{:S(2)}) copy-start(bf16[8,289,289]{2,0,1:T(8,128)(2,1)} %gather_fusion) | copy-start | bytes 4009012
  70.4 1.9 %copy-start.3 = (bf16[8,289,289]{2,0,1:T(8,128)(2,1)S(1)}, bf16[8,289,289]{2,0,1:T(8,128)(2,1)}, u32[]{:S(2)}) copy-start(bf16[8,289,289]{2,0,1:T(8,128)(2,1)} %param.10) | copy-start | bytes 4009012
  84.9 39.7 %all-to-all-start.2 = ((bf16[289,32,2]{0,2,1:T(2,128)(2,1)}), bf16[289,32,2]{0,2,1:T(2,128)(2,1)S(1)}, u32[]{:S(2)}, u32[]{:S(2)}) async-start(bf16[289,32,2]{0,2,1:T(2,128)(2,1)} %broadcast_in_dim.45), calls=%async_computation.2 | async-start | bytes 98304 | tf_op jit(solution)/shard_map/all_to_all | solution.py:77
  125.3 4.6 %copy-start.1 = (bf16[2312,289]{0,1:T(8,128)(2,1)S(1)}, bf16[2312,289]{0,1:T(8,128)(2,1)}, u32[]{:S(2)}) copy-start(bf16[2312,289]{0,1:T(8,128)(2,1)} %reshape.154) | copy-start | bytes 4009012
  130.4 1.1 copy-start.5

commit v6 on v2

--- a/solution.py
+++ b/solution.py
@@ -6,7 +6,8 @@
 from jax.sharding import PartitionSpec as P
 
 LOCAL_LEVELS = 3
-LANES = 384
+LANE = 128
+CHUNKS = 3
 
 
 def lift_level(children, up_shift):
@@ -30,43 +31,45 @@
     kinds = fs_ref.shape[0]
     rows = buf_ref.shape[0]
     for k in range(kinds):
-        table_ref[pl.ds(k * rows, rows), :] = jnp.dot(
-            buf_ref[...], fs_ref[k], preferred_element_type=jnp.float32
-        )
-    targets = out_ref.shape[0]
+        for j in range(CHUNKS):
+            part = jnp.dot(
+                buf_ref[...], fs_ref[k, :, pl.ds(j * LANE, LANE)], preferred_element_type=jnp.float32
+            )
+            table_ref[pl.ds(CHUNKS * k * rows + j, rows, stride=CHUNKS), :] = part
+    targets = out_ref.shape[0] // CHUNKS
     lists = idx_ref.shape[0] // targets
 
     def body(t, carry):
         base = t * lists
-        acc = table_ref[pl.ds(idx_ref[base], 1), :]
+        acc = table_ref[pl.ds(idx_ref[base], CHUNKS), :]
         for l in range(1, lists):
-            acc = acc + table_ref[pl.ds(idx_ref[base + l], 1), :]
-        out_ref[pl.ds(t, 1), :] = acc
+            acc = acc + table_ref[pl.ds(idx_ref[base + l], CHUNKS), :]
+        out_ref[pl.ds(t * CHUNKS, CHUNKS), :] = acc
         return carry
 
-    lax.fori_loop(0, targets, body, 0)
+    lax.fori_loop(0, targets, body, 0, unroll=8)
 
 
 def far_field(buffer, far_shift, leaf_src, leaf_kind):
     coefs, rows = buffer.shape
     kinds = far_shift.shape[0]
     lists, targets = leaf_src.shape
-    pad = LANES - coefs
-    buf_t = jnp.pad(buffer.T, ((0, 0), (0, pad)))
-    fs_t = jnp.pad(far_shift.transpose(0, 2, 1), ((0, 0), (0, pad), (0, pad)))
-    idx = (leaf_kind * rows + leaf_src).T.reshape(lists * targets)
+    width = CHUNKS * LANE
+    buf_t = jnp.pad(buffer.T, ((0, 0), (0, width - coefs)))
+    fs_t = jnp.pad(far_shift.transpose(0, 2, 1), ((0, 0), (0, width - coefs), (0, width - coefs)))
+    idx = (CHUNKS * (leaf_kind * rows + leaf_src)).T.reshape(lists * targets)
     out = pl.pallas_call(
         far_kernel,
-        out_shape=jax.ShapeDtypeStruct((targets, LANES), jnp.float32),
+        out_shape=jax.ShapeDtypeStruct((targets * CHUNKS, LANE), jnp.float32),
         in_specs=[
             pl.BlockSpec(memory_space=pltpu.SMEM),
             pl.BlockSpec(memory_space=pltpu.VMEM),
             pl.BlockSpec(memory_space=pltpu.VMEM),
         ],
         out_specs=pl.BlockSpec(memory_space=pltpu.VMEM),
-        scratch_shapes=[pltpu.VMEM((kinds * rows, LANES), jnp.float32)],
+        scratch_shapes=[pltpu.VMEM((kinds * rows * CHUNKS, LANE), jnp.float32)],
     )(idx, buf_t, fs_t)
-    return out[:, :coefs].T
+    return out.reshape(targets, width)[:, :coefs].T
 
 
 def gather_columns(column_block, axes):

time: 132 us -> 123 us (0.932)
  Pallas kernels: 26.8 us -> 17.6 us
    pallas_call x1, Pallas kernels: 26.8 us -> 17.6 us  [far_field(): pl.pallas_call(far_kernel, out_shape=jax.ShapeDtypeStruct((targets * CHUN...]
  transfers between devices with their start and end apart: 3 -> 3, of which waited for: 3 -> 3; matrix products, arithmetic and copies ran while one was open for 30% -> 33% of each run, Pallas kernels for 0% -> 0%
where the time goes in v6:
time: 123 us; the launch traced here: 122 us
  local copies, waits for them, and re-layouts  40.7 us (33%)
  starting transfers between devices  29.1 us (24%)
  waiting for transfers between devices  21.2 us (17%)
  Pallas kernels  17.6 us (14%)
  matrix products  9.87 us (8%)
  other arithmetic  3.56 us (3%)
    all_to_all x2, starting transfers between devices, gather_columns(): return lax.all_to_all(spread, axes, split_axis=1, concat_axis=1, tiled=True)  22.7 us
    pallas_call x1, Pallas kernels, far_field(): pl.pallas_call(far_kernel, out_shape=jax.ShapeDtypeStruct((targets * CHUN...  17.6 us
    all_to_all x2, waiting for transfers between devices, gather_columns(): return lax.all_to_all(spread, axes, split_axis=1, concat_axis=1, tiled=True)  13.4 us
    unnamed x23, local copies, waits for them, and re-layouts  8.28 us
    all_to_all x1, waiting for transfers between devices, on_device(): lax.all_to_all(outgoing, ('gy', 'gz'), split_axis=1, concat_axis=1, tiled...  7.78 us
    gather x1, local copies, waits for them, and re-layouts, on_device(): jnp.take(far_shift, coarse_kinds, axis=0).transpose(1, 0, 2)  6.81 us
    all_to_all x1, starting transfers between devices, on_device(): lax.all_to_all(outgoing, ('gy', 'gz'), split_axis=1, concat_axis=1, tiled...  6.35 us
    reshape x1, local copies, waits for them, and re-layouts, lift_level(): shift_table = up_shift.transpose(1, 0, 2).reshape(coefs, 8 * coefs)  4.21 us
  transfers between devices with their start and end apart: 3, of which 3 were waited for; matrix products, arithmetic and copies ran while one was open for 33% of the time, Pallas kernels for 0%

profile of v6, /device:TPU:8, one launch (start us, length us, event | category | flops | bytes accessed | tf_op | source)
XLA Modules:
  0.0 122.3 jit_solution(5653357206186950671)
XLA Ops:
  0.0 1.2 copy.38
  1.2 0.0 copy-start.2
  1.2 4.2 %reshape.152 = bf16[289,2312]{1,0:T(8,128)(2,1)} reshape(bf16[289,8,289]{2,1,0:T(8,128)(2,1)} %bitcast.112) | data formatting | bytes 2672672 | tf_op jit(solution)/shard_map/reshape | solution.py:17
  5.4 0.0 copy-done.2
  5.4 0.7 fusion.17
  6.1 0.0 copy-start.6
  6.2 0.6 fusion.26
  6.7 0.1 reshape.188
  6.9 1.9 %convolution_reduce_fusion.1 = bf16[289]{0:T(512)(128)(2,1)S(1)} fusion(bf16[2312,1]{0,1:T(2,128)(2,1)S(1)} %reshape.188, bf16[289,2312]{1,0:T(8,128)(2,1)} %reshape.152), kind=kOutput, calls=%fused_computation.28 | convolution fusion | flops 1336336 | bytes 1341538 | tf_op jit(solution)/shard_map/dot_general | solution.py:18
  8.7 0.6 reshape.153
  9.4 15.2 %all-to-all-start = ((bf16[289,16,1]{0,2,1:T(2,128)(2,1)}), bf16[289,16,1]{0,2,1:T(2,128)(2,1)S(1)}, u32[]{:S(2)}, u32[]{:S(2)}) async-start(bf16[289,16,1]{0,2,1:T(2,128)(2,1)} %reshape.153), calls=%async_computation | async-start | bytes 49152 | tf_op jit(solution)/shard_map/all_to_all | solution.py:80
  24.6 0.0 copy-done.6
  24.6 0.1 copy.48
  24.7 0.1 reshape.160
  24.8 3.9 %gather_fusion.2 = bf16[1024,289]{1,0:T(8,128)(2,1)S(1)} fusion(bf16[289,512]{0,1:T(8,128)(2,1)S(1)} %copy.38, s32[1024]{0:T(1024)S(1)} %broadcast_clamp_fusion), kind=kCustom, calls=%fused_computation.2 | custom fusion | bytes 1187840 | tf_op jit(solution)/shard_map/jit(_take)/gather | solution.py:101
  28.7 0.1 copy.47
  28.8 8.3 %all-to-all-done = bf16[289,16,1]{0,2,1:T(2,128)(2,1)S(1)} async-done(((bf16[289,16,1]{0,2,1:T(2,128)(2,1)}), bf16[289,16,1]{0,2,1:T(2,128)(2,1)S(1)}, u32[]{:S(2)}, u32[]{:S(2)}) %all-to-all-start) | async-done | bytes 9280 | tf_op jit(solution)/shard_map/all_to_all | solution.py:80
  37.1 0.6 fusion.38
  37.7 0.0 copy-start.4
  37.7 0.0 copy-start.5
  37.7 0.7 broadcast_in_dim.43
  38.4 7.5 %all-to-all-start.1 = ((bf16[289,32,2]{0,2,1:T(2,128)(2,1)}), bf16[289,32,2]{0,2,1:T(2,128)(2,1)S(1)}, u32[]{:S(2)}, u32[]{:S(2)}) async-start(bf16[289,32,2]{0,2,1:T(2,128)(2,1)} %broadcast_in_dim.43), calls=%async_computation.1 | async-start | bytes 98304 | tf_op jit(solution)/shard_map/all_to_all | solution.py:80
  45.9 0.0 copy-start
  45.9 1.1 broadcast_select_fusion
  47.0 5.1 %all-to-all-done.1 = bf16[289,32,2]{0,2,1:T(2,128)(2,1)S(1)} async-done(((bf16[289,32,2]{0,2,1:T(2,128)(2,1)}), bf16[289,32,2]{0,2,1:T(2,128)(2,1)S(1)}, u32[]{:S(2)}, u32[]{:S(2)}) %all-to-all-start.1) | async-done | bytes 37024 | tf_op jit(solution)/shard_map/all_to_all | solution.py:80
  52.1 6.3 %all-to-all-start.2 = ((bf16[289,64,16]{0,2,1:T(8,128)(2,1)}), bf16[289,64,16]{0,2,1:T(8,128)(2,1)S(1)}, u32[]{:S(2)}, u32[]{:S(2)}) async-start(bf16[289,64,16]{0,2,1:T(8,128)(2,1)} %broadcast_select_fusion), calls=%async_computation.2 | async-start | bytes 1572864 | tf_op jit(solution)/shard_map/all_to_all | solution.py:102
  58.5 0.0 copy-done.4
  58.5 0.0 copy-done.5
  58.5 0.1 copy.46
  58.7 0.8 reshape.158.idx_ref
  59.4 0.0 copy-done
  59.4 2.8 %copy.51 = bf16[8,289,289]{1,2,0:T(8,128)(2,1)} copy(bf16[8,289,289]{2,0,1:T(8,128)(2,1)S(1)} %copy-done) | data formatting | bytes 2672672 | tf_op args[3]
  62.2 4.2 %copy.45 = bf16[8,289,289]{1,0,2:T(8,128)(2,1)} copy(bf16[8,289,289]{2,0,1:T(8,128)(2,1)} %param.11) | data formatting | bytes 2672672 | tf_op args[2]
  66.4 0.0 copy-start.7
  66.4 4.1 %reshape.155 = bf16[2312,289]{0,1:T(8,128)(2,1)} reshape(bf16[8,289,289]{1,0,2:T(8,128)(2,1)} %copy.45) | data formatting | bytes 2672672 | tf_op jit(solution)/shard_map/reshape | solution.py:25
  70.5 0.0 copy-done.7
  70.5 0.2 fusion.52
  70.7 6.8 %gather_fusion = bf16[8,289,289]{2,0,1:T(8,128)(2,1)} fusion(bf16[8,289,289]{2,0,1:T(8,128)(2,1)S(1)} %copy-done, s32[1024]{0:T(1024)S(1)} %pad_clamp_fusion.1), kind=kCustom, calls=%fused_computation | custom fusion | bytes 2672704 | tf_op jit(solution)/shard_map/jit(_take)/gather | solution.py:114
  77.5 0.0 copy-start.8
  77.5 0.0 copy-start.3
  77.5 3.3 %pad.9.fs_ref = bf16[8,384,384]{2,1,0:T(8,128)(2,1)} pad(bf16[8,289,289]{2,1,0:T(8,128)(2,1)} %bitcast.116, bf16[]{:T(256)} %constant.90.clone.1), padding=0_0x0_95x0_95 | pad | bytes 3695634 | tf_op jit(solution)/shard_map/jit(_pad)/pad | solution.py:59
  80.8 0.0 copy-done.8
  80.8 0.2 fusion.53
  81.0 0.2 and_reduce_fusion
  81.2 1.9 %constant_dynamic-slice_fusion = bf16[1,289,289]{2,0,1:T(2,128)(2,1)S(1)} fusion(bf16[8,289,289]{2,0,1:T(8,128)(2,1)} %param.11, s32[]{:T(128)S(6)} %select_n.70), kind=kLoop, calls=%fused_computation.59 | loop fusion | bytes 334088 | tf_op jit(solution)/shard_map/dynamic_slice | solution.py:122
  83.2 0.0 copy-done.3
  83.2 1.6 %select_bitcast_fusion = bf16[289,8,289]{2,1,0:T(8,128)(2,1)} fusion(bf16[8,289,289]{2,0,1:T(8,128)(2,1)S(1)} %copy-done.3, pred[8]{0:T(512)(128)(4,1)S(1)} %get-tuple-element.6), kind=kLoop, calls=%fused_computation.10 | loop fusion | flops 668168 | bytes 2672680 | tf_op jit(solution)/shard_map/jit(_take)/select_n | solution.py:114
  84.8 0.6 gather_fusion.1
  85.4 0.1 select_bitcast_fusion.1
  85.5 2.2 %fusion.35 = bf16[289]{0:T(512)(128)(2,1)S(1)} fusion(bf16[289,8,289]{2,1,0:T(8,128)(2,1)} %select_bitcast_fusion, bf16[8,289,1]{1,0,2:T(8,128)(2,1)S(1)} %select_bitcast_fusion.1), kind=kOutput, calls=%fused_computation.26 | convolution fusion | flops 1336336 | bytes 1341538 | tf_op jit(solution)/shard_map/dot_general | solution.py:119
  87.7 0.2 convolution_reduce_fusion
  87.9 2.2 %fusion.1 = bf16[1,8,289]{2,0,1:T(2,128)(2,1)S(1)} fusion(bf16[289,1,1]{0,1,2:T(2,128)(2,1)S(1)} %reshape.195, bf16[8,289,289]{2,0,1:T(8,128)(2,1)} %param.11), kind=kOutput, calls=%fused_computation.6 | convolution fusion | flops 1336336 | bytes 1341538 | tf_op jit(solution)/shard_map/dot_general | solution.py:24
  90.0 0.0 copy-done.1
  90.1 0.3 fusion
  90.4 0.1 convert_element_type.75
  90.5 1.2 convolution_bitcast_fusion
  91.7 1.5 %reshape.156 = f32[8,289,64]{1,0,2:T(8,128)S(1)} reshape(f32[2312,64]{0,1:T(8,128)} %convolution_bitcast_fusion) | data formatting | bytes 1183744 | tf_op jit(solution)/shard_map/reshape | solution.py:27
  93.3 7.8 %all-to-all-done.2 = bf16[289,64,16]{0,2,1:T(8,128)(2,1)S(1)} async-done(((bf16[289,64,16]{0,2,1:T(8,128)(2,1)}), bf16[289,64,16]{0,2,1:T(8,128)(2,1)S(1)}, u32[]{:S(2)}, u32[]{:S(2)}) %all-to-all-start.2) | async-done | bytes 591904 | tf_op jit(solution)/shard_map/all_to_all | solution.py:102
  101.0 0.1 maximum_bitcast_fusion
  101.2 1.2 pad.8.buf_ref
  102.3 17.6 %shard_map.91 = f32[1536,128]{1,0:T(8,128)} custom-call(s32[8192]{0:T(1024)} %reshape.158.idx_ref, bf16[1536,384]{1,0:T(8,128)(2,1)} %pad.8.buf_ref, bf16[8,384,384]{2,1,0:T(8,128)(2,1)} %pad.9.fs_ref), custom_call_target="tpu_custom_call" | custom-call | tf_op jit(solution)/shard_map/pallas_call | solution.py:61
  120.0 1.3 %reshape.161 = f32[512,384]{1,0:T(8,128)S(1)} reshape(f32[1536,128]{1,0:T(8,128)} %shard_map.91) | data formatting | bytes 1572864 | tf_op jit(solution)/shard_map/reshape | solution.py:72
  121.3 0.1 fusion.42
  121.4 0.9 copy.52
  (11 shorter events, 0.1 us)
Async XLA Ops:
  1.2 4.2 %copy-start.2 = (bf16[8,289,289]{2,0,1:T(8,128)(2,1)S(1)}, bf16[8,289,289]{2,0,1:T(8,128)(2,1)}, u32[]{:S(2)}) copy-start(bf16[8,289,289]{2,0,1:T(8,128)(2,1)} %param.10) | copy-start | bytes 4009012
  6.1 18.4 %copy-start.6 = (s32[1,1,64,16]{2,3,1,0:T(8,128)S(1)}, s32[1,1,64,16]{2,3,1,0:T(8,128)}, u32[]{:S(2)}) copy-start(s32[1,1,64,16]{2,3,1,0:T(8,128)} %param.13) | copy-start | bytes 12292
  9.4 27.8 %all-to-all-start = ((bf16[289,16,1]{0,2,1:T(2,128)(2,1)}), bf16[289,16,1]{0,2,1:T(2,128)(2,1)S(1)}, u32[]{:S(2)}, u32[]{:S(2)}) async-start(bf16[289,16,1]{0,2,1:T(2,128)(2,1)} %reshape.153), calls=%async_computation | async-start | bytes 49152 | tf_op jit(solution)/shard_map/all_to_all | solution.py:80
  37.7 20.8 %copy-start.4 = (s32[16,512]{1,0:T(8,128)S(1)}, s32[16,512]{1,0:T(8,128)}, u32[]{:S(2)}) copy-start(s32[16,512]{1,0:T(8,128)} %param.14) | copy-start | bytes 98308
  37.7 20.8 %copy-start.5 = (s32[16,512]{1,0:T(8,128)S(1)}, s32[16,512]{1,0:T(8,128)}, u32[]{:S(2)}) copy-start(s32[16,512]{1,0:T(8,128)} %param.15) | copy-start | bytes 98308
  38.4 13.7 %all-to-all-start.1 = ((bf16[289,32,2]{0,2,1:T(2,128)(2,1)}), bf16[289,32,2]{0,2,1:T(2,128)(2,1)S(1)}, u32[]{:S(2)}, u32[]{:S(2)}) async-start(bf16[289,32,2]{0,2,1:T(2,128)(2,1)} %broadcast_in_dim.43), calls=%async_computation.1 | async-start | bytes 98304 | tf_op jit(solution)/shard_map/all_to_all | solution.py:80
  45.9 13.5 %copy-start = (bf16[8,289,289]{2,0,1:T(8,128)(2,1)S(1)}, bf16[8,289,289]{2,0,1:T(8,128)(2,1)}, u32[]{:S(2)}) copy-start(bf16[8,289,289]{2,0,1:T(8,128)(2,1)} %param.12) | copy-start | bytes 4009012
  52.1 48.9 %all-to-all-start.2 = ((bf16[289,64,16]{0,2,1:T(8,128)(2,1)}), bf16[289,64,16]{0,2,1:T(8,128)(2,1)S(1)}, u32[]{:S(2)}, u32[]{:S(2)}) async-start(bf16[289,64,16]{0,2,1:T(8,128)(2,1)} %broadcast_select_fusion), calls=%async_computation.2 | async-start | bytes 1572864 | tf_op jit(solution)/shard_map/all_to_all | solution.py:102
  66.4 4.1 %copy-start.7 = (s32[8,64]{1,0:T(8,128)S(1)}, s32[8,64]{1,0:T(8,128)}, u32[]{:S(2)}) copy-start(s32[8,64]{1,0:T(8,128)} %param.17) | copy-start | bytes 6148
  77.5 3.3 %copy-start.8 = (s32[8,64]{1,0:T(8,128)S(1)}, s32[8,64]{1,0:T(8,128)}, u32[]{:S(2)}) copy-start(s32[8,64]{1,0:T(8,128)} %param.16) | copy-start | bytes 6148
  77.5 5.7 %copy-start.3 = (bf16[8,289,289]{2,0,1:T(8,128)(2,1)S(1)}, bf16[8,289,289]{2,0,1:T(8,128)(2,1)}, u32[]{:S(2)}) copy-start(bf16[8,289,289]{2,0,1:T(8,128)(2,1)} %gather_fusion) | copy-start | bytes 4009012
  85.5 4.6 %copy-start.1 = (bf16[2312,289]{0,1:T(8,128)(2,1)S(1)}, bf16[2312,289]{0,1:T(8,128)(2,1)}, u32[]{:S(2)}) copy-start(bf16[2312,289]{0,1:T(8,128)(2,1)} %reshape.155) | copy-start | bytes 4009012

commit v7 on v6

--- a/solution.py
+++ b/solution.py
@@ -13,9 +13,11 @@
 def lift_level(children, up_shift):
     coefs = children.shape[0]
     count = children.shape[1] // 8
-    child_stack = children.reshape(coefs, count, 8).transpose(2, 0, 1).reshape(8 * coefs, count)
-    shift_table = up_shift.transpose(1, 0, 2).reshape(coefs, 8 * coefs)
-    return jnp.dot(shift_table, child_stack, preferred_element_type=jnp.float32)
+    child_stack = children.reshape(coefs, count, 8).transpose(2, 0, 1)
+    per_octant = lax.dot_general(
+        up_shift, child_stack, (((2,), (1,)), ((0,), (0,))), preferred_element_type=jnp.float32
+    )
+    return per_octant.sum(axis=0)
 
 
 def lower_level(parent, down_shift):

time: 123 us -> 119 us (0.967)
  local copies, waits for them, and re-layouts: 40.7 us -> 35.4 us
  waiting for transfers between devices: 21.2 us -> 23.1 us
    reshape x1 -> x0, local copies, waits for them, and re-layouts: 4.21 us -> none  [lift_level(): shift_table = up_shift.transpose(1, 0, 2).reshape(coefs, 8 * coefs)]
    all_to_all x1, waiting for transfers between devices: 7.78 us -> 9.68 us  [on_device(): lax.all_to_all(outgoing, ('gy', 'gz'), split_axis=1, concat_axis=1, tiled...]
  transfers between devices with their start and end apart: 3 -> 3, of which waited for: 3 -> 3; matrix products, arithmetic and copies ran while one was open for 33% -> 32% of each run, Pallas kernels for 0% -> 0%
where the time goes in v7:
time: 119 us; the launch traced here: 118 us
  local copies, waits for them, and re-layouts  35.4 us (30%)
  starting transfers between devices  29.1 us (24%)
  waiting for transfers between devices  23.1 us (19%)
  Pallas kernels  17.6 us (15%)
  matrix products  9.27 us (8%)
  other arithmetic  3.56 us (3%)
    all_to_all x2, starting transfers between devices, gather_columns(): return lax.all_to_all(spread, axes, split_axis=1, concat_axis=1, tiled=True)  22.7 us
    pallas_call x1, Pallas kernels, far_field(): pl.pallas_call(far_kernel, out_shape=jax.ShapeDtypeStruct((targets * CHUN...  17.6 us
    all_to_all x2, waiting for transfers between devices, gather_columns(): return lax.all_to_all(spread, axes, split_axis=1, concat_axis=1, tiled=True)  13.4 us
    all_to_all x1, waiting for transfers between devices, on_device(): lax.all_to_all(outgoing, ('gy', 'gz'), split_axis=1, concat_axis=1, tiled...  9.68 us
    unnamed x23, local copies, waits for them, and re-layouts  8.41 us
    gather x1, local copies, waits for them, and re-layouts, on_device(): jnp.take(far_shift, coarse_kinds, axis=0).transpose(1, 0, 2)  6.81 us
    all_to_all x1, starting transfers between devices, on_device(): lax.all_to_all(outgoing, ('gy', 'gz'), split_axis=1, concat_axis=1, tiled...  6.35 us
    reshape x1, local copies, waits for them, and re-layouts, lower_level(): down_shift.reshape(8 * coefs, coefs)  4.08 us
  transfers between devices with their start and end apart: 3, of which 3 were waited for; matrix products, arithmetic and copies ran while one was open for 32% of the time, Pallas kernels for 0%

profile of v7, /device:TPU:8, one launch (start us, length us, event | category | flops | bytes accessed | tf_op | source)
XLA Modules:
  0.0 118.3 jit_solution(12367746837694007545)
XLA Ops:
  0.0 0.0 copy-start.3
  0.0 1.3 %copy.34 = bf16[289,512]{0,1:T(8,128)(2,1)S(1)} copy(bf16[289,512]{1,0:T(8,128)(2,1)} %param.9) | data formatting | bytes 591872 | tf_op args[0]
  1.3 2.2 %fusion.19 = bf16[289,8,8]{0,2,1:T(8,128)(2,1)S(1)} fusion(bf16[8,289,289]{2,0,1:T(8,128)(2,1)} %param.10, bf16[8,289,64]{1,0,2:T(8,128)(2,1)S(1)} %bitcast.102), kind=kOutput, calls=%fused_computation.22 | convolution fusion | flops 85544000 | bytes 1669264 | tf_op jit(solution)/shard_map/dot_general | solution.py:17
  3.5 0.0 copy-done.3
  3.5 0.0 copy-start.6
  3.6 0.6 fusion.28
  4.1 0.6 fusion.37
  4.8 0.6 reshape.141
  5.4 15.2 %all-to-all-start = ((bf16[289,16,1]{0,2,1:T(2,128)(2,1)}), bf16[289,16,1]{0,2,1:T(2,128)(2,1)S(1)}, u32[]{:S(2)}, u32[]{:S(2)}) async-start(bf16[289,16,1]{0,2,1:T(2,128)(2,1)} %reshape.141), calls=%async_computation | async-start | bytes 49152 | tf_op jit(solution)/shard_map/all_to_all | solution.py:82
  20.6 0.0 copy-done.6
  20.6 0.1 copy.44
  20.7 0.1 reshape.148
  20.8 3.9 %gather_fusion.2 = bf16[1024,289]{1,0:T(8,128)(2,1)S(1)} fusion(bf16[289,512]{0,1:T(8,128)(2,1)S(1)} %copy.34, s32[1024]{0:T(1024)S(1)} %broadcast_clamp_fusion), kind=kCustom, calls=%fused_computation.2 | custom fusion | bytes 1187840 | tf_op jit(solution)/shard_map/jit(_take)/gather | solution.py:103
  24.7 0.1 copy.43
  24.8 8.3 %all-to-all-done = bf16[289,16,1]{0,2,1:T(2,128)(2,1)S(1)} async-done(((bf16[289,16,1]{0,2,1:T(2,128)(2,1)}), bf16[289,16,1]{0,2,1:T(2,128)(2,1)S(1)}, u32[]{:S(2)}, u32[]{:S(2)}) %all-to-all-start) | async-done | bytes 9280 | tf_op jit(solution)/shard_map/all_to_all | solution.py:82
  33.2 0.6 fusion.43
  33.7 0.0 copy-start.4
  33.8 0.0 copy-start.5
  33.8 0.7 broadcast_in_dim.43
  34.4 7.5 %all-to-all-start.1 = ((bf16[289,32,2]{0,2,1:T(2,128)(2,1)}), bf16[289,32,2]{0,2,1:T(2,128)(2,1)S(1)}, u32[]{:S(2)}, u32[]{:S(2)}) async-start(bf16[289,32,2]{0,2,1:T(2,128)(2,1)} %broadcast_in_dim.43), calls=%async_computation.1 | async-start | bytes 98304 | tf_op jit(solution)/shard_map/all_to_all | solution.py:82
  42.0 0.0 copy-start
  42.0 1.1 broadcast_select_fusion
  43.1 5.1 %all-to-all-done.1 = bf16[289,32,2]{0,2,1:T(2,128)(2,1)S(1)} async-done(((bf16[289,32,2]{0,2,1:T(2,128)(2,1)}), bf16[289,32,2]{0,2,1:T(2,128)(2,1)S(1)}, u32[]{:S(2)}, u32[]{:S(2)}) %all-to-all-start.1) | async-done | bytes 37024 | tf_op jit(solution)/shard_map/all_to_all | solution.py:82
  48.1 6.3 %all-to-all-start.2 = ((bf16[289,64,16]{0,2,1:T(8,128)(2,1)}), bf16[289,64,16]{0,2,1:T(8,128)(2,1)S(1)}, u32[]{:S(2)}, u32[]{:S(2)}) async-start(bf16[289,64,16]{0,2,1:T(8,128)(2,1)} %broadcast_select_fusion), calls=%async_computation.2 | async-start | bytes 1572864 | tf_op jit(solution)/shard_map/all_to_all | solution.py:104
  54.5 0.0 copy-done.4
  54.5 0.0 copy-done.5
  54.6 0.1 copy.42
  54.7 0.8 reshape.146.idx_ref
  55.4 0.0 copy-done
  55.4 2.8 %copy.47 = bf16[8,289,289]{1,2,0:T(8,128)(2,1)} copy(bf16[8,289,289]{2,0,1:T(8,128)(2,1)S(1)} %copy-done) | data formatting | bytes 2672672 | tf_op args[3]
  58.2 4.2 %copy.41 = bf16[8,289,289]{1,0,2:T(8,128)(2,1)} copy(bf16[8,289,289]{2,0,1:T(8,128)(2,1)} %param.11) | data formatting | bytes 2672672 | tf_op args[2]
  62.4 0.0 copy-start.7
  62.4 4.1 %reshape.143 = bf16[2312,289]{0,1:T(8,128)(2,1)} reshape(bf16[8,289,289]{1,0,2:T(8,128)(2,1)} %copy.41) | data formatting | bytes 2672672 | tf_op jit(solution)/shard_map/reshape | solution.py:27
  66.5 0.0 copy-done.7
  66.5 0.2 fusion.58
  66.7 6.8 %gather_fusion = bf16[8,289,289]{2,0,1:T(8,128)(2,1)} fusion(bf16[8,289,289]{2,0,1:T(8,128)(2,1)S(1)} %copy-done, s32[1024]{0:T(1024)S(1)} %pad_clamp_fusion.1), kind=kCustom, calls=%fused_computation | custom fusion | bytes 2672704 | tf_op jit(solution)/shard_map/jit(_take)/gather | solution.py:116
  73.5 0.0 copy-start.8
  73.5 0.0 copy-start.2
  73.5 3.3 %pad.9.fs_ref = bf16[8,384,384]{2,1,0:T(8,128)(2,1)} pad(bf16[8,289,289]{2,1,0:T(8,128)(2,1)} %bitcast.103, bf16[]{:T(256)} %constant.91.clone.1), padding=0_0x0_95x0_95 | pad | bytes 3695634 | tf_op jit(solution)/shard_map/jit(_pad)/pad | solution.py:61
  76.8 0.0 copy-done.8
  76.8 0.2 fusion.59
  77.0 0.2 and_reduce_fusion
  77.3 1.9 %constant_dynamic-slice_fusion = bf16[1,289,289]{2,0,1:T(2,128)(2,1)S(1)} fusion(bf16[8,289,289]{2,0,1:T(8,128)(2,1)} %param.11, s32[]{:T(128)S(6)} %select_n.70), kind=kLoop, calls=%fused_computation.62 | loop fusion | bytes 334088 | tf_op jit(solution)/shard_map/dynamic_slice | solution.py:124
  79.2 0.0 copy-done.2
  79.2 1.6 %select_bitcast_fusion = bf16[289,8,289]{2,1,0:T(8,128)(2,1)} fusion(bf16[8,289,289]{2,0,1:T(8,128)(2,1)S(1)} %copy-done.2, pred[8]{0:T(512)(128)(4,1)S(1)} %get-tuple-element.6), kind=kLoop, calls=%fused_computation.10 | loop fusion | flops 668168 | bytes 2672680 | tf_op jit(solution)/shard_map/jit(_take)/select_n | solution.py:116
  80.8 0.6 gather_fusion.1
  81.4 0.1 select_bitcast_fusion.1
  81.5 0.0 copy-start.1
  81.5 2.2 %fusion.40 = bf16[289]{0:T(512)(128)(2,1)S(1)} fusion(bf16[289,8,289]{2,1,0:T(8,128)(2,1)} %select_bitcast_fusion, bf16[8,289,1]{1,0,2:T(8,128)(2,1)S(1)} %select_bitcast_fusion.1), kind=kOutput, calls=%fused_computation.29 | convolution fusion | flops 1336336 | bytes 1341538 | tf_op jit(solution)/shard_map/dot_general | solution.py:121
  83.7 0.2 convolution_reduce_fusion
  83.9 2.2 %fusion.1 = bf16[1,8,289]{2,0,1:T(2,128)(2,1)S(1)} fusion(bf16[289,1,1]{0,1,2:T(2,128)(2,1)S(1)} %reshape.183, bf16[8,289,289]{2,0,1:T(8,128)(2,1)} %param.11), kind=kOutput, calls=%fused_computation.6 | convolution fusion | flops 1336336 | bytes 1341538 | tf_op jit(solution)/shard_map/dot_general | solution.py:26
  86.1 0.0 copy-done.1
  86.1 0.3 fusion
  86.4 0.1 convert_element_type.75
  86.6 0.4 convolution_bitcast_fusion
  86.9 0.4 reshape.144
  87.4 9.7 %all-to-all-done.2 = bf16[289,64,16]{0,2,1:T(8,128)(2,1)S(1)} async-done(((bf16[289,64,16]{0,2,1:T(8,128)(2,1)}), bf16[289,64,16]{0,2,1:T(8,128)(2,1)S(1)}, u32[]{:S(2)}, u32[]{:S(2)}) %all-to-all-start.2) | async-done | bytes 591904 | tf_op jit(solution)/shard_map/all_to_all | solution.py:104
  97.1 0.1 maximum_bitcast_fusion
  97.2 1.2 pad.8.buf_ref
  98.4 17.6 %shard_map.91 = f32[1536,128]{1,0:T(8,128)} custom-call(s32[8192]{0:T(1024)} %reshape.146.idx_ref, bf16[1536,384]{1,0:T(8,128)(2,1)} %pad.8.buf_ref, bf16[8,384,384]{2,1,0:T(8,128)(2,1)} %pad.9.fs_ref), custom_call_target="tpu_custom_call" | custom-call | tf_op jit(solution)/shard_map/pallas_call | solution.py:63
  116.0 1.3 %reshape.149 = f32[512,384]{1,0:T(8,128)S(1)} reshape(f32[1536,128]{1,0:T(8,128)} %shard_map.91) | data formatting | bytes 1572864 | tf_op jit(solution)/shard_map/reshape | solution.py:74
  117.3 0.1 fusion.47
  117.4 0.9 copy.48
  (10 shorter events, 0.1 us)
Async XLA Ops:
  0.0 3.5 %copy-start.3 = (bf16[8,289,289]{2,0,1:T(8,128)(2,1)S(1)}, bf16[8,289,289]{2,0,1:T(8,128)(2,1)}, u32[]{:S(2)}) copy-start(bf16[8,289,289]{2,0,1:T(8,128)(2,1)} %param.10) | copy-start | bytes 4009012
  3.5 17.0 %copy-start.6 = (s32[1,1,64,16]{2,3,1,0:T(8,128)S(1)}, s32[1,1,64,16]{2,3,1,0:T(8,128)}, u32[]{:S(2)}) copy-start(s32[1,1,64,16]{2,3,1,0:T(8,128)} %param.13) | copy-start | bytes 12292
  5.4 27.8 %all-to-all-start = ((bf16[289,16,1]{0,2,1:T(2,128)(2,1)}), bf16[289,16,1]{0,2,1:T(2,128)(2,1)S(1)}, u32[]{:S(2)}, u32[]{:S(2)}) async-start(bf16[289,16,1]{0,2,1:T(2,128)(2,1)} %reshape.141), calls=%async_computation | async-start | bytes 49152 | tf_op jit(solution)/shard_map/all_to_all | solution.py:82
  33.7 20.8 %copy-start.4 = (s32[16,512]{1,0:T(8,128)S(1)}, s32[16,512]{1,0:T(8,128)}, u32[]{:S(2)}) copy-start(s32[16,512]{1,0:T(8,128)} %param.14) | copy-start | bytes 98308
  33.8 20.8 %copy-start.5 = (s32[16,512]{1,0:T(8,128)S(1)}, s32[16,512]{1,0:T(8,128)}, u32[]{:S(2)}) copy-start(s32[16,512]{1,0:T(8,128)} %param.15) | copy-start | bytes 98308
  34.4 13.7 %all-to-all-start.1 = ((bf16[289,32,2]{0,2,1:T(2,128)(2,1)}), bf16[289,32,2]{0,2,1:T(2,128)(2,1)S(1)}, u32[]{:S(2)}, u32[]{:S(2)}) async-start(bf16[289,32,2]{0,2,1:T(2,128)(2,1)} %broadcast_in_dim.43), calls=%async_computation.1 | async-start | bytes 98304 | tf_op jit(solution)/shard_map/all_to_all | solution.py:82
  42.0 13.5 %copy-start = (bf16[8,289,289]{2,0,1:T(8,128)(2,1)S(1)}, bf16[8,289,289]{2,0,1:T(8,128)(2,1)}, u32[]{:S(2)}) copy-start(bf16[8,289,289]{2,0,1:T(8,128)(2,1)} %param.12) | copy-start | bytes 4009012
  48.1 48.9 %all-to-all-start.2 = ((bf16[289,64,16]{0,2,1:T(8,128)(2,1)}), bf16[289,64,16]{0,2,1:T(8,128)(2,1)S(1)}, u32[]{:S(2)}, u32[]{:S(2)}) async-start(bf16[289,64,16]{0,2,1:T(8,128)(2,1)} %broadcast_select_fusion), calls=%async_computation.2 | async-start | bytes 1572864 | tf_op jit(solution)/shard_map/all_to_all | solution.py:104
  62.4 4.1 %copy-start.7 = (s32[8,64]{1,0:T(8,128)S(1)}, s32[8,64]{1,0:T(8,128)}, u32[]{:S(2)}) copy-start(s32[8,64]{1,0:T(8,128)} %param.17) | copy-start | bytes 6148
  73.5 3.3 %copy-start.8 = (s32[8,64]{1,0:T(8,128)S(1)}, s32[8,64]{1,0:T(8,128)}, u32[]{:S(2)}) copy-start(s32[8,64]{1,0:T(8,128)} %param.16) | copy-start | bytes 6148
  73.5 5.7 %copy-start.2 = (bf16[8,289,289]{2,0,1:T(8,128)(2,1)S(1)}, bf16[8,289,289]{2,0,1:T(8,128)(2,1)}, u32[]{:S(2)}) copy-start(bf16[8,289,289]{2,0,1:T(8,128)(2,1)} %gather_fusion) | copy-start | bytes 4009012
  81.5 4.6 %copy-start.1 = (bf16[2312,289]{0,1:T(8,128)(2,1)S(1)}, bf16[2312,289]{0,1:T(8,128)(2,1)}, u32[]{:S(2)}) copy-start(bf16[2312,289]{0,1:T(8,128)(2,1)} %reshape.143) | copy-start | bytes 4009012

commit v8 on v7

--- a/solution.py
+++ b/solution.py
@@ -29,7 +29,7 @@
     return spread.reshape(8, coefs, count).transpose(1, 2, 0).reshape(coefs, 8 * count)
 
 
-def far_kernel(idx_ref, buf_ref, fs_ref, out_ref, table_ref):
+def far_kernel(idx_ref, buf_ref, fs_ref, out_ref, table_ref, acc_ref):
     kinds = fs_ref.shape[0]
     rows = buf_ref.shape[0]
     for k in range(kinds):
@@ -38,7 +38,7 @@
                 buf_ref[...], fs_ref[k, :, pl.ds(j * LANE, LANE)], preferred_element_type=jnp.float32
             )
             table_ref[pl.ds(CHUNKS * k * rows + j, rows, stride=CHUNKS), :] = part
-    targets = out_ref.shape[0] // CHUNKS
+    targets = out_ref.shape[1]
     lists = idx_ref.shape[0] // targets
 
     def body(t, carry):
@@ -46,10 +46,12 @@
         acc = table_ref[pl.ds(idx_ref[base], CHUNKS), :]
         for l in range(1, lists):
             acc = acc + table_ref[pl.ds(idx_ref[base + l], CHUNKS), :]
-        out_ref[pl.ds(t * CHUNKS, CHUNKS), :] = acc
+        acc_ref[pl.ds(t * CHUNKS, CHUNKS), :] = acc
         return carry
 
     lax.fori_loop(0, targets, body, 0, unroll=8)
+    for j in range(CHUNKS):
+        out_ref[pl.ds(j * LANE, LANE), :] = acc_ref[pl.ds(j, targets, stride=CHUNKS), :].T
 
 
 def far_field(buffer, far_shift, leaf_src, leaf_kind):
@@ -62,16 +64,19 @@
     idx = (CHUNKS * (leaf_kind * rows + leaf_src)).T.reshape(lists * targets)
     out = pl.pallas_call(
         far_kernel,
-        out_shape=jax.ShapeDtypeStruct((targets * CHUNKS, LANE), jnp.float32),
+        out_shape=jax.ShapeDtypeStruct((width, targets), jnp.float32),
         in_specs=[
             pl.BlockSpec(memory_space=pltpu.SMEM),
             pl.BlockSpec(memory_space=pltpu.VMEM),
             pl.BlockSpec(memory_space=pltpu.VMEM),
         ],
         out_specs=pl.BlockSpec(memory_space=pltpu.VMEM),
-        scratch_shapes=[pltpu.VMEM((kinds * rows * CHUNKS, LANE), jnp.float32)],
+        scratch_shapes=[
+            pltpu.VMEM((kinds * rows * CHUNKS, LANE), jnp.float32),
+            pltpu.VMEM((targets * CHUNKS, LANE), jnp.float32),
+        ],
     )(idx, buf_t, fs_t)
-    return out.reshape(targets, width)[:, :coefs].T
+    return out[:coefs, :]
 
 
 def gather_columns(column_block, axes):

time: 119 us -> 118 us (level)
  local copies, waits for them, and re-layouts: 35.4 us -> 32.9 us
  waiting for transfers between devices: 23.1 us -> 24.9 us
  other arithmetic: 3.56 us -> 5.32 us
  matrix products: 9.27 us -> 7.79 us
    convert_element_type x1, other arithmetic: 0.08 us -> 1.87 us  [on_device(): return (chain_part + far_total).astype(jnp.bfloat16)]
    all_to_all x1, waiting for transfers between devices: 9.68 us -> 11.5 us  [on_device(): lax.all_to_all(outgoing, ('gy', 'gz'), split_axis=1, concat_axis=1, tiled...]
    dot_general x3, matrix products: 2.88 us -> 1.4 us  [lower_level(): jnp.dot(down_shift.reshape(8 * coefs, coefs), parent, preferred_element_t...]
    reshape x1 -> x0, local copies, waits for them, and re-layouts: 1.31 us -> none  [far_field(): return out.reshape(targets, width)[:, :coefs].T]
  transfers between devices with their start and end apart: 3 -> 3, of which waited for: 3 -> 3; matrix products, arithmetic and copies ran while one was open for 32% -> 31% of each run, Pallas kernels for 0% -> 0%
where the time goes in v8:
time: 118 us
  local copies, waits for them, and re-layouts  32.9 us (28%)
  starting transfers between devices  29.1 us (25%)
  waiting for transfers between devices  24.9 us (21%)
  Pallas kernels  17.7 us (15%)
  matrix products  7.79 us (7%)
  other arithmetic  5.32 us (5%)
    all_to_all x2, starting transfers between devices, gather_columns(): return lax.all_to_all(spread, axes, split_axis=1, concat_axis=1, tiled=True)  22.7 us
    pallas_call x1, Pallas kernels, far_field(): pl.pallas_call(far_kernel, out_shape=jax.ShapeDtypeStruct((width, targets...  17.7 us
    all_to_all x2, waiting for transfers between devices, gather_columns(): return lax.all_to_all(spread, axes, split_axis=1, concat_axis=1, tiled=True)  13.4 us
    all_to_all x1, waiting for transfers between devices, on_device(): lax.all_to_all(outgoing, ('gy', 'gz'), split_axis=1, concat_axis=1, tiled...  11.5 us
    unnamed x23, local copies, waits for them, and re-layouts  8.45 us
    gather x1, local copies, waits for them, and re-layouts, on_device(): jnp.take(far_shift, coarse_kinds, axis=0).transpose(1, 0, 2)  6.86 us
    all_to_all x1, starting transfers between devices, on_device(): lax.all_to_all(outgoing, ('gy', 'gz'), split_axis=1, concat_axis=1, tiled...  6.35 us
    dot_general x4, matrix products, lift_level(): lax.dot_general(up_shift, child_stack, (((2,), (1,)), ((0,), (0,))), pref...  3.99 us
  transfers between devices with their start and end apart: 3, of which 3 were waited for; matrix products, arithmetic and copies ran while one was open for 31% of the time, Pallas kernels for 0%

profile of v8, /device:TPU:8, one launch (start us, length us, event | category | flops | bytes accessed | tf_op | source)
XLA Modules:
  0.0 117.9 jit_solution(18251546904169792380)
XLA Ops:
  0.0 0.0 copy-start.3
  0.0 1.3 %copy.33 = bf16[289,512]{0,1:T(8,128)(2,1)S(1)} copy(bf16[289,512]{1,0:T(8,128)(2,1)} %param.9) | data formatting | bytes 591872 | tf_op args[0]
  1.3 2.2 %fusion.19 = bf16[289,8,8]{0,2,1:T(8,128)(2,1)S(1)} fusion(bf16[8,289,289]{2,0,1:T(8,128)(2,1)} %param.10, bf16[8,289,64]{1,0,2:T(8,128)(2,1)S(1)} %bitcast.95), kind=kOutput, calls=%fused_computation.22 | convolution fusion | flops 85544000 | bytes 1669264 | tf_op jit(solution)/shard_map/dot_general | solution.py:17
  3.5 0.0 copy-done.3
  3.5 0.0 copy-start.6
  3.6 0.6 fusion.28
  4.1 0.6 fusion.37
  4.8 0.6 reshape.138
  5.4 15.2 %all-to-all-start = ((bf16[289,16,1]{0,2,1:T(2,128)(2,1)}), bf16[289,16,1]{0,2,1:T(2,128)(2,1)S(1)}, u32[]{:S(2)}, u32[]{:S(2)}) async-start(bf16[289,16,1]{0,2,1:T(2,128)(2,1)} %reshape.138), calls=%async_computation | async-start | bytes 49152 | tf_op jit(solution)/shard_map/all_to_all | solution.py:87
  20.6 0.0 copy-done.6
  20.6 0.1 copy.43
  20.7 0.1 reshape.145
  20.8 3.9 %gather_fusion.2 = bf16[1024,289]{1,0:T(8,128)(2,1)S(1)} fusion(bf16[289,512]{0,1:T(8,128)(2,1)S(1)} %copy.33, s32[1024]{0:T(1024)S(1)} %broadcast_clamp_fusion), kind=kCustom, calls=%fused_computation.2 | custom fusion | bytes 1187840 | tf_op jit(solution)/shard_map/jit(_take)/gather | solution.py:108
  24.7 0.1 copy.42
  24.8 8.3 %all-to-all-done = bf16[289,16,1]{0,2,1:T(2,128)(2,1)S(1)} async-done(((bf16[289,16,1]{0,2,1:T(2,128)(2,1)}), bf16[289,16,1]{0,2,1:T(2,128)(2,1)S(1)}, u32[]{:S(2)}, u32[]{:S(2)}) %all-to-all-start) | async-done | bytes 9280 | tf_op jit(solution)/shard_map/all_to_all | solution.py:87
  33.2 0.6 fusion.43
  33.7 0.0 copy-start
  33.8 0.7 broadcast_in_dim.43
  34.4 7.5 %all-to-all-start.1 = ((bf16[289,32,2]{0,2,1:T(2,128)(2,1)}), bf16[289,32,2]{0,2,1:T(2,128)(2,1)S(1)}, u32[]{:S(2)}, u32[]{:S(2)}) async-start(bf16[289,32,2]{0,2,1:T(2,128)(2,1)} %broadcast_in_dim.43), calls=%async_computation.1 | async-start | bytes 98304 | tf_op jit(solution)/shard_map/all_to_all | solution.py:87
  42.0 1.1 broadcast_select_fusion
  43.0 5.1 %all-to-all-done.1 = bf16[289,32,2]{0,2,1:T(2,128)(2,1)S(1)} async-done(((bf16[289,32,2]{0,2,1:T(2,128)(2,1)}), bf16[289,32,2]{0,2,1:T(2,128)(2,1)S(1)}, u32[]{:S(2)}, u32[]{:S(2)}) %all-to-all-start.1) | async-done | bytes 37024 | tf_op jit(solution)/shard_map/all_to_all | solution.py:87
  48.1 6.3 %all-to-all-start.2 = ((bf16[289,64,16]{0,2,1:T(8,128)(2,1)}), bf16[289,64,16]{0,2,1:T(8,128)(2,1)S(1)}, u32[]{:S(2)}, u32[]{:S(2)}) async-start(bf16[289,64,16]{0,2,1:T(8,128)(2,1)} %broadcast_select_fusion), calls=%async_computation.2 | async-start | bytes 1572864 | tf_op jit(solution)/shard_map/all_to_all | solution.py:109
  54.5 0.0 copy-done
  54.5 0.0 copy-start.7
  54.6 2.8 %copy.46 = bf16[8,289,289]{1,2,0:T(8,128)(2,1)} copy(bf16[8,289,289]{2,0,1:T(8,128)(2,1)S(1)} %copy-done) | data formatting | bytes 2672672 | tf_op args[3]
  57.3 0.0 copy-done.7
  57.4 0.2 fusion.57
  57.5 6.9 %gather_fusion = bf16[8,289,289]{2,0,1:T(8,128)(2,1)} fusion(bf16[8,289,289]{2,0,1:T(8,128)(2,1)S(1)} %copy-done, s32[1024]{0:T(1024)S(1)} %pad_clamp_fusion.1), kind=kCustom, calls=%fused_computation | custom fusion | bytes 2672704 | tf_op jit(solution)/shard_map/jit(_take)/gather | solution.py:121
  64.4 4.2 %copy.40 = bf16[8,289,289]{1,0,2:T(8,128)(2,1)} copy(bf16[8,289,289]{2,0,1:T(8,128)(2,1)} %param.11) | data formatting | bytes 2672672 | tf_op args[2]
  68.6 0.0 copy-start.4
  68.6 0.0 copy-start.5
  68.6 3.4 %reshape.140 = bf16[2312,289]{0,1:T(8,128)(2,1)S(1)} reshape(bf16[8,289,289]{1,0,2:T(8,128)(2,1)} %copy.40) | data formatting | bytes 2672672 | tf_op jit(solution)/shard_map/reshape | solution.py:27
  72.1 0.0 copy-done.4
  72.1 0.0 copy-done.5
  72.1 0.1 copy.41
  72.2 0.8 reshape.143.idx_ref
  73.0 0.0 copy-start.8
  73.0 0.0 copy-start.2
  73.0 3.3 %pad.9.fs_ref = bf16[8,384,384]{2,1,0:T(8,128)(2,1)} pad(bf16[8,289,289]{2,1,0:T(8,128)(2,1)} %bitcast.96, bf16[]{:T(256)} %constant.91.clone.1), padding=0_0x0_95x0_95 | pad | bytes 3695634 | tf_op jit(solution)/shard_map/jit(_pad)/pad | solution.py:63
  76.3 0.0 copy-done.8
  76.3 0.2 fusion.58
  76.5 0.2 and_reduce_fusion
  76.7 1.9 %constant_dynamic-slice_fusion = bf16[1,289,289]{2,0,1:T(2,128)(2,1)S(1)} fusion(bf16[8,289,289]{2,0,1:T(8,128)(2,1)} %param.11, s32[]{:T(128)S(6)} %select_n.70), kind=kLoop, calls=%fused_computation.61 | loop fusion | bytes 334088 | tf_op jit(solution)/shard_map/dynamic_slice | solution.py:129
  78.7 0.0 copy-done.2
  78.7 1.5 %select_bitcast_fusion = bf16[289,8,289]{2,1,0:T(8,128)(2,1)} fusion(bf16[8,289,289]{2,0,1:T(8,128)(2,1)S(1)} %copy-done.2, pred[8]{0:T(512)(128)(4,1)S(1)} %get-tuple-element.6), kind=kLoop, calls=%fused_computation.10 | loop fusion | flops 668168 | bytes 2672680 | tf_op jit(solution)/shard_map/jit(_take)/select_n | solution.py:121
  80.3 0.6 gather_fusion.1
  80.8 0.0 copy-start.1
  80.9 0.1 select_bitcast_fusion.1
  80.9 2.2 %fusion.40 = bf16[289]{0:T(512)(128)(2,1)S(1)} fusion(bf16[289,8,289]{2,1,0:T(8,128)(2,1)} %select_bitcast_fusion, bf16[8,289,1]{1,0,2:T(8,128)(2,1)S(1)} %select_bitcast_fusion.1), kind=kOutput, calls=%fused_computation.29 | convolution fusion | flops 1336336 | bytes 1341538 | tf_op jit(solution)/shard_map/dot_general | solution.py:126
  83.1 0.2 convolution_reduce_fusion
  83.4 0.0 copy-done.1
  83.4 0.7 fusion.1
  84.1 0.3 fusion
  84.4 0.1 convert_element_type.75
  84.5 0.4 convolution_bitcast_fusion
  84.9 0.4 reshape.141
  85.4 0.2 copy.47
  85.6 11.5 %all-to-all-done.2 = bf16[289,64,16]{0,2,1:T(8,128)(2,1)S(1)} async-done(((bf16[289,64,16]{0,2,1:T(8,128)(2,1)}), bf16[289,64,16]{0,2,1:T(8,128)(2,1)S(1)}, u32[]{:S(2)}, u32[]{:S(2)}) %all-to-all-start.2) | async-done | bytes 591904 | tf_op jit(solution)/shard_map/all_to_all | solution.py:109
  97.1 0.1 maximum_bitcast_fusion
  97.2 1.2 pad.8.buf_ref
  98.4 17.7 %shard_map.91 = f32[384,512]{1,0:T(8,128)} custom-call(s32[8192]{0:T(1024)} %reshape.143.idx_ref, bf16[1536,384]{1,0:T(8,128)(2,1)} %pad.8.buf_ref, bf16[8,384,384]{2,1,0:T(8,128)(2,1)} %pad.9.fs_ref), custom_call_target="tpu_custom_call" | custom-call | tf_op jit(solution)/shard_map/pallas_call | solution.py:65
  116.0 1.9 %fusion.46 = bf16[289,512]{1,0:T(8,128)(2,1)} fusion(f32[289,512]{1,0:T(8,128)S(1)} %copy.47, f32[384,512]{1,0:T(8,128)} %shard_map.91), kind=kLoop, calls=%fused_computation.34 | loop fusion | flops 295936 | bytes 1479680 | tf_op jit(solution)/shard_map/convert_element_type | solution.py:137
  (10 shorter events, 0.1 us)
Async XLA Ops:
  0.0 3.5 %copy-start.3 = (bf16[8,289,289]{2,0,1:T(8,128)(2,1)S(1)}, bf16[8,289,289]{2,0,1:T(8,128)(2,1)}, u32[]{:S(2)}) copy-start(bf16[8,289,289]{2,0,1:T(8,128)(2,1)} %param.10) | copy-start | bytes 4009012
  3.5 17.0 %copy-start.6 = (s32[1,1,64,16]{2,3,1,0:T(8,128)S(1)}, s32[1,1,64,16]{2,3,1,0:T(8,128)}, u32[]{:S(2)}) copy-start(s32[1,1,64,16]{2,3,1,0:T(8,128)} %param.13) | copy-start | bytes 12292
  5.4 27.8 %all-to-all-start = ((bf16[289,16,1]{0,2,1:T(2,128)(2,1)}), bf16[289,16,1]{0,2,1:T(2,128)(2,1)S(1)}, u32[]{:S(2)}, u32[]{:S(2)}) async-start(bf16[289,16,1]{0,2,1:T(2,128)(2,1)} %reshape.138), calls=%async_computation | async-start | bytes 49152 | tf_op jit(solution)/shard_map/all_to_all | solution.py:87
  33.7 20.8 %copy-start = (bf16[8,289,289]{2,0,1:T(8,128)(2,1)S(1)}, bf16[8,289,289]{2,0,1:T(8,128)(2,1)}, u32[]{:S(2)}) copy-start(bf16[8,289,289]{2,0,1:T(8,128)(2,1)} %param.12) | copy-start | bytes 4009012
  34.4 13.7 %all-to-all-start.1 = ((bf16[289,32,2]{0,2,1:T(2,128)(2,1)}), bf16[289,32,2]{0,2,1:T(2,128)(2,1)S(1)}, u32[]{:S(2)}, u32[]{:S(2)}) async-start(bf16[289,32,2]{0,2,1:T(2,128)(2,1)} %broadcast_in_dim.43), calls=%async_computation.1 | async-start | bytes 98304 | tf_op jit(solution)/shard_map/all_to_all | solution.py:87
  48.1 48.9 %all-to-all-start.2 = ((bf16[289,64,16]{0,2,1:T(8,128)(2,1)}), bf16[289,64,16]{0,2,1:T(8,128)(2,1)S(1)}, u32[]{:S(2)}, u32[]{:S(2)}) async-start(bf16[289,64,16]{0,2,1:T(8,128)(2,1)} %broadcast_select_fusion), calls=%async_computation.2 | async-start | bytes 1572864 | tf_op jit(solution)/shard_map/all_to_all | solution.py:109
  54.5 2.8 %copy-start.7 = (s32[8,64]{1,0:T(8,128)S(1)}, s32[8,64]{1,0:T(8,128)}, u32[]{:S(2)}) copy-start(s32[8,64]{1,0:T(8,128)} %param.17) | copy-start | bytes 6148
  68.6 3.4 %copy-start.4 = (s32[16,512]{1,0:T(8,128)S(1)}, s32[16,512]{1,0:T(8,128)}, u32[]{:S(2)}) copy-start(s32[16,512]{1,0:T(8,128)} %param.14) | copy-start | bytes 98308
  68.6 3.5 %copy-start.5 = (s32[16,512]{1,0:T(8,128)S(1)}, s32[16,512]{1,0:T(8,128)}, u32[]{:S(2)}) copy-start(s32[16,512]{1,0:T(8,128)} %param.15) | copy-start | bytes 98308
  73.0 3.3 %copy-start.8 = (s32[8,64]{1,0:T(8,128)S(1)}, s32[8,64]{1,0:T(8,128)}, u32[]{:S(2)}) copy-start(s32[8,64]{1,0:T(8,128)} %param.16) | copy-start | bytes 6148
  73.0 5.7 %copy-start.2 = (bf16[8,289,289]{2,0,1:T(8,128)(2,1)S(1)}, bf16[8,289,289]{2,0,1:T(8,128)(2,1)}, u32[]{:S(2)}) copy-start(bf16[8,289,289]{2,0,1:T(8,128)(2,1)} %gather_fusion) | copy-start | bytes 4009012
  80.8 2.5 %copy-start.1 = (bf16[8,289,289]{2,0,1:T(8,128)(2,1)S(1)}, bf16[8,289,289]{2,0,1:T(8,128)(2,1)}, u32[]{:S(2)}) copy-start(bf16[8,289,289]{2,0,1:T(8,128)(2,1)} %param.11) | copy-start | bytes 4009012

commit v9 on v8

--- a/solution.py
+++ b/solution.py
@@ -33,11 +33,11 @@
     kinds = fs_ref.shape[0]
     rows = buf_ref.shape[0]
     for k in range(kinds):
+        whole = jnp.dot(buf_ref[...], fs_ref[k], preferred_element_type=jnp.float32)
         for j in range(CHUNKS):
-            part = jnp.dot(
-                buf_ref[...], fs_ref[k, :, pl.ds(j * LANE, LANE)], preferred_element_type=jnp.float32
-            )
-            table_ref[pl.ds(CHUNKS * k * rows + j, rows, stride=CHUNKS), :] = part
+            table_ref[pl.ds(CHUNKS * k * rows + j, rows, stride=CHUNKS), :] = whole[
+                :, j * LANE : (j + 1) * LANE
+            ]
     targets = out_ref.shape[1]
     lists = idx_ref.shape[0] // targets
 

time: 118 us -> 117 us (level)
  Pallas kernels: 17.7 us -> 16 us
    pallas_call x1, Pallas kernels: 17.7 us -> 16 us  [far_field(): pl.pallas_call(far_kernel, out_shape=jax.ShapeDtypeStruct((width, targets...]
where the time goes in v9:
time: 117 us; the launch traced here: 116 us
  local copies, waits for them, and re-layouts  32.9 us (28%)
  starting transfers between devices  29.1 us (25%)
  waiting for transfers between devices  24.9 us (21%)
  Pallas kernels  16 us (14%)
  matrix products  7.79 us (7%)
  other arithmetic  5.32 us (5%)
    all_to_all x2, starting transfers between devices, gather_columns(): return lax.all_to_all(spread, axes, split_axis=1, concat_axis=1, tiled=True)  22.7 us
    pallas_call x1, Pallas kernels, far_field(): pl.pallas_call(far_kernel, out_shape=jax.ShapeDtypeStruct((width, targets...  16 us
    all_to_all x2, waiting for transfers between devices, gather_columns(): return lax.all_to_all(spread, axes, split_axis=1, concat_axis=1, tiled=True)  13.4 us
    all_to_all x1, waiting for transfers between devices, on_device(): lax.all_to_all(outgoing, ('gy', 'gz'), split_axis=1, concat_axis=1, tiled...  11.5 us
    unnamed x23, local copies, waits for them, and re-layouts  8.45 us
    gather x1, local copies, waits for them, and re-layouts, on_device(): jnp.take(far_shift, coarse_kinds, axis=0).transpose(1, 0, 2)  6.86 us
    all_to_all x1, starting transfers between devices, on_device(): lax.all_to_all(outgoing, ('gy', 'gz'), split_axis=1, concat_axis=1, tiled...  6.35 us
    dot_general x4, matrix products, lift_level(): lax.dot_general(up_shift, child_stack, (((2,), (1,)), ((0,), (0,))), pref...  3.99 us
  transfers between devices with their start and end apart: 3, of which 3 were waited for; matrix products, arithmetic and copies ran while one was open for 31% of the time, Pallas kernels for 0%

profile of v9, /device:TPU:8, one launch (start us, length us, event | category | flops | bytes accessed | tf_op | source)
XLA Modules:
  0.0 116.2 jit_solution(2207937633122123362)
XLA Ops:
  0.0 0.0 copy-start.3
  0.0 1.3 %copy.33 = bf16[289,512]{0,1:T(8,128)(2,1)S(1)} copy(bf16[289,512]{1,0:T(8,128)(2,1)} %param.9) | data formatting | bytes 591872 | tf_op args[0]
  1.3 2.2 %fusion.19 = bf16[289,8,8]{0,2,1:T(8,128)(2,1)S(1)} fusion(bf16[8,289,289]{2,0,1:T(8,128)(2,1)} %param.10, bf16[8,289,64]{1,0,2:T(8,128)(2,1)S(1)} %bitcast.95), kind=kOutput, calls=%fused_computation.22 | convolution fusion | flops 85544000 | bytes 1669264 | tf_op jit(solution)/shard_map/dot_general | solution.py:17
  3.5 0.0 copy-done.3
  3.5 0.0 copy-start.6
  3.6 0.6 fusion.28
  4.1 0.6 fusion.37
  4.8 0.6 reshape.138
  5.4 15.2 %all-to-all-start = ((bf16[289,16,1]{0,2,1:T(2,128)(2,1)}), bf16[289,16,1]{0,2,1:T(2,128)(2,1)S(1)}, u32[]{:S(2)}, u32[]{:S(2)}) async-start(bf16[289,16,1]{0,2,1:T(2,128)(2,1)} %reshape.138), calls=%async_computation | async-start | bytes 49152 | tf_op jit(solution)/shard_map/all_to_all | solution.py:87
  20.6 0.0 copy-done.6
  20.6 0.1 copy.43
  20.7 0.1 reshape.145
  20.8 3.9 %gather_fusion.2 = bf16[1024,289]{1,0:T(8,128)(2,1)S(1)} fusion(bf16[289,512]{0,1:T(8,128)(2,1)S(1)} %copy.33, s32[1024]{0:T(1024)S(1)} %broadcast_clamp_fusion), kind=kCustom, calls=%fused_computation.2 | custom fusion | bytes 1187840 | tf_op jit(solution)/shard_map/jit(_take)/gather | solution.py:108
  24.7 0.1 copy.42
  24.8 8.3 %all-to-all-done = bf16[289,16,1]{0,2,1:T(2,128)(2,1)S(1)} async-done(((bf16[289,16,1]{0,2,1:T(2,128)(2,1)}), bf16[289,16,1]{0,2,1:T(2,128)(2,1)S(1)}, u32[]{:S(2)}, u32[]{:S(2)}) %all-to-all-start) | async-done | bytes 9280 | tf_op jit(solution)/shard_map/all_to_all | solution.py:87
  33.2 0.6 fusion.43
  33.7 0.0 copy-start
  33.8 0.7 broadcast_in_dim.43
  34.4 7.5 %all-to-all-start.1 = ((bf16[289,32,2]{0,2,1:T(2,128)(2,1)}), bf16[289,32,2]{0,2,1:T(2,128)(2,1)S(1)}, u32[]{:S(2)}, u32[]{:S(2)}) async-start(bf16[289,32,2]{0,2,1:T(2,128)(2,1)} %broadcast_in_dim.43), calls=%async_computation.1 | async-start | bytes 98304 | tf_op jit(solution)/shard_map/all_to_all | solution.py:87
  42.0 1.1 broadcast_select_fusion
  43.0 5.1 %all-to-all-done.1 = bf16[289,32,2]{0,2,1:T(2,128)(2,1)S(1)} async-done(((bf16[289,32,2]{0,2,1:T(2,128)(2,1)}), bf16[289,32,2]{0,2,1:T(2,128)(2,1)S(1)}, u32[]{:S(2)}, u32[]{:S(2)}) %all-to-all-start.1) | async-done | bytes 37024 | tf_op jit(solution)/shard_map/all_to_all | solution.py:87
  48.1 6.3 %all-to-all-start.2 = ((bf16[289,64,16]{0,2,1:T(8,128)(2,1)}), bf16[289,64,16]{0,2,1:T(8,128)(2,1)S(1)}, u32[]{:S(2)}, u32[]{:S(2)}) async-start(bf16[289,64,16]{0,2,1:T(8,128)(2,1)} %broadcast_select_fusion), calls=%async_computation.2 | async-start | bytes 1572864 | tf_op jit(solution)/shard_map/all_to_all | solution.py:109
  54.5 0.0 copy-done
  54.5 0.0 copy-start.7
  54.6 2.8 %copy.46 = bf16[8,289,289]{1,2,0:T(8,128)(2,1)} copy(bf16[8,289,289]{2,0,1:T(8,128)(2,1)S(1)} %copy-done) | data formatting | bytes 2672672 | tf_op args[3]
  57.3 0.0 copy-done.7
  57.4 0.2 fusion.57
  57.5 6.9 %gather_fusion = bf16[8,289,289]{2,0,1:T(8,128)(2,1)} fusion(bf16[8,289,289]{2,0,1:T(8,128)(2,1)S(1)} %copy-done, s32[1024]{0:T(1024)S(1)} %pad_clamp_fusion.1), kind=kCustom, calls=%fused_computation | custom fusion | bytes 2672704 | tf_op jit(solution)/shard_map/jit(_take)/gather | solution.py:121
  64.4 4.2 %copy.40 = bf16[8,289,289]{1,0,2:T(8,128)(2,1)} copy(bf16[8,289,289]{2,0,1:T(8,128)(2,1)} %param.11) | data formatting | bytes 2672672 | tf_op args[2]
  68.6 0.0 copy-start.4
  68.6 0.0 copy-start.5
  68.6 3.4 %reshape.140 = bf16[2312,289]{0,1:T(8,128)(2,1)S(1)} reshape(bf16[8,289,289]{1,0,2:T(8,128)(2,1)} %copy.40) | data formatting | bytes 2672672 | tf_op jit(solution)/shard_map/reshape | solution.py:27
  72.1 0.0 copy-done.4
  72.1 0.0 copy-done.5
  72.1 0.1 copy.41
  72.2 0.8 reshape.143.idx_ref
  73.0 0.0 copy-start.8
  73.0 0.0 copy-start.2
  73.0 3.3 %pad.9.fs_ref = bf16[8,384,384]{2,1,0:T(8,128)(2,1)} pad(bf16[8,289,289]{2,1,0:T(8,128)(2,1)} %bitcast.96, bf16[]{:T(256)} %constant.91.clone.1), padding=0_0x0_95x0_95 | pad | bytes 3695634 | tf_op jit(solution)/shard_map/jit(_pad)/pad | solution.py:63
  76.3 0.0 copy-done.8
  76.3 0.2 fusion.58
  76.5 0.2 and_reduce_fusion
  76.7 1.9 %constant_dynamic-slice_fusion = bf16[1,289,289]{2,0,1:T(2,128)(2,1)S(1)} fusion(bf16[8,289,289]{2,0,1:T(8,128)(2,1)} %param.11, s32[]{:T(128)S(6)} %select_n.70), kind=kLoop, calls=%fused_computation.61 | loop fusion | bytes 334088 | tf_op jit(solution)/shard_map/dynamic_slice | solution.py:129
  78.7 0.0 copy-done.2
  78.7 1.5 %select_bitcast_fusion = bf16[289,8,289]{2,1,0:T(8,128)(2,1)} fusion(bf16[8,289,289]{2,0,1:T(8,128)(2,1)S(1)} %copy-done.2, pred[8]{0:T(512)(128)(4,1)S(1)} %get-tuple-element.6), kind=kLoop, calls=%fused_computation.10 | loop fusion | flops 668168 | bytes 2672680 | tf_op jit(solution)/shard_map/jit(_take)/select_n | solution.py:121
  80.3 0.6 gather_fusion.1
  80.8 0.0 copy-start.1
  80.9 0.1 select_bitcast_fusion.1
  80.9 2.2 %fusion.40 = bf16[289]{0:T(512)(128)(2,1)S(1)} fusion(bf16[289,8,289]{2,1,0:T(8,128)(2,1)} %select_bitcast_fusion, bf16[8,289,1]{1,0,2:T(8,128)(2,1)S(1)} %select_bitcast_fusion.1), kind=kOutput, calls=%fused_computation.29 | convolution fusion | flops 1336336 | bytes 1341538 | tf_op jit(solution)/shard_map/dot_general | solution.py:126
  83.1 0.2 convolution_reduce_fusion
  83.4 0.0 copy-done.1
  83.4 0.7 fusion.1
  84.1 0.3 fusion
  84.4 0.1 convert_element_type.75
  84.5 0.4 convolution_bitcast_fusion
  84.9 0.4 reshape.141
  85.4 0.2 copy.47
  85.6 11.5 %all-to-all-done.2 = bf16[289,64,16]{0,2,1:T(8,128)(2,1)S(1)} async-done(((bf16[289,64,16]{0,2,1:T(8,128)(2,1)}), bf16[289,64,16]{0,2,1:T(8,128)(2,1)S(1)}, u32[]{:S(2)}, u32[]{:S(2)}) %all-to-all-start.2) | async-done | bytes 591904 | tf_op jit(solution)/shard_map/all_to_all | solution.py:109
  97.1 0.1 maximum_bitcast_fusion
  97.2 1.2 pad.8.buf_ref
  98.4 16.0 %shard_map.91 = f32[384,512]{1,0:T(8,128)} custom-call(s32[8192]{0:T(1024)} %reshape.143.idx_ref, bf16[1536,384]{1,0:T(8,128)(2,1)} %pad.8.buf_ref, bf16[8,384,384]{2,1,0:T(8,128)(2,1)} %pad.9.fs_ref), custom_call_target="tpu_custom_call" | custom-call | tf_op jit(solution)/shard_map/pallas_call | solution.py:65
  114.4 1.9 %fusion.46 = bf16[289,512]{1,0:T(8,128)(2,1)} fusion(f32[289,512]{1,0:T(8,128)S(1)} %copy.47, f32[384,512]{1,0:T(8,128)} %shard_map.91), kind=kLoop, calls=%fused_computation.34 | loop fusion | flops 295936 | bytes 1479680 | tf_op jit(solution)/shard_map/convert_element_type | solution.py:137
  (10 shorter events, 0.1 us)
Async XLA Ops:
  0.0 3.5 %copy-start.3 = (bf16[8,289,289]{2,0,1:T(8,128)(2,1)S(1)}, bf16[8,289,289]{2,0,1:T(8,128)(2,1)}, u32[]{:S(2)}) copy-start(bf16[8,289,289]{2,0,1:T(8,128)(2,1)} %param.10) | copy-start | bytes 4009012
  3.5 17.0 %copy-start.6 = (s32[1,1,64,16]{2,3,1,0:T(8,128)S(1)}, s32[1,1,64,16]{2,3,1,0:T(8,128)}, u32[]{:S(2)}) copy-start(s32[1,1,64,16]{2,3,1,0:T(8,128)} %param.13) | copy-start | bytes 12292
  5.4 27.8 %all-to-all-start = ((bf16[289,16,1]{0,2,1:T(2,128)(2,1)}), bf16[289,16,1]{0,2,1:T(2,128)(2,1)S(1)}, u32[]{:S(2)}, u32[]{:S(2)}) async-start(bf16[289,16,1]{0,2,1:T(2,128)(2,1)} %reshape.138), calls=%async_computation | async-start | bytes 49152 | tf_op jit(solution)/shard_map/all_to_all | solution.py:87
  33.7 20.8 %copy-start = (bf16[8,289,289]{2,0,1:T(8,128)(2,1)S(1)}, bf16[8,289,289]{2,0,1:T(8,128)(2,1)}, u32[]{:S(2)}) copy-start(bf16[8,289,289]{2,0,1:T(8,128)(2,1)} %param.12) | copy-start | bytes 4009012
  34.4 13.7 %all-to-all-start.1 = ((bf16[289,32,2]{0,2,1:T(2,128)(2,1)}), bf16[289,32,2]{0,2,1:T(2,128)(2,1)S(1)}, u32[]{:S(2)}, u32[]{:S(2)}) async-start(bf16[289,32,2]{0,2,1:T(2,128)(2,1)} %broadcast_in_dim.43), calls=%async_computation.1 | async-start | bytes 98304 | tf_op jit(solution)/shard_map/all_to_all | solution.py:87
  48.1 48.9 %all-to-all-start.2 = ((bf16[289,64,16]{0,2,1:T(8,128)(2,1)}), bf16[289,64,16]{0,2,1:T(8,128)(2,1)S(1)}, u32[]{:S(2)}, u32[]{:S(2)}) async-start(bf16[289,64,16]{0,2,1:T(8,128)(2,1)} %broadcast_select_fusion), calls=%async_computation.2 | async-start | bytes 1572864 | tf_op jit(solution)/shard_map/all_to_all | solution.py:109
  54.5 2.8 %copy-start.7 = (s32[8,64]{1,0:T(8,128)S(1)}, s32[8,64]{1,0:T(8,128)}, u32[]{:S(2)}) copy-start(s32[8,64]{1,0:T(8,128)} %param.17) | copy-start | bytes 6148
  68.6 3.4 %copy-start.4 = (s32[16,512]{1,0:T(8,128)S(1)}, s32[16,512]{1,0:T(8,128)}, u32[]{:S(2)}) copy-start(s32[16,512]{1,0:T(8,128)} %param.14) | copy-start | bytes 98308
  68.6 3.5 %copy-start.5 = (s32[16,512]{1,0:T(8,128)S(1)}, s32[16,512]{1,0:T(8,128)}, u32[]{:S(2)}) copy-start(s32[16,512]{1,0:T(8,128)} %param.15) | copy-start | bytes 98308
  73.0 3.3 %copy-start.8 = (s32[8,64]{1,0:T(8,128)S(1)}, s32[8,64]{1,0:T(8,128)}, u32[]{:S(2)}) copy-start(s32[8,64]{1,0:T(8,128)} %param.16) | copy-start | bytes 6148
  73.0 5.7 %copy-start.2 = (bf16[8,289,289]{2,0,1:T(8,128)(2,1)S(1)}, bf16[8,289,289]{2,0,1:T(8,128)(2,1)}, u32[]{:S(2)}) copy-start(bf16[8,289,289]{2,0,1:T(8,128)(2,1)} %gather_fusion) | copy-start | bytes 4009012
  80.8 2.5 %copy-start.1 = (bf16[8,289,289]{2,0,1:T(8,128)(2,1)S(1)}, bf16[8,289,289]{2,0,1:T(8,128)(2,1)}, u32[]{:S(2)}) copy-start(bf16[8,289,289]{2,0,1:T(8,128)(2,1)} %param.11) | copy-start | bytes 4009012

commit v10 on v9

--- a/solution.py
+++ b/solution.py
@@ -29,15 +29,17 @@
     return spread.reshape(8, coefs, count).transpose(1, 2, 0).reshape(coefs, 8 * count)
 
 
-def far_kernel(idx_ref, buf_ref, fs_ref, out_ref, table_ref, acc_ref):
+def far_kernel(idx_ref, own_ref, arr_ref, fs_ref, out_ref, table_ref, acc_ref):
     kinds = fs_ref.shape[0]
-    rows = buf_ref.shape[0]
+    own = own_ref.shape[0]
+    rows = own + arr_ref.shape[0]
     for k in range(kinds):
-        whole = jnp.dot(buf_ref[...], fs_ref[k], preferred_element_type=jnp.float32)
-        for j in range(CHUNKS):
-            table_ref[pl.ds(CHUNKS * k * rows + j, rows, stride=CHUNKS), :] = whole[
-                :, j * LANE : (j + 1) * LANE
-            ]
+        for src_ref, first in ((own_ref, 0), (arr_ref, own)):
+            whole = jnp.dot(src_ref[...], fs_ref[k], preferred_element_type=jnp.float32)
+            for j in range(CHUNKS):
+                table_ref[
+                    pl.ds(CHUNKS * (k * rows + first) + j, src_ref.shape[0], stride=CHUNKS), :
+                ] = whole[:, j * LANE : (j + 1) * LANE]
     targets = out_ref.shape[1]
     lists = idx_ref.shape[0] // targets
 
@@ -54,28 +56,25 @@
         out_ref[pl.ds(j * LANE, LANE), :] = acc_ref[pl.ds(j, targets, stride=CHUNKS), :].T
 
 
-def far_field(buffer, far_shift, leaf_src, leaf_kind):
-    coefs, rows = buffer.shape
+def far_field(own_rows, arrived_rows, far_shift, leaf_src, leaf_kind):
+    rows = own_rows.shape[0] + arrived_rows.shape[0]
+    coefs = own_rows.shape[1]
     kinds = far_shift.shape[0]
     lists, targets = leaf_src.shape
     width = CHUNKS * LANE
-    buf_t = jnp.pad(buffer.T, ((0, 0), (0, width - coefs)))
-    fs_t = jnp.pad(far_shift.transpose(0, 2, 1), ((0, 0), (0, width - coefs), (0, width - coefs)))
+    fs_t = jnp.pad(far_shift.transpose(0, 2, 1), ((0, 0), (0, 0), (0, width - coefs)))
     idx = (CHUNKS * (leaf_kind * rows + leaf_src)).T.reshape(lists * targets)
+    vmem = pl.BlockSpec(memory_space=pltpu.VMEM)
     out = pl.pallas_call(
         far_kernel,
         out_shape=jax.ShapeDtypeStruct((width, targets), jnp.float32),
-        in_specs=[
-            pl.BlockSpec(memory_space=pltpu.SMEM),
-            pl.BlockSpec(memory_space=pltpu.VMEM),
-            pl.BlockSpec(memory_space=pltpu.VMEM),
-        ],
-        out_specs=pl.BlockSpec(memory_space=pltpu.VMEM),
+        in_specs=[pl.BlockSpec(memory_space=pltpu.SMEM), vmem, vmem, vmem],
+        out_specs=vmem,
         scratch_shapes=[
             pltpu.VMEM((kinds * rows * CHUNKS, LANE), jnp.float32),
             pltpu.VMEM((targets * CHUNKS, LANE), jnp.float32),
         ],
-    )(idx, buf_t, fs_t)
+    )(idx, own_rows, arrived_rows, fs_t)
     return out[:coefs, :]
 
 
@@ -105,8 +104,9 @@
     peer_count = lax.axis_size(("gy", "gz"))
     slot_count = send_list.shape[3]
     send_order = send_list.reshape(peer_count * slot_count)
-    outgoing = jnp.take(multipoles, send_order, axis=1)
-    arrived = lax.all_to_all(outgoing, ("gy", "gz"), split_axis=1, concat_axis=1, tiled=True)
+    own_rows = multipoles.T
+    outgoing = jnp.take(own_rows, send_order, axis=0)
+    arrived_rows = lax.all_to_all(outgoing, ("gy", "gz"), split_axis=0, concat_axis=0, tiled=True)
     upward = multipoles
     for level in range(LOCAL_LEVELS):
         upward = lift_level(upward, up_shift).astype(jnp.bfloat16)
@@ -132,8 +132,7 @@
     for level in range(LOCAL_LEVELS - 1):
         downward = lower_level(downward, down_shift).astype(jnp.bfloat16)
     chain_part = lower_level(downward, down_shift)
-    buffer = jnp.concatenate([multipoles, arrived], axis=1)
-    far_total = far_field(buffer, far_shift, leaf_src, leaf_kind)
+    far_total = far_field(own_rows, arrived_rows, far_shift, leaf_src, leaf_kind)
     return (chain_part + far_total).astype(jnp.bfloat16)
 
 

time: 117 us -> 118 us (level)
  local copies, waits for them, and re-layouts: 32.9 us -> 29.9 us
  waiting for transfers between devices: 24.9 us -> 26.8 us
  matrix products: 7.79 us -> 9.35 us
    all_to_all x1, waiting for transfers between devices: 11.5 us -> 13.4 us  [on_device(): lax.all_to_all(outgoing, ('gy', 'gz'), split_axis=0, concat_axis=0, tiled...]
    dot_general x4, matrix products: 3.99 us -> 5.61 us  [lift_level(): lax.dot_general(up_shift, child_stack, (((2,), (1,)), ((0,), (0,))), pref...]
    pad x2 -> x1, local copies, waits for them, and re-layouts: 4.47 us -> 3.04 us  [far_field(): jnp.pad(far_shift.transpose(0, 2, 1), ((0, 0), (0, 0), (0, width - coefs)))]
    unnamed x23 -> x33, local copies, waits for them, and re-layouts: 8.45 us -> 7.38 us
  transfers between devices with their start and end apart: 3 -> 3, of which waited for: 3 -> 3; matrix products, arithmetic and copies ran while one was open for 31% -> 30% of each run, Pallas kernels for 0% -> 0%
where the time goes in v10:
time: 118 us; the launch traced here: 117 us
  local copies, waits for them, and re-layouts  29.9 us (25%)
  starting transfers between devices  29.3 us (25%)
  waiting for transfers between devices  26.8 us (23%)
  Pallas kernels  15.9 us (13%)
  matrix products  9.35 us (8%)
  other arithmetic  5.87 us (5%)
    all_to_all x2, starting transfers between devices, gather_columns(): return lax.all_to_all(spread, axes, split_axis=1, concat_axis=1, tiled=True)  22.7 us
    pallas_call x1, Pallas kernels, far_field(): pl.pallas_call(far_kernel, out_shape=jax.ShapeDtypeStruct((width, targets...  15.9 us
    all_to_all x2, waiting for transfers between devices, gather_columns(): return lax.all_to_all(spread, axes, split_axis=1, concat_axis=1, tiled=True)  13.4 us
    all_to_all x1, waiting for transfers between devices, on_device(): lax.all_to_all(outgoing, ('gy', 'gz'), split_axis=0, concat_axis=0, tiled...  13.4 us
    unnamed x33, local copies, waits for them, and re-layouts  7.38 us
    gather x1, local copies, waits for them, and re-layouts, on_device(): jnp.take(far_shift, coarse_kinds, axis=0).transpose(1, 0, 2)  7.09 us
    all_to_all x1, starting transfers between devices, on_device(): lax.all_to_all(outgoing, ('gy', 'gz'), split_axis=0, concat_axis=0, tiled...  6.53 us
    dot_general x4, matrix products, lift_level(): lax.dot_general(up_shift, child_stack, (((2,), (1,)), ((0,), (0,))), pref...  5.61 us
  transfers between devices with their start and end apart: 3, of which 3 were waited for; matrix products, arithmetic and copies ran while one was open for 30% of the time, Pallas kernels for 0%

profile of v10, /device:TPU:8, one launch (start us, length us, event | category | flops | bytes accessed | tf_op | source)
XLA Modules:
  0.0 117.2 jit_solution(595366927203493972)
XLA Ops:
  0.0 0.0 copy-start.4
  0.0 1.3 %copy.31 = bf16[289,512]{0,1:T(8,128)(2,1)S(1)} copy(bf16[289,512]{1,0:T(8,128)(2,1)} %param.9) | data formatting | bytes 591872 | tf_op args[0]
  1.3 0.0 copy-start.1
  1.3 2.4 %fusion.19 = bf16[289,8,8]{0,2,1:T(8,128)(2,1)S(1)} fusion(bf16[8,289,289]{2,0,1:T(8,128)(2,1)} %param.10, bf16[8,289,64]{1,0,2:T(8,128)(2,1)S(1)} %bitcast.92), kind=kOutput, calls=%fused_computation.21 | convolution fusion | flops 85544000 | bytes 1669264 | tf_op jit(solution)/shard_map/dot_general | solution.py:17
  3.7 0.0 copy-done.4
  3.7 0.0 copy-start.10
  3.7 0.6 fusion.28
  4.3 0.6 fusion.37
  4.9 0.6 reshape.138
  5.5 15.2 %all-to-all-start = ((bf16[289,16,1]{0,2,1:T(2,128)(2,1)}), bf16[289,16,1]{0,2,1:T(2,128)(2,1)S(1)}, u32[]{:S(2)}, u32[]{:S(2)}) async-start(bf16[289,16,1]{0,2,1:T(2,128)(2,1)} %reshape.138), calls=%async_computation | async-start | bytes 49152 | tf_op jit(solution)/shard_map/all_to_all | solution.py:86
  20.7 0.0 copy-done.10
  20.7 0.1 copy.42
  20.8 0.1 reshape.145
  21.0 0.1 copy.41
  21.1 0.0 copy-done.1
  21.1 3.9 %gather_fusion.2 = bf16[1024,289]{1,0:T(8,128)(2,1)S(1)} fusion(bf16[512,289]{1,0:T(8,128)(2,1)S(1)} %bitcast.93, s32[1024]{0:T(1024)S(1)} %broadcast_clamp_fusion), kind=kCustom, calls=%fused_computation.2 | custom fusion | bytes 1187840 | tf_op jit(solution)/shard_map/jit(_take)/gather | solution.py:108
  25.0 8.3 %all-to-all-done = bf16[289,16,1]{0,2,1:T(2,128)(2,1)S(1)} async-done(((bf16[289,16,1]{0,2,1:T(2,128)(2,1)}), bf16[289,16,1]{0,2,1:T(2,128)(2,1)S(1)}, u32[]{:S(2)}, u32[]{:S(2)}) %all-to-all-start) | async-done | bytes 9280 | tf_op jit(solution)/shard_map/all_to_all | solution.py:86
  33.3 2.1 %fusion.43 = bf16[289,2]{0,1:T(2,128)(2,1)S(1)} fusion(bf16[8,289,289]{2,0,1:T(8,128)(2,1)} %param.10, bf16[289,2,8]{0,2,1:T(8,128)(2,1)S(1)} %bitcast.99), kind=kOutput, calls=%fused_computation.30 | convolution fusion | flops 2673250 | bytes 1346740 | tf_op jit(solution)/shard_map/dot_general | solution.py:17
  35.4 0.0 copy-start
  35.4 0.7 broadcast_in_dim.43
  36.0 7.5 %all-to-all-start.1 = ((bf16[289,32,2]{0,2,1:T(2,128)(2,1)}), bf16[289,32,2]{0,2,1:T(2,128)(2,1)S(1)}, u32[]{:S(2)}, u32[]{:S(2)}) async-start(bf16[289,32,2]{0,2,1:T(2,128)(2,1)} %broadcast_in_dim.43), calls=%async_computation.1 | async-start | bytes 98304 | tf_op jit(solution)/shard_map/all_to_all | solution.py:86
  43.6 1.1 broadcast_select_fusion
  44.7 5.1 %all-to-all-done.1 = bf16[289,32,2]{0,2,1:T(2,128)(2,1)S(1)} async-done(((bf16[289,32,2]{0,2,1:T(2,128)(2,1)}), bf16[289,32,2]{0,2,1:T(2,128)(2,1)S(1)}, u32[]{:S(2)}, u32[]{:S(2)}) %all-to-all-start.1) | async-done | bytes 37024 | tf_op jit(solution)/shard_map/all_to_all | solution.py:86
  49.8 0.0 copy-start.6
  49.8 6.5 %all-to-all-start.2 = ((bf16[64,16,289]{2,1,0:T(8,128)(2,1)}), bf16[64,16,289]{2,1,0:T(8,128)(2,1)}, u32[]{:S(2)}, u32[]{:S(2)}) async-start(bf16[64,16,289]{2,1,0:T(8,128)(2,1)} %broadcast_select_fusion), calls=%async_computation.2 | async-start | bytes 1572864 | tf_op jit(solution)/shard_map/all_to_all | solution.py:109
  56.3 0.0 copy-done
  56.3 0.0 copy-start.11
  56.4 2.8 %copy.43 = bf16[8,289,289]{1,2,0:T(8,128)(2,1)} copy(bf16[8,289,289]{2,0,1:T(8,128)(2,1)S(1)} %copy-done) | data formatting | bytes 2672672 | tf_op args[3]
  59.2 0.0 copy-done.6
  59.2 0.0 copy-done.11
  59.2 0.2 fusion.57
  59.4 0.6 pad_clamp_fusion.1
  60.0 0.0 copy-start.2
  60.0 7.1 %gather_fusion = bf16[8,289,289]{2,0,1:T(8,128)(2,1)} fusion(bf16[8,289,289]{2,0,1:T(8,128)(2,1)S(1)} %copy-done, s32[1024]{0:T(1024)} %pad_clamp_fusion.1), kind=kCustom, calls=%fused_computation | custom fusion | bytes 2672704 | tf_op jit(solution)/shard_map/jit(_take)/gather | solution.py:121
  67.1 0.0 copy-done.2
  67.1 3.1 %copy.38 = bf16[8,289,289]{1,0,2:T(8,128)(2,1)} copy(bf16[8,289,289]{2,0,1:T(8,128)(2,1)S(1)} %copy-done.2) | data formatting | bytes 2672672 | tf_op args[2]
  70.2 3.4 %reshape.140 = bf16[2312,289]{0,1:T(8,128)(2,1)S(1)} reshape(bf16[8,289,289]{1,0,2:T(8,128)(2,1)} %copy.38) | data formatting | bytes 2672672 | tf_op jit(solution)/shard_map/reshape | solution.py:27
  73.6 0.0 copy-done.8
  73.6 0.0 copy-done.9
  73.6 0.1 copy.39
  73.8 0.7 reshape.143.idx_ref
  74.5 3.0 %pad.4.fs_ref = bf16[8,289,384]{2,1,0:T(8,128)(2,1)} pad(bf16[8,289,289]{2,1,0:T(8,128)(2,1)} %bitcast.95, bf16[]{:T(256)} %constant.91.clone.1), padding=0_0x0_0x0_95 | pad | bytes 3111954 | tf_op jit(solution)/shard_map/jit(_pad)/pad | solution.py:65
  77.6 0.0 copy-done.13
  77.6 0.2 fusion.58
  77.8 0.0 copy-done.12
  77.8 0.2 and_reduce_fusion
  78.0 1.2 %constant_dynamic-slice_fusion = bf16[1,289,289]{2,0,1:T(2,128)(2,1)} fusion(bf16[8,289,289]{2,0,1:T(8,128)(2,1)S(1)} %copy-done.2, s32[]{:T(128)S(6)} %select_n.70), kind=kLoop, calls=%fused_computation.60 | loop fusion | bytes 334088 | tf_op jit(solution)/shard_map/dynamic_slice | solution.py:129
  79.2 0.0 copy-done.3
  79.2 1.6 %select_bitcast_fusion = bf16[289,8,289]{2,1,0:T(8,128)(2,1)} fusion(bf16[8,289,289]{2,0,1:T(8,128)(2,1)S(1)} %copy-done.3, pred[8]{0:T(512)(128)(4,1)S(1)} %get-tuple-element.6), kind=kLoop, calls=%fused_computation.10 | loop fusion | flops 668168 | bytes 2672680 | tf_op jit(solution)/shard_map/jit(_take)/select_n | solution.py:121
  80.8 0.0 copy-done.7
  80.9 0.6 gather_fusion.1
  81.4 0.1 select_bitcast_fusion.1
  81.5 2.1 %fusion.40 = bf16[289]{0:T(512)(128)(2,1)S(1)} fusion(bf16[289,8,289]{2,1,0:T(8,128)(2,1)} %select_bitcast_fusion, bf16[8,289,1]{1,0,2:T(8,128)(2,1)S(1)} %select_bitcast_fusion.1), kind=kOutput, calls=%fused_computation.28 | convolution fusion | flops 1336336 | bytes 1341538 | tf_op jit(solution)/shard_map/dot_general | solution.py:126
  83.7 0.0 copy-done.5
  83.7 0.2 convolution_reduce_fusion
  83.9 0.7 fusion.1
  84.6 0.3 fusion
  84.9 0.1 convert_element_type.73
  85.1 0.4 convolution_bitcast_fusion
  85.5 0.4 reshape.141
  85.9 0.2 copy.44
  86.1 13.4 %all-to-all-done.2 = bf16[64,16,289]{2,1,0:T(8,128)(2,1)} async-done(((bf16[64,16,289]{2,1,0:T(8,128)(2,1)}), bf16[64,16,289]{2,1,0:T(8,128)(2,1)}, u32[]{:S(2)}, u32[]{:S(2)}) %all-to-all-start.2) | async-done | bytes 591904 | tf_op jit(solution)/shard_map/all_to_all | solution.py:109
  99.5 15.9 %shard_map.91 = f32[384,512]{1,0:T(8,128)} custom-call(s32[8192]{0:T(1024)} %reshape.143.idx_ref, bf16[512,289]{1,0:T(8,128)(2,1)} %bitcast.94, bf16[1024,289]{1,0:T(8,128)(2,1)} %bitcast.28.arr_ref, bf16[8,289,384]{2,1,0:T(8,128)(2,1)} %pad.4.fs_ref), custom_call_target="tpu_custom_call" | custom-call | tf_op jit(solution)/shard_map/pallas_call | solution.py:68
  115.4 1.9 %fusion.46 = bf16[289,512]{1,0:T(8,128)(2,1)} fusion(f32[289,512]{1,0:T(8,128)S(1)} %copy.44, f32[384,512]{1,0:T(8,128)} %shard_map.91), kind=kLoop, calls=%fused_computation.33 | loop fusion | flops 295936 | bytes 1479680 | tf_op jit(solution)/shard_map/convert_element_type | solution.py:136
  (16 shorter events, 0.1 us)
Async XLA Ops:
  0.0 3.7 %copy-start.4 = (bf16[8,289,289]{2,0,1:T(8,128)(2,1)S(1)}, bf16[8,289,289]{2,0,1:T(8,128)(2,1)}, u32[]{:S(2)}) copy-start(bf16[8,289,289]{2,0,1:T(8,128)(2,1)} %param.10) | copy-start | bytes 4009012
  1.3 19.7 %copy-start.1 = (bf16[289,512]{0,1:T(8,128)(2,1)}, bf16[289,512]{0,1:T(8,128)(2,1)S(1)}, u32[]{:S(2)}) copy-start(bf16[289,512]{0,1:T(8,128)(2,1)S(1)} %copy.31) | copy-start | bytes 887812
  3.7 17.0 %copy-start.10 = (s32[1,1,64,16]{2,3,1,0:T(8,128)S(1)}, s32[1,1,64,16]{2,3,1,0:T(8,128)}, u32[]{:S(2)}) copy-start(s32[1,1,64,16]{2,3,1,0:T(8,128)} %param.13) | copy-start | bytes 12292
  5.5 27.8 %all-to-all-start = ((bf16[289,16,1]{0,2,1:T(2,128)(2,1)}), bf16[289,16,1]{0,2,1:T(2,128)(2,1)S(1)}, u32[]{:S(2)}, u32[]{:S(2)}) async-start(bf16[289,16,1]{0,2,1:T(2,128)(2,1)} %reshape.138), calls=%async_computation | async-start | bytes 49152 | tf_op jit(solution)/shard_map/all_to_all | solution.py:86
  35.4 21.0 %copy-start = (bf16[8,289,289]{2,0,1:T(8,128)(2,1)S(1)}, bf16[8,289,289]{2,0,1:T(8,128)(2,1)}, u32[]{:S(2)}) copy-start(bf16[8,289,289]{2,0,1:T(8,128)(2,1)} %param.12) | copy-start | bytes 4009012
  36.0 13.7 %all-to-all-start.1 = ((bf16[289,32,2]{0,2,1:T(2,128)(2,1)}), bf16[289,32,2]{0,2,1:T(2,128)(2,1)S(1)}, u32[]{:S(2)}, u32[]{:S(2)}) async-start(bf16[289,32,2]{0,2,1:T(2,128)(2,1)} %broadcast_in_dim.43), calls=%async_computation.1 | async-start | bytes 98304 | tf_op jit(solution)/shard_map/all_to_all | solution.py:86
  49.8 9.4 %copy-start.6 = (bf16[289,32,2]{0,2,1:T(2,128)(2,1)}, bf16[289,32,2]{0,2,1:T(2,128)(2,1)S(1)}, u32[]{:S(2)}) copy-start(bf16[289,32,2]{0,2,1:T(2,128)(2,1)S(1)} %all-to-all-done.1) | copy-start | bytes 110980
  49.8 49.7 %all-to-all-start.2 = ((bf16[64,16,289]{2,1,0:T(8,128)(2,1)}), bf16[64,16,289]{2,1,0:T(8,128)(2,1)}, u32[]{:S(2)}, u32[]{:S(2)}) async-start(bf16[64,16,289]{2,1,0:T(8,128)(2,1)} %broadcast_select_fusion), calls=%async_computation.2 | async-start | bytes 1572864 | tf_op jit(solution)/shard_map/all_to_all | solution.py:109
  56.3 2.8 %copy-start.11 = (s32[8,64]{1,0:T(8,128)S(1)}, s32[8,64]{1,0:T(8,128)}, u32[]{:S(2)}) copy-start(s32[8,64]{1,0:T(8,128)} %param.17) | copy-start | bytes 6148
  60.0 7.1 %copy-start.2 = (bf16[8,289,289]{2,0,1:T(8,128)(2,1)S(1)}, bf16[8,289,289]{2,0,1:T(8,128)(2,1)}, u32[]{:S(2)}) copy-start(bf16[8,289,289]{2,0,1:T(8,128)(2,1)} %param.11) | copy-start | bytes 4009012
  70.2 3.4 %copy-start.8 = (s32[16,512]{1,0:T(8,128)S(1)}, s32[16,512]{1,0:T(8,128)}, u32[]{:S(2)}) copy-start(s32[16,512]{1,0:T(8,128)} %param.14) | copy-start | bytes 98308
  70.2 3.5 %copy-start.9 = (s32[16,512]{1,0:T(8,128)S(1)}, s32[16,512]{1,0:T(8,128)}, u32[]{:S(2)}) copy-start(s32[16,512]{1,0:T(8,128)} %param.15) | copy-start | bytes 98308
  74.5 3.1 %copy-start.13 = (s32[8,64]{1,0:T(8,128)S(1)}, s32[8,64]{1,0:T(8,128)}, u32[]{:S(2)}) copy-start(s32[8,64]{1,0:T(8,128)} %param.16) | copy-start | bytes 6148
  74.5 3.2 %copy-start.12 = (s32[8,64]{1,0:T(8,128)S(1)}, s32[8,64]{1,0:T(8,128)}, u32[]{:S(2)}) copy-start(s32[8,64]{1,0:T(8,128)} %param.17) | copy-start | bytes 6148
  74.5 4.7 %copy-start.3 = (bf16[8,289,289]{2,0,1:T(8,128)(2,1)S(1)}, bf16[8,289,289]{2,0,1:T(8,128)(2,1)}, u32[]{:S(2)}) copy-start(bf16[8,289,289]{2,0,1:T(8,128)(2,1)} %gather_fusion) | copy-start | bytes 4009012
  79.2 1.6 %copy-start.7 = (bf16[289,32,2]{0,2,1:T(2,128)(2,1)S(1)}, bf16[289,32,2]{0,2,1:T(2,128)(2,1)}, u32[]{:S(2)}) copy-start(bf16[289,32,2]{0,2,1:T(2,128)(2,1)} %copy-done.6) | copy-start | bytes 110980
  81.4 2.2 %copy-start.5 = (bf16[1,289,289]{2,0,1:T(2,128)(2,1)S(1)}, bf16[1,289,289]{2,0,1:T(2,128)(2,1)}, u32[]{:S(2)}) copy-start(bf16[1,289,289]{2,0,1:T(2,128)(2,1)} %constant_dynamic-slice_fusion) | copy-start | bytes 501130

commit v11 on v9

--- a/solution.py
+++ b/solution.py
@@ -110,9 +110,9 @@
     upward = multipoles
     for level in range(LOCAL_LEVELS):
         upward = lift_level(upward, up_shift).astype(jnp.bfloat16)
-    row_boxes = gather_columns(upward, "gz")
-    row_multi = lift_level(row_boxes, up_shift).astype(jnp.bfloat16)
-    coarse_multi = gather_columns(row_multi, ("gx", "gy"))
+    slice_boxes = gather_columns(upward, ("gy", "gz"))
+    slice_multi = lift_level(slice_boxes, up_shift).astype(jnp.bfloat16)
+    coarse_multi = gather_columns(slice_multi, "gx")
     coarse_cols = coarse_src[:, coarse_box]
     coarse_kinds = coarse_kind[:, coarse_box]
     list_len = coarse_cols.shape[0]

time: 117 us -> 118 us (level)
  waiting for transfers between devices: 24.9 us -> 26.2 us
    all_to_all x2, waiting for transfers between devices: 13.4 us -> 14.7 us  [gather_columns(): return lax.all_to_all(spread, axes, split_axis=1, concat_axis=1, tiled=True)]
where the time goes in v11:
time: 118 us
  local copies, waits for them, and re-layouts  32.9 us (28%)
  starting transfers between devices  29.1 us (25%)
  waiting for transfers between devices  26.2 us (22%)
  Pallas kernels  16 us (14%)
  matrix products  7.79 us (7%)
  other arithmetic  5.32 us (5%)
    all_to_all x2, starting transfers between devices, gather_columns(): return lax.all_to_all(spread, axes, split_axis=1, concat_axis=1, tiled=True)  23 us
    pallas_call x1, Pallas kernels, far_field(): pl.pallas_call(far_kernel, out_shape=jax.ShapeDtypeStruct((width, targets...  16 us
    all_to_all x2, waiting for transfers between devices, gather_columns(): return lax.all_to_all(spread, axes, split_axis=1, concat_axis=1, tiled=True)  14.7 us
    all_to_all x1, waiting for transfers between devices, on_device(): lax.all_to_all(outgoing, ('gy', 'gz'), split_axis=1, concat_axis=1, tiled...  11.5 us
    unnamed x23, local copies, waits for them, and re-layouts  8.45 us
    gather x1, local copies, waits for them, and re-layouts, on_device(): jnp.take(far_shift, coarse_kinds, axis=0).transpose(1, 0, 2)  6.86 us
    all_to_all x1, starting transfers between devices, on_device(): lax.all_to_all(outgoing, ('gy', 'gz'), split_axis=1, concat_axis=1, tiled...  6.03 us
    dot_general x4, matrix products, lift_level(): lax.dot_general(up_shift, child_stack, (((2,), (1,)), ((0,), (0,))), pref...  3.99 us
  transfers between devices with their start and end apart: 3, of which 3 were waited for; matrix products, arithmetic and copies ran while one was open for 31% of the time, Pallas kernels for 0%

profile of v11, /device:TPU:8, one launch (start us, length us, event | category | flops | bytes accessed | tf_op | source)
XLA Modules:
  0.0 117.6 jit_solution(9727071977654752860)
XLA Ops:
  0.0 0.0 copy-start.2
  0.0 1.3 %copy.33 = bf16[289,512]{0,1:T(8,128)(2,1)S(1)} copy(bf16[289,512]{1,0:T(8,128)(2,1)} %param.9) | data formatting | bytes 591872 | tf_op args[0]
  1.3 2.2 %fusion.19 = bf16[289,8,8]{0,2,1:T(8,128)(2,1)S(1)} fusion(bf16[8,289,289]{2,0,1:T(8,128)(2,1)} %param.10, bf16[8,289,64]{1,0,2:T(8,128)(2,1)S(1)} %bitcast.94), kind=kOutput, calls=%fused_computation.22 | convolution fusion | flops 85544000 | bytes 1669264 | tf_op jit(solution)/shard_map/dot_general | solution.py:17
  3.5 0.0 copy-done.2
  3.5 0.0 copy-start.6
  3.6 0.6 fusion.34
  4.1 0.6 fusion.40
  4.8 0.7 reshape.138
  5.5 18.7 %all-to-all-start = ((bf16[289,64,1]{0,2,1:T(2,128)(2,1)}), bf16[289,64,1]{0,2,1:T(2,128)(2,1)S(1)}, u32[]{:S(2)}, u32[]{:S(2)}) async-start(bf16[289,64,1]{0,2,1:T(2,128)(2,1)} %reshape.138), calls=%async_computation | async-start | bytes 196608 | tf_op jit(solution)/shard_map/all_to_all | solution.py:87
  24.2 0.0 copy-done.6
  24.2 0.1 copy.43
  24.3 0.1 reshape.145
  24.4 3.9 %gather_fusion.2 = bf16[1024,289]{1,0:T(8,128)(2,1)S(1)} fusion(bf16[289,512]{0,1:T(8,128)(2,1)S(1)} %copy.33, s32[1024]{0:T(1024)S(1)} %broadcast_clamp_fusion), kind=kCustom, calls=%fused_computation.2 | custom fusion | bytes 1187840 | tf_op jit(solution)/shard_map/jit(_take)/gather | solution.py:108
  28.3 0.1 copy.42
  28.4 10.3 %all-to-all-done = bf16[289,64,1]{0,2,1:T(2,128)(2,1)S(1)} async-done(((bf16[289,64,1]{0,2,1:T(2,128)(2,1)}), bf16[289,64,1]{0,2,1:T(2,128)(2,1)S(1)}, u32[]{:S(2)}, u32[]{:S(2)}) %all-to-all-start) | async-done | bytes 37024 | tf_op jit(solution)/shard_map/all_to_all | solution.py:87
  38.8 0.6 fusion.37
  39.3 0.0 copy-start
  39.3 0.6 broadcast_in_dim.43
  40.0 4.3 %all-to-all-start.1 = ((bf16[289,8,8]{0,2,1:T(8,128)(2,1)}), bf16[289,8,8]{0,2,1:T(8,128)(2,1)S(1)}, u32[]{:S(2)}, u32[]{:S(2)}) async-start(bf16[289,8,8]{0,2,1:T(8,128)(2,1)} %broadcast_in_dim.43), calls=%async_computation.1 | async-start | bytes 98304 | tf_op jit(solution)/shard_map/all_to_all | solution.py:87
  44.3 1.1 broadcast_select_fusion
  45.4 4.4 %all-to-all-done.1 = bf16[289,8,8]{0,2,1:T(8,128)(2,1)S(1)} async-done(((bf16[289,8,8]{0,2,1:T(8,128)(2,1)}), bf16[289,8,8]{0,2,1:T(8,128)(2,1)S(1)}, u32[]{:S(2)}, u32[]{:S(2)}) %all-to-all-start.1) | async-done | bytes 37024 | tf_op jit(solution)/shard_map/all_to_all | solution.py:87
  49.8 6.0 %all-to-all-start.2 = ((bf16[289,64,16]{0,2,1:T(8,128)(2,1)}), bf16[289,64,16]{0,2,1:T(8,128)(2,1)S(1)}, u32[]{:S(2)}, u32[]{:S(2)}) async-start(bf16[289,64,16]{0,2,1:T(8,128)(2,1)} %broadcast_select_fusion), calls=%async_computation.2 | async-start | bytes 1572864 | tf_op jit(solution)/shard_map/all_to_all | solution.py:109
  55.9 0.0 copy-done
  55.9 0.0 copy-start.7
  55.9 2.8 %copy.46 = bf16[8,289,289]{1,2,0:T(8,128)(2,1)} copy(bf16[8,289,289]{2,0,1:T(8,128)(2,1)S(1)} %copy-done) | data formatting | bytes 2672672 | tf_op args[3]
  58.7 0.0 copy-done.7
  58.7 0.2 fusion.57
  58.9 6.9 %gather_fusion = bf16[8,289,289]{2,0,1:T(8,128)(2,1)} fusion(bf16[8,289,289]{2,0,1:T(8,128)(2,1)S(1)} %copy-done, s32[1024]{0:T(1024)S(1)} %pad_clamp_fusion.1), kind=kCustom, calls=%fused_computation | custom fusion | bytes 2672704 | tf_op jit(solution)/shard_map/jit(_take)/gather | solution.py:121
  65.8 4.2 %copy.40 = bf16[8,289,289]{1,0,2:T(8,128)(2,1)} copy(bf16[8,289,289]{2,0,1:T(8,128)(2,1)} %param.11) | data formatting | bytes 2672672 | tf_op args[2]
  70.0 0.0 copy-start.4
  70.0 0.0 copy-start.5
  70.0 3.5 %reshape.140 = bf16[2312,289]{0,1:T(8,128)(2,1)S(1)} reshape(bf16[8,289,289]{1,0,2:T(8,128)(2,1)} %copy.40) | data formatting | bytes 2672672 | tf_op jit(solution)/shard_map/reshape | solution.py:27
  73.5 0.0 copy-done.4
  73.5 0.0 copy-done.5
  73.5 0.1 copy.41
  73.6 0.8 reshape.143.idx_ref
  74.4 0.0 copy-start.8
  74.4 0.0 copy-start.3
  74.4 3.3 %pad.9.fs_ref = bf16[8,384,384]{2,1,0:T(8,128)(2,1)} pad(bf16[8,289,289]{2,1,0:T(8,128)(2,1)} %bitcast.96, bf16[]{:T(256)} %constant.91.clone.1), padding=0_0x0_95x0_95 | pad | bytes 3695634 | tf_op jit(solution)/shard_map/jit(_pad)/pad | solution.py:63
  77.7 0.0 copy-done.8
  77.7 0.2 fusion.58
  77.9 0.2 and_reduce_fusion
  78.1 1.9 %constant_dynamic-slice_fusion = bf16[1,289,289]{2,0,1:T(2,128)(2,1)S(1)} fusion(bf16[8,289,289]{2,0,1:T(8,128)(2,1)} %param.11, s32[]{:T(128)S(6)} %select_n.70), kind=kLoop, calls=%fused_computation.61 | loop fusion | bytes 334088 | tf_op jit(solution)/shard_map/dynamic_slice | solution.py:129
  80.1 0.0 copy-done.3
  80.1 1.5 %select_bitcast_fusion = bf16[289,8,289]{2,1,0:T(8,128)(2,1)} fusion(bf16[8,289,289]{2,0,1:T(8,128)(2,1)S(1)} %copy-done.3, pred[8]{0:T(512)(128)(4,1)S(1)} %get-tuple-element.6), kind=kLoop, calls=%fused_computation.10 | loop fusion | flops 668168 | bytes 2672680 | tf_op jit(solution)/shard_map/jit(_take)/select_n | solution.py:121
  81.6 0.6 gather_fusion.1
  82.2 0.0 copy-start.1
  82.2 0.1 select_bitcast_fusion.1
  82.3 2.2 %fusion.43 = bf16[289]{0:T(512)(128)(2,1)S(1)} fusion(bf16[289,8,289]{2,1,0:T(8,128)(2,1)} %select_bitcast_fusion, bf16[8,289,1]{1,0,2:T(8,128)(2,1)S(1)} %select_bitcast_fusion.1), kind=kOutput, calls=%fused_computation.30 | convolution fusion | flops 1336336 | bytes 1341538 | tf_op jit(solution)/shard_map/dot_general | solution.py:126
  84.5 0.2 convolution_reduce_fusion
  84.7 0.0 copy-done.1
  84.7 0.7 fusion.1
  85.4 0.3 fusion
  85.7 0.1 convert_element_type.75
  85.9 0.4 convolution_bitcast_fusion
  86.3 0.4 reshape.141
  86.7 0.2 copy.47
  87.0 11.5 %all-to-all-done.2 = bf16[289,64,16]{0,2,1:T(8,128)(2,1)S(1)} async-done(((bf16[289,64,16]{0,2,1:T(8,128)(2,1)}), bf16[289,64,16]{0,2,1:T(8,128)(2,1)S(1)}, u32[]{:S(2)}, u32[]{:S(2)}) %all-to-all-start.2) | async-done | bytes 591904 | tf_op jit(solution)/shard_map/all_to_all | solution.py:109
  98.5 0.1 maximum_bitcast_fusion
  98.6 1.2 pad.8.buf_ref
  99.8 16.0 %shard_map.91 = f32[384,512]{1,0:T(8,128)} custom-call(s32[8192]{0:T(1024)} %reshape.143.idx_ref, bf16[1536,384]{1,0:T(8,128)(2,1)} %pad.8.buf_ref, bf16[8,384,384]{2,1,0:T(8,128)(2,1)} %pad.9.fs_ref), custom_call_target="tpu_custom_call" | custom-call | tf_op jit(solution)/shard_map/pallas_call | solution.py:65
  115.8 1.9 %fusion.46 = bf16[289,512]{1,0:T(8,128)(2,1)} fusion(f32[289,512]{1,0:T(8,128)S(1)} %copy.47, f32[384,512]{1,0:T(8,128)} %shard_map.91), kind=kLoop, calls=%fused_computation.34 | loop fusion | flops 295936 | bytes 1479680 | tf_op jit(solution)/shard_map/convert_element_type | solution.py:137
  (9 shorter events, 0.1 us)
Async XLA Ops:
  0.0 3.5 %copy-start.2 = (bf16[8,289,289]{2,0,1:T(8,128)(2,1)S(1)}, bf16[8,289,289]{2,0,1:T(8,128)(2,1)}, u32[]{:S(2)}) copy-start(bf16[8,289,289]{2,0,1:T(8,128)(2,1)} %param.10) | copy-start | bytes 4009012
  3.5 20.7 %copy-start.6 = (s32[1,1,64,16]{2,3,1,0:T(8,128)S(1)}, s32[1,1,64,16]{2,3,1,0:T(8,128)}, u32[]{:S(2)}) copy-start(s32[1,1,64,16]{2,3,1,0:T(8,128)} %param.13) | copy-start | bytes 12292
  5.5 33.3 %all-to-all-start = ((bf16[289,64,1]{0,2,1:T(2,128)(2,1)}), bf16[289,64,1]{0,2,1:T(2,128)(2,1)S(1)}, u32[]{:S(2)}, u32[]{:S(2)}) async-start(bf16[289,64,1]{0,2,1:T(2,128)(2,1)} %reshape.138), calls=%async_computation | async-start | bytes 196608 | tf_op jit(solution)/shard_map/all_to_all | solution.py:87
  39.3 16.6 %copy-start = (bf16[8,289,289]{2,0,1:T(8,128)(2,1)S(1)}, bf16[8,289,289]{2,0,1:T(8,128)(2,1)}, u32[]{:S(2)}) copy-start(bf16[8,289,289]{2,0,1:T(8,128)(2,1)} %param.12) | copy-start | bytes 4009012
  40.0 9.8 %all-to-all-start.1 = ((bf16[289,8,8]{0,2,1:T(8,128)(2,1)}), bf16[289,8,8]{0,2,1:T(8,128)(2,1)S(1)}, u32[]{:S(2)}, u32[]{:S(2)}) async-start(bf16[289,8,8]{0,2,1:T(8,128)(2,1)} %broadcast_in_dim.43), calls=%async_computation.1 | async-start | bytes 98304 | tf_op jit(solution)/shard_map/all_to_all | solution.py:87
  49.8 48.7 %all-to-all-start.2 = ((bf16[289,64,16]{0,2,1:T(8,128)(2,1)}), bf16[289,64,16]{0,2,1:T(8,128)(2,1)S(1)}, u32[]{:S(2)}, u32[]{:S(2)}) async-start(bf16[289,64,16]{0,2,1:T(8,128)(2,1)} %broadcast_select_fusion), calls=%async_computation.2 | async-start | bytes 1572864 | tf_op jit(solution)/shard_map/all_to_all | solution.py:109
  55.9 2.8 %copy-start.7 = (s32[8,64]{1,0:T(8,128)S(1)}, s32[8,64]{1,0:T(8,128)}, u32[]{:S(2)}) copy-start(s32[8,64]{1,0:T(8,128)} %param.17) | copy-start | bytes 6148
  70.0 3.5 %copy-start.4 = (s32[16,512]{1,0:T(8,128)S(1)}, s32[16,512]{1,0:T(8,128)}, u32[]{:S(2)}) copy-start(s32[16,512]{1,0:T(8,128)} %param.14) | copy-start | bytes 98308
  70.0 3.5 %copy-start.5 = (s32[16,512]{1,0:T(8,128)S(1)}, s32[16,512]{1,0:T(8,128)}, u32[]{:S(2)}) copy-start(s32[16,512]{1,0:T(8,128)} %param.15) | copy-start | bytes 98308
  74.4 3.3 %copy-start.8 = (s32[8,64]{1,0:T(8,128)S(1)}, s32[8,64]{1,0:T(8,128)}, u32[]{:S(2)}) copy-start(s32[8,64]{1,0:T(8,128)} %param.16) | copy-start | bytes 6148
  74.4 5.7 %copy-start.3 = (bf16[8,289,289]{2,0,1:T(8,128)(2,1)S(1)}, bf16[8,289,289]{2,0,1:T(8,128)(2,1)}, u32[]{:S(2)}) copy-start(bf16[8,289,289]{2,0,1:T(8,128)(2,1)} %gather_fusion) | copy-start | bytes 4009012
  82.2 2.5 %copy-start.1 = (bf16[8,289,289]{2,0,1:T(8,128)(2,1)S(1)}, bf16[8,289,289]{2,0,1:T(8,128)(2,1)}, u32[]{:S(2)}) copy-start(bf16[8,289,289]{2,0,1:T(8,128)(2,1)} %param.11) | copy-start | bytes 4009012

commit v12 on v9

--- a/solution.py
+++ b/solution.py
@@ -29,7 +29,7 @@
     return spread.reshape(8, coefs, count).transpose(1, 2, 0).reshape(coefs, 8 * count)
 
 
-def far_kernel(idx_ref, buf_ref, fs_ref, out_ref, table_ref, acc_ref):
+def far_kernel(idx_ref, buf_ref, fs_ref, chain_ref, out_ref, table_ref, acc_ref):
     kinds = fs_ref.shape[0]
     rows = buf_ref.shape[0]
     for k in range(kinds):
@@ -50,11 +50,15 @@
         return carry
 
     lax.fori_loop(0, targets, body, 0, unroll=8)
+    coefs = out_ref.shape[0]
     for j in range(CHUNKS):
-        out_ref[pl.ds(j * LANE, LANE), :] = acc_ref[pl.ds(j, targets, stride=CHUNKS), :].T
+        block = acc_ref[pl.ds(j, targets, stride=CHUNKS), :].T
+        used = min(LANE, coefs - j * LANE)
+        near = chain_ref[pl.ds(j * LANE, used), :]
+        out_ref[pl.ds(j * LANE, used), :] = (block[:used] + near).astype(out_ref.dtype)
 
 
-def far_field(buffer, far_shift, leaf_src, leaf_kind):
+def far_field(buffer, far_shift, leaf_src, leaf_kind, chain_part):
     coefs, rows = buffer.shape
     kinds = far_shift.shape[0]
     lists, targets = leaf_src.shape
@@ -64,9 +68,10 @@
     idx = (CHUNKS * (leaf_kind * rows + leaf_src)).T.reshape(lists * targets)
     out = pl.pallas_call(
         far_kernel,
-        out_shape=jax.ShapeDtypeStruct((width, targets), jnp.float32),
+        out_shape=jax.ShapeDtypeStruct((coefs, targets), jnp.bfloat16),
         in_specs=[
             pl.BlockSpec(memory_space=pltpu.SMEM),
+            pl.BlockSpec(memory_space=pltpu.VMEM),
             pl.BlockSpec(memory_space=pltpu.VMEM),
             pl.BlockSpec(memory_space=pltpu.VMEM),
         ],
@@ -75,8 +80,8 @@
             pltpu.VMEM((kinds * rows * CHUNKS, LANE), jnp.float32),
             pltpu.VMEM((targets * CHUNKS, LANE), jnp.float32),
         ],
-    )(idx, buf_t, fs_t)
-    return out[:coefs, :]
+    )(idx, buf_t, fs_t, chain_part)
+    return out
 
 
 def gather_columns(column_block, axes):
@@ -133,8 +138,7 @@
         downward = lower_level(downward, down_shift).astype(jnp.bfloat16)
     chain_part = lower_level(downward, down_shift)
     buffer = jnp.concatenate([multipoles, arrived], axis=1)
-    far_total = far_field(buffer, far_shift, leaf_src, leaf_kind)
-    return (chain_part + far_total).astype(jnp.bfloat16)
+    return far_field(buffer, far_shift, leaf_src, leaf_kind, chain_part)
 
 
 def solution(mesh):

time: 117 us -> 115 us (0.983)
  other arithmetic: 5.32 us -> 3.46 us
    convert_element_type x1 -> x0, other arithmetic: 1.87 us -> none  [on_device(): return (chain_part + far_total).astype(jnp.bfloat16)]
  transfers between devices with their start and end apart: 3 -> 3, of which waited for: 3 -> 3; matrix products, arithmetic and copies ran while one was open for 31% -> 32% of each run, Pallas kernels for 0% -> 0%
where the time goes in v12:
time: 115 us; the launch traced here: 114 us
  local copies, waits for them, and re-layouts  33.7 us (29%)
  starting transfers between devices  29.1 us (25%)
  waiting for transfers between devices  24.1 us (21%)
  Pallas kernels  15.9 us (14%)
  matrix products  7.79 us (7%)
  other arithmetic  3.46 us (3%)
    all_to_all x2, starting transfers between devices, gather_columns(): return lax.all_to_all(spread, axes, split_axis=1, concat_axis=1, tiled=True)  22.7 us
    pallas_call x1, Pallas kernels, far_field(): pl.pallas_call(far_kernel, out_shape=jax.ShapeDtypeStruct((coefs, targets...  15.9 us
    all_to_all x2, waiting for transfers between devices, gather_columns(): return lax.all_to_all(spread, axes, split_axis=1, concat_axis=1, tiled=True)  13.4 us
    all_to_all x1, waiting for transfers between devices, on_device(): lax.all_to_all(outgoing, ('gy', 'gz'), split_axis=1, concat_axis=1, tiled...  10.6 us
    unnamed x23, local copies, waits for them, and re-layouts  8.46 us
    gather x1, local copies, waits for them, and re-layouts, on_device(): jnp.take(far_shift, coarse_kinds, axis=0).transpose(1, 0, 2)  6.85 us
    all_to_all x1, starting transfers between devices, on_device(): lax.all_to_all(outgoing, ('gy', 'gz'), split_axis=1, concat_axis=1, tiled...  6.35 us
    dot_general x4, matrix products, lift_level(): lax.dot_general(up_shift, child_stack, (((2,), (1,)), ((0,), (0,))), pref...  3.99 us
  transfers between devices with their start and end apart: 3, of which 3 were waited for; matrix products, arithmetic and copies ran while one was open for 32% of the time, Pallas kernels for 0%

profile of v12, /device:TPU:8, one launch (start us, length us, event | category | flops | bytes accessed | tf_op | source)
XLA Modules:
  0.0 114.3 jit_solution(8567518309129709221)
XLA Ops:
  0.0 0.0 copy-start.3
  0.0 1.3 %copy.36 = bf16[289,512]{0,1:T(8,128)(2,1)S(1)} copy(bf16[289,512]{1,0:T(8,128)(2,1)} %param.9) | data formatting | bytes 591872 | tf_op args[0]
  1.3 2.2 %fusion.19 = bf16[289,8,8]{0,2,1:T(8,128)(2,1)S(1)} fusion(bf16[8,289,289]{2,0,1:T(8,128)(2,1)} %param.10, bf16[8,289,64]{1,0,2:T(8,128)(2,1)S(1)} %bitcast.95), kind=kOutput, calls=%fused_computation.22 | convolution fusion | flops 85544000 | bytes 1669264 | tf_op jit(solution)/shard_map/dot_general | solution.py:17
  3.5 0.0 copy-done.3
  3.5 0.0 copy-start.6
  3.6 0.6 fusion.28
  4.1 0.6 fusion.37
  4.8 0.6 reshape.141
  5.4 15.2 %all-to-all-start.1 = ((bf16[289,16,1]{0,2,1:T(2,128)(2,1)}), bf16[289,16,1]{0,2,1:T(2,128)(2,1)S(1)}, u32[]{:S(2)}, u32[]{:S(2)}) async-start(bf16[289,16,1]{0,2,1:T(2,128)(2,1)} %reshape.141), calls=%async_computation.1 | async-start | bytes 49152 | tf_op jit(solution)/shard_map/all_to_all | solution.py:92
  20.6 0.0 copy-done.6
  20.6 0.1 copy.34
  20.7 0.1 reshape.138
  20.8 3.9 %gather_fusion = bf16[1024,289]{1,0:T(8,128)(2,1)S(1)} fusion(bf16[289,512]{0,1:T(8,128)(2,1)S(1)} %copy.36, s32[1024]{0:T(1024)S(1)} %broadcast_clamp_fusion), kind=kCustom, calls=%fused_computation | custom fusion | bytes 1187840 | tf_op jit(solution)/shard_map/jit(_take)/gather | solution.py:113
  24.7 0.1 copy.33
  24.8 8.3 %all-to-all-done.1 = bf16[289,16,1]{0,2,1:T(2,128)(2,1)S(1)} async-done(((bf16[289,16,1]{0,2,1:T(2,128)(2,1)}), bf16[289,16,1]{0,2,1:T(2,128)(2,1)S(1)}, u32[]{:S(2)}, u32[]{:S(2)}) %all-to-all-start.1) | async-done | bytes 9280 | tf_op jit(solution)/shard_map/all_to_all | solution.py:92
  33.2 0.6 fusion.43
  33.7 0.0 copy-start
  33.8 0.7 broadcast_in_dim.45
  34.4 7.5 %all-to-all-start.2 = ((bf16[289,32,2]{0,2,1:T(2,128)(2,1)}), bf16[289,32,2]{0,2,1:T(2,128)(2,1)S(1)}, u32[]{:S(2)}, u32[]{:S(2)}) async-start(bf16[289,32,2]{0,2,1:T(2,128)(2,1)} %broadcast_in_dim.45), calls=%async_computation.2 | async-start | bytes 98304 | tf_op jit(solution)/shard_map/all_to_all | solution.py:92
  42.0 1.1 broadcast_select_fusion
  43.0 5.1 %all-to-all-done.2 = bf16[289,32,2]{0,2,1:T(2,128)(2,1)S(1)} async-done(((bf16[289,32,2]{0,2,1:T(2,128)(2,1)}), bf16[289,32,2]{0,2,1:T(2,128)(2,1)S(1)}, u32[]{:S(2)}, u32[]{:S(2)}) %all-to-all-start.2) | async-done | bytes 37024 | tf_op jit(solution)/shard_map/all_to_all | solution.py:92
  48.1 6.3 %all-to-all-start = ((bf16[289,64,16]{0,2,1:T(8,128)(2,1)}), bf16[289,64,16]{0,2,1:T(8,128)(2,1)S(1)}, u32[]{:S(2)}, u32[]{:S(2)}) async-start(bf16[289,64,16]{0,2,1:T(8,128)(2,1)} %broadcast_select_fusion), calls=%async_computation | async-start | bytes 1572864 | tf_op jit(solution)/shard_map/all_to_all | solution.py:114
  54.5 0.0 copy-done
  54.5 0.0 copy-start.7
  54.6 2.8 %copy.37 = bf16[8,289,289]{1,2,0:T(8,128)(2,1)} copy(bf16[8,289,289]{2,0,1:T(8,128)(2,1)S(1)} %copy-done) | data formatting | bytes 2672672 | tf_op args[3]
  57.4 0.0 copy-done.7
  57.4 0.2 fusion.56
  57.6 6.8 %gather_fusion.1 = bf16[8,289,289]{2,0,1:T(8,128)(2,1)} fusion(bf16[8,289,289]{2,0,1:T(8,128)(2,1)S(1)} %copy-done, s32[1024]{0:T(1024)S(1)} %pad_clamp_fusion.1), kind=kCustom, calls=%fused_computation.1 | custom fusion | bytes 2672704 | tf_op jit(solution)/shard_map/jit(_take)/gather | solution.py:126
  64.4 4.2 %copy.46 = bf16[8,289,289]{1,0,2:T(8,128)(2,1)} copy(bf16[8,289,289]{2,0,1:T(8,128)(2,1)} %param.11) | data formatting | bytes 2672672 | tf_op args[2]
  68.6 0.0 copy-start.4
  68.6 0.0 copy-start.5
  68.6 3.4 %reshape.143 = bf16[2312,289]{0,1:T(8,128)(2,1)S(1)} reshape(bf16[8,289,289]{1,0,2:T(8,128)(2,1)} %copy.46) | data formatting | bytes 2672672 | tf_op jit(solution)/shard_map/reshape | solution.py:27
  72.1 0.0 copy-done.4
  72.1 0.0 copy-done.5
  72.1 0.1 copy.32
  72.2 0.7 reshape.136.idx_ref
  73.0 0.0 copy-start.8
  73.0 0.0 copy-start.2
  73.0 3.3 %pad.9.fs_ref = bf16[8,384,384]{2,1,0:T(8,128)(2,1)} pad(bf16[8,289,289]{2,1,0:T(8,128)(2,1)} %bitcast.96, bf16[]{:T(256)} %constant.79.clone.1), padding=0_0x0_95x0_95 | pad | bytes 3695634 | tf_op jit(solution)/shard_map/jit(_pad)/pad | solution.py:67
  76.3 0.0 copy-done.8
  76.3 0.2 fusion.57
  76.5 0.2 and_reduce_fusion
  76.7 1.9 %constant_dynamic-slice_fusion = bf16[1,289,289]{2,0,1:T(2,128)(2,1)S(1)} fusion(bf16[8,289,289]{2,0,1:T(8,128)(2,1)} %param.11, s32[]{:T(128)S(6)} %select_n.73), kind=kLoop, calls=%fused_computation.59 | loop fusion | bytes 334088 | tf_op jit(solution)/shard_map/dynamic_slice | solution.py:134
  78.7 0.0 copy-done.2
  78.7 1.5 %select_bitcast_fusion = bf16[289,8,289]{2,1,0:T(8,128)(2,1)} fusion(bf16[8,289,289]{2,0,1:T(8,128)(2,1)S(1)} %copy-done.2, pred[8]{0:T(512)(128)(4,1)S(1)} %get-tuple-element.6), kind=kLoop, calls=%fused_computation.10 | loop fusion | flops 668168 | bytes 2672680 | tf_op jit(solution)/shard_map/jit(_take)/select_n | solution.py:126
  80.3 0.6 gather_fusion.2
  80.8 0.0 copy-start.1
  80.8 0.1 select_bitcast_fusion.1
  80.9 2.2 %fusion.40 = bf16[289]{0:T(512)(128)(2,1)S(1)} fusion(bf16[289,8,289]{2,1,0:T(8,128)(2,1)} %select_bitcast_fusion, bf16[8,289,1]{1,0,2:T(8,128)(2,1)S(1)} %select_bitcast_fusion.1), kind=kOutput, calls=%fused_computation.29 | convolution fusion | flops 1336336 | bytes 1341538 | tf_op jit(solution)/shard_map/dot_general | solution.py:131
  83.1 0.2 convolution_reduce_fusion
  83.3 0.0 copy-done.1
  83.4 0.7 fusion.1
  84.0 0.3 fusion
  84.4 0.1 convert_element_type.72
  84.5 0.4 convolution_bitcast_fusion
  84.9 0.4 reshape.144
  85.4 1.1 copy.47.chain_ref
  86.4 10.6 %all-to-all-done = bf16[289,64,16]{0,2,1:T(8,128)(2,1)S(1)} async-done(((bf16[289,64,16]{0,2,1:T(8,128)(2,1)}), bf16[289,64,16]{0,2,1:T(8,128)(2,1)S(1)}, u32[]{:S(2)}, u32[]{:S(2)}) %all-to-all-start) | async-done | bytes 591904 | tf_op jit(solution)/shard_map/all_to_all | solution.py:114
  97.1 0.1 maximum_bitcast_fusion
  97.2 1.2 %pad.8.buf_ref = bf16[1536,384]{1,0:T(8,128)(2,1)} pad(bf16[1536,289]{1,0:T(8,128)(2,1)S(1)} %maximum_bitcast_fusion, bf16[]{:T(256)} %constant.79.clone.1), padding=0_0x0_95 | pad | bytes 2067458 | tf_op jit(solution)/shard_map/jit(_pad)/pad | solution.py:66
  98.4 15.9 %shard_map.91 = bf16[289,512]{1,0:T(8,128)(2,1)} custom-call(s32[8192]{0:T(1024)} %reshape.136.idx_ref, bf16[1536,384]{1,0:T(8,128)(2,1)} %pad.8.buf_ref, bf16[8,384,384]{2,1,0:T(8,128)(2,1)} %pad.9.fs_ref, f32[289,512]{1,0:T(8,128)} %copy.47.chain_ref), custom_call_target="tpu_custom_call" | custom-call | tf_op jit(solution)/shard_map/pallas_call | solution.py:69
  (10 shorter events, 0.1 us)
Async XLA Ops:
  0.0 3.5 %copy-start.3 = (bf16[8,289,289]{2,0,1:T(8,128)(2,1)S(1)}, bf16[8,289,289]{2,0,1:T(8,128)(2,1)}, u32[]{:S(2)}) copy-start(bf16[8,289,289]{2,0,1:T(8,128)(2,1)} %param.10) | copy-start | bytes 4009012
  3.5 17.0 %copy-start.6 = (s32[1,1,64,16]{2,3,1,0:T(8,128)S(1)}, s32[1,1,64,16]{2,3,1,0:T(8,128)}, u32[]{:S(2)}) copy-start(s32[1,1,64,16]{2,3,1,0:T(8,128)} %param.13) | copy-start | bytes 12292
  5.4 27.8 %all-to-all-start.1 = ((bf16[289,16,1]{0,2,1:T(2,128)(2,1)}), bf16[289,16,1]{0,2,1:T(2,128)(2,1)S(1)}, u32[]{:S(2)}, u32[]{:S(2)}) async-start(bf16[289,16,1]{0,2,1:T(2,128)(2,1)} %reshape.141), calls=%async_computation.1 | async-start | bytes 49152 | tf_op jit(solution)/shard_map/all_to_all | solution.py:92
  33.7 20.8 %copy-start = (bf16[8,289,289]{2,0,1:T(8,128)(2,1)S(1)}, bf16[8,289,289]{2,0,1:T(8,128)(2,1)}, u32[]{:S(2)}) copy-start(bf16[8,289,289]{2,0,1:T(8,128)(2,1)} %param.12) | copy-start | bytes 4009012
  34.4 13.7 %all-to-all-start.2 = ((bf16[289,32,2]{0,2,1:T(2,128)(2,1)}), bf16[289,32,2]{0,2,1:T(2,128)(2,1)S(1)}, u32[]{:S(2)}, u32[]{:S(2)}) async-start(bf16[289,32,2]{0,2,1:T(2,128)(2,1)} %broadcast_in_dim.45), calls=%async_computation.2 | async-start | bytes 98304 | tf_op jit(solution)/shard_map/all_to_all | solution.py:92
  48.1 48.9 %all-to-all-start = ((bf16[289,64,16]{0,2,1:T(8,128)(2,1)}), bf16[289,64,16]{0,2,1:T(8,128)(2,1)S(1)}, u32[]{:S(2)}, u32[]{:S(2)}) async-start(bf16[289,64,16]{0,2,1:T(8,128)(2,1)} %broadcast_select_fusion), calls=%async_computation | async-start | bytes 1572864 | tf_op jit(solution)/shard_map/all_to_all | solution.py:114
  54.5 2.8 %copy-start.7 = (s32[8,64]{1,0:T(8,128)S(1)}, s32[8,64]{1,0:T(8,128)}, u32[]{:S(2)}) copy-start(s32[8,64]{1,0:T(8,128)} %param.17) | copy-start | bytes 6148
  68.6 3.4 %copy-start.4 = (s32[16,512]{1,0:T(8,128)S(1)}, s32[16,512]{1,0:T(8,128)}, u32[]{:S(2)}) copy-start(s32[16,512]{1,0:T(8,128)} %param.14) | copy-start | bytes 98308
  68.6 3.5 %copy-start.5 = (s32[16,512]{1,0:T(8,128)S(1)}, s32[16,512]{1,0:T(8,128)}, u32[]{:S(2)}) copy-start(s32[16,512]{1,0:T(8,128)} %param.15) | copy-start | bytes 98308
  73.0 3.3 %copy-start.8 = (s32[8,64]{1,0:T(8,128)S(1)}, s32[8,64]{1,0:T(8,128)}, u32[]{:S(2)}) copy-start(s32[8,64]{1,0:T(8,128)} %param.16) | copy-start | bytes 6148
  73.0 5.7 %copy-start.2 = (bf16[8,289,289]{2,0,1:T(8,128)(2,1)S(1)}, bf16[8,289,289]{2,0,1:T(8,128)(2,1)}, u32[]{:S(2)}) copy-start(bf16[8,289,289]{2,0,1:T(8,128)(2,1)} %gather_fusion.1) | copy-start | bytes 4009012
  80.8 2.5 %copy-start.1 = (bf16[8,289,289]{2,0,1:T(8,128)(2,1)S(1)}, bf16[8,289,289]{2,0,1:T(8,128)(2,1)}, u32[]{:S(2)}) copy-start(bf16[8,289,289]{2,0,1:T(8,128)(2,1)} %param.11) | copy-start | bytes 4009012

commit v13 on v12

--- a/solution.py
+++ b/solution.py
@@ -29,15 +29,17 @@
     return spread.reshape(8, coefs, count).transpose(1, 2, 0).reshape(coefs, 8 * count)
 
 
-def far_kernel(idx_ref, buf_ref, fs_ref, chain_ref, out_ref, table_ref, acc_ref):
+def far_kernel(idx_ref, own_ref, arr_ref, fs_ref, chain_ref, out_ref, table_ref, acc_ref):
     kinds = fs_ref.shape[0]
-    rows = buf_ref.shape[0]
+    own = own_ref.shape[0]
+    rows = own + arr_ref.shape[0]
     for k in range(kinds):
-        whole = jnp.dot(buf_ref[...], fs_ref[k], preferred_element_type=jnp.float32)
-        for j in range(CHUNKS):
-            table_ref[pl.ds(CHUNKS * k * rows + j, rows, stride=CHUNKS), :] = whole[
-                :, j * LANE : (j + 1) * LANE
-            ]
+        for src_ref, first in ((own_ref, 0), (arr_ref, own)):
+            whole = jnp.dot(src_ref[...], fs_ref[k], preferred_element_type=jnp.float32)
+            for j in range(CHUNKS):
+                table_ref[
+                    pl.ds(CHUNKS * (k * rows + first) + j, src_ref.shape[0], stride=CHUNKS), :
+                ] = whole[:, j * LANE : (j + 1) * LANE]
     targets = out_ref.shape[1]
     lists = idx_ref.shape[0] // targets
 
@@ -58,12 +60,14 @@
         out_ref[pl.ds(j * LANE, used), :] = (block[:used] + near).astype(out_ref.dtype)
 
 
-def far_field(buffer, far_shift, leaf_src, leaf_kind, chain_part):
-    coefs, rows = buffer.shape
+def far_field(own_cols, arrived_cols, far_shift, leaf_src, leaf_kind, chain_part):
+    coefs = own_cols.shape[0]
+    rows = own_cols.shape[1] + arrived_cols.shape[1]
     kinds = far_shift.shape[0]
     lists, targets = leaf_src.shape
     width = CHUNKS * LANE
-    buf_t = jnp.pad(buffer.T, ((0, 0), (0, width - coefs)))
+    own_t = jnp.pad(own_cols.T, ((0, 0), (0, width - coefs)))
+    arr_t = jnp.pad(arrived_cols.T, ((0, 0), (0, width - coefs)))
     fs_t = jnp.pad(far_shift.transpose(0, 2, 1), ((0, 0), (0, width - coefs), (0, width - coefs)))
     idx = (CHUNKS * (leaf_kind * rows + leaf_src)).T.reshape(lists * targets)
     out = pl.pallas_call(
@@ -74,13 +78,14 @@
             pl.BlockSpec(memory_space=pltpu.VMEM),
             pl.BlockSpec(memory_space=pltpu.VMEM),
             pl.BlockSpec(memory_space=pltpu.VMEM),
+            pl.BlockSpec(memory_space=pltpu.VMEM),
         ],
         out_specs=pl.BlockSpec(memory_space=pltpu.VMEM),
         scratch_shapes=[
             pltpu.VMEM((kinds * rows * CHUNKS, LANE), jnp.float32),
             pltpu.VMEM((targets * CHUNKS, LANE), jnp.float32),
         ],
-    )(idx, buf_t, fs_t, chain_part)
+    )(idx, own_t, arr_t, fs_t, chain_part)
     return out
 
 
@@ -137,8 +142,7 @@
     for level in range(LOCAL_LEVELS - 1):
         downward = lower_level(downward, down_shift).astype(jnp.bfloat16)
     chain_part = lower_level(downward, down_shift)
-    buffer = jnp.concatenate([multipoles, arrived], axis=1)
-    return far_field(buffer, far_shift, leaf_src, leaf_kind, chain_part)
+    return far_field(multipoles, arrived, far_shift, leaf_src, leaf_kind, chain_part)
 
 
 def solution(mesh):

time: 115 us -> 115 us (level)
  waiting for transfers between devices: 24.1 us -> 18.7 us
  matrix products: 7.79 us -> 9.99 us
  local copies, waits for them, and re-layouts: 33.7 us -> 35.2 us
  other arithmetic: 3.46 us -> 4.84 us
    all_to_all x1, waiting for transfers between devices: 10.6 us -> 5.33 us  [on_device(): lax.all_to_all(outgoing, ('gy', 'gz'), split_axis=1, concat_axis=1, tiled...]
    dot_general x3, matrix products: 1.4 us -> 3.71 us  [lower_level(): jnp.dot(down_shift.reshape(8 * coefs, coefs), parent, preferred_element_t...]
    select_n x2, other arithmetic: 1.72 us -> 3.22 us  [on_device(): jnp.take(far_shift, coarse_kinds, axis=0).transpose(1, 0, 2)]
    unnamed x23 -> x19, local copies, waits for them, and re-layouts: 8.46 us -> 8.42 us
  transfers between devices with their start and end apart: 3 -> 3, of which waited for: 3 -> 3; matrix products, arithmetic and copies ran while one was open for 32% -> 37% of each run, Pallas kernels for 0% -> 0%
where the time goes in v13:
time: 115 us; the launch traced here: 114 us
  local copies, waits for them, and re-layouts  35.2 us (31%)
  starting transfers between devices  29.1 us (25%)
  waiting for transfers between devices  18.7 us (16%)
  Pallas kernels  15.9 us (14%)
  matrix products  9.99 us (9%)
  other arithmetic  4.84 us (4%)
    all_to_all x2, starting transfers between devices, gather_columns(): return lax.all_to_all(spread, axes, split_axis=1, concat_axis=1, tiled=True)  22.7 us
    pallas_call x1, Pallas kernels, far_field(): pl.pallas_call(far_kernel, out_shape=jax.ShapeDtypeStruct((coefs, targets...  15.9 us
    all_to_all x2, waiting for transfers between devices, gather_columns(): return lax.all_to_all(spread, axes, split_axis=1, concat_axis=1, tiled=True)  13.4 us
    unnamed x19, local copies, waits for them, and re-layouts  8.42 us
    gather x1, local copies, waits for them, and re-layouts, on_device(): jnp.take(far_shift, coarse_kinds, axis=0).transpose(1, 0, 2)  6.83 us
    all_to_all x1, starting transfers between devices, on_device(): lax.all_to_all(outgoing, ('gy', 'gz'), split_axis=1, concat_axis=1, tiled...  6.35 us
    all_to_all x1, waiting for transfers between devices, on_device(): lax.all_to_all(outgoing, ('gy', 'gz'), split_axis=1, concat_axis=1, tiled...  5.33 us
    dot_general x4, matrix products, lift_level(): lax.dot_general(up_shift, child_stack, (((2,), (1,)), ((0,), (0,))), pref...  3.99 us
  transfers between devices with their start and end apart: 3, of which 3 were waited for; matrix products, arithmetic and copies ran while one was open for 37% of the time, Pallas kernels for 0%

profile of v13, /device:TPU:8, one launch (start us, length us, event | category | flops | bytes accessed | tf_op | source)
XLA Modules:
  0.0 114.0 jit_solution(9600611503226112420)
XLA Ops:
  0.0 0.0 copy-start.1
  0.0 1.3 %copy.33 = bf16[289,512]{0,1:T(8,128)(2,1)S(1)} copy(bf16[289,512]{1,0:T(8,128)(2,1)} %param.9) | data formatting | bytes 591872 | tf_op args[0]
  1.3 2.2 %fusion.19 = bf16[289,8,8]{0,2,1:T(8,128)(2,1)S(1)} fusion(bf16[8,289,289]{2,0,1:T(8,128)(2,1)} %param.10, bf16[8,289,64]{1,0,2:T(8,128)(2,1)S(1)} %bitcast.96), kind=kOutput, calls=%fused_computation.21 | convolution fusion | flops 85544000 | bytes 1669264 | tf_op jit(solution)/shard_map/dot_general | solution.py:17
  3.5 0.0 copy-done.1
  3.5 0.0 copy-start.4
  3.6 0.6 fusion.28
  4.1 0.6 fusion.37
  4.8 0.6 reshape.141
  5.4 15.2 %all-to-all-start.1 = ((bf16[289,16,1]{0,2,1:T(2,128)(2,1)}), bf16[289,16,1]{0,2,1:T(2,128)(2,1)S(1)}, u32[]{:S(2)}, u32[]{:S(2)}) async-start(bf16[289,16,1]{0,2,1:T(2,128)(2,1)} %reshape.141), calls=%async_computation.1 | async-start | bytes 49152 | tf_op jit(solution)/shard_map/all_to_all | solution.py:97
  20.6 0.0 copy-done.4
  20.6 0.1 copy.35
  20.7 0.1 reshape.138
  20.8 3.9 %gather_fusion = bf16[1024,289]{1,0:T(8,128)(2,1)S(1)} fusion(bf16[289,512]{0,1:T(8,128)(2,1)S(1)} %copy.33, s32[1024]{0:T(1024)S(1)} %broadcast_clamp_fusion), kind=kCustom, calls=%fused_computation | custom fusion | bytes 1187840 | tf_op jit(solution)/shard_map/jit(_take)/gather | solution.py:118
  24.7 0.1 copy.34
  24.8 8.3 %all-to-all-done.1 = bf16[289,16,1]{0,2,1:T(2,128)(2,1)S(1)} async-done(((bf16[289,16,1]{0,2,1:T(2,128)(2,1)}), bf16[289,16,1]{0,2,1:T(2,128)(2,1)S(1)}, u32[]{:S(2)}, u32[]{:S(2)}) %all-to-all-start.1) | async-done | bytes 9280 | tf_op jit(solution)/shard_map/all_to_all | solution.py:97
  33.2 0.6 fusion.43
  33.7 0.0 copy-start
  33.8 0.7 broadcast_in_dim.45
  34.4 7.5 %all-to-all-start.2 = ((bf16[289,32,2]{0,2,1:T(2,128)(2,1)}), bf16[289,32,2]{0,2,1:T(2,128)(2,1)S(1)}, u32[]{:S(2)}, u32[]{:S(2)}) async-start(bf16[289,32,2]{0,2,1:T(2,128)(2,1)} %broadcast_in_dim.45), calls=%async_computation.2 | async-start | bytes 98304 | tf_op jit(solution)/shard_map/all_to_all | solution.py:97
  42.0 1.1 broadcast_select_fusion
  43.1 5.1 %all-to-all-done.2 = bf16[289,32,2]{0,2,1:T(2,128)(2,1)S(1)} async-done(((bf16[289,32,2]{0,2,1:T(2,128)(2,1)}), bf16[289,32,2]{0,2,1:T(2,128)(2,1)S(1)}, u32[]{:S(2)}, u32[]{:S(2)}) %all-to-all-start.2) | async-done | bytes 37024 | tf_op jit(solution)/shard_map/all_to_all | solution.py:97
  48.1 6.3 %all-to-all-start = ((bf16[289,64,16]{0,2,1:T(8,128)(2,1)}), bf16[289,64,16]{0,2,1:T(8,128)(2,1)S(1)}, u32[]{:S(2)}, u32[]{:S(2)}) async-start(bf16[289,64,16]{0,2,1:T(8,128)(2,1)} %broadcast_select_fusion), calls=%async_computation | async-start | bytes 1572864 | tf_op jit(solution)/shard_map/all_to_all | solution.py:119
  54.5 0.0 copy-done
  54.5 0.0 copy-start.5
  54.6 2.8 %copy.37 = bf16[8,289,289]{1,2,0:T(8,128)(2,1)} copy(bf16[8,289,289]{2,0,1:T(8,128)(2,1)S(1)} %copy-done) | data formatting | bytes 2672672 | tf_op args[3]
  57.3 0.0 copy-done.5
  57.3 0.2 fusion.56
  57.5 6.8 %gather_fusion.1 = bf16[8,289,289]{2,0,1:T(8,128)(2,1)} fusion(bf16[8,289,289]{2,0,1:T(8,128)(2,1)S(1)} %copy-done, s32[1024]{0:T(1024)S(1)} %pad_clamp_fusion.1), kind=kCustom, calls=%fused_computation.1 | custom fusion | bytes 2672704 | tf_op jit(solution)/shard_map/jit(_take)/gather | solution.py:131
  64.3 4.2 %copy.46 = bf16[8,289,289]{1,0,2:T(8,128)(2,1)} copy(bf16[8,289,289]{2,0,1:T(8,128)(2,1)} %param.11) | data formatting | bytes 2672672 | tf_op args[2]
  68.6 3.4 %reshape.143 = bf16[2312,289]{0,1:T(8,128)(2,1)S(1)} reshape(bf16[8,289,289]{1,0,2:T(8,128)(2,1)} %copy.46) | data formatting | bytes 2672672 | tf_op jit(solution)/shard_map/reshape | solution.py:27
  72.0 0.8 pad.12.own_ref
  72.8 0.0 copy-start.2
  72.8 0.0 copy-start.3
  72.8 0.0 copy-start.6
  72.8 3.2 %pad.14.fs_ref = bf16[8,384,384]{2,1,0:T(8,128)(2,1)} pad(bf16[8,289,289]{2,1,0:T(8,128)(2,1)} %bitcast.98, bf16[]{:T(256)} %constant.75.clone.1), padding=0_0x0_95x0_95 | pad | bytes 3695634 | tf_op jit(solution)/shard_map/jit(_pad)/pad | solution.py:71
  76.0 0.0 copy-done.2
  76.0 0.0 copy-done.3
  76.0 0.1 copy.32
  76.1 0.7 reshape.136.idx_ref
  76.9 0.0 copy-done.6
  76.9 0.2 fusion.57
  77.1 0.2 and_reduce_fusion
  77.3 1.9 %constant_dynamic-slice_fusion = bf16[1,289,289]{2,0,1:T(2,128)(2,1)S(1)} fusion(bf16[8,289,289]{2,0,1:T(8,128)(2,1)} %param.11, s32[]{:T(128)S(6)} %select_n.73), kind=kLoop, calls=%fused_computation.58 | loop fusion | bytes 334088 | tf_op jit(solution)/shard_map/dynamic_slice | solution.py:139
  79.3 3.0 %select_bitcast_fusion = bf16[289,8,289]{2,1,0:T(8,128)(2,1)} fusion(bf16[8,289,289]{2,0,1:T(8,128)(2,1)} %gather_fusion.1, pred[8]{0:T(512)(128)(4,1)S(1)} %get-tuple-element.6), kind=kLoop, calls=%fused_computation.10 | loop fusion | flops 668168 | bytes 2672680 | tf_op jit(solution)/shard_map/jit(_take)/select_n | solution.py:131
  82.3 0.6 gather_fusion.2
  82.9 0.1 select_bitcast_fusion.1
  83.0 2.1 %fusion.40 = bf16[289]{0:T(512)(128)(2,1)S(1)} fusion(bf16[289,8,289]{2,1,0:T(8,128)(2,1)} %select_bitcast_fusion, bf16[8,289,1]{1,0,2:T(8,128)(2,1)S(1)} %select_bitcast_fusion.1), kind=kOutput, calls=%fused_computation.28 | convolution fusion | flops 1336336 | bytes 1341538 | tf_op jit(solution)/shard_map/dot_general | solution.py:136
  85.1 0.2 convolution_reduce_fusion
  85.3 2.2 %fusion.1 = bf16[1,8,289]{2,0,1:T(2,128)(2,1)S(1)} fusion(bf16[289,1,1]{0,1,2:T(2,128)(2,1)S(1)} %reshape.179, bf16[8,289,289]{2,0,1:T(8,128)(2,1)} %param.11), kind=kOutput, calls=%fused_computation.6 | convolution fusion | flops 1336336 | bytes 1341538 | tf_op jit(solution)/shard_map/dot_general | solution.py:26
  87.5 0.3 fusion
  87.8 0.1 convert_element_type.74
  88.0 1.2 %convolution_bitcast_fusion = f32[2312,64]{0,1:T(8,128)} fusion(bf16[2312,289]{0,1:T(8,128)(2,1)S(1)} %reshape.143, bf16[8,289,8]{1,0,2:T(8,128)(2,1)S(1)} %convert_element_type.74), kind=kOutput, calls=%fused_computation.3 | convolution fusion | flops 85525504 | bytes 1965200 | tf_op jit(solution)/shard_map/dot_general | solution.py:26
  89.2 1.5 %reshape.144 = f32[8,289,64]{1,0,2:T(8,128)S(1)} reshape(f32[2312,64]{0,1:T(8,128)} %convolution_bitcast_fusion) | data formatting | bytes 1183744 | tf_op jit(solution)/shard_map/reshape | solution.py:29
  90.7 1.1 copy.47.chain_ref
  91.7 5.3 %all-to-all-done = bf16[289,64,16]{0,2,1:T(8,128)(2,1)S(1)} async-done(((bf16[289,64,16]{0,2,1:T(8,128)(2,1)}), bf16[289,64,16]{0,2,1:T(8,128)(2,1)S(1)}, u32[]{:S(2)}, u32[]{:S(2)}) %all-to-all-start) | async-done | bytes 591904 | tf_op jit(solution)/shard_map/all_to_all | solution.py:119
  97.1 1.0 pad.13.arr_ref
  98.1 15.9 %shard_map.91 = bf16[289,512]{1,0:T(8,128)(2,1)} custom-call(s32[8192]{0:T(1024)} %reshape.136.idx_ref, bf16[512,384]{1,0:T(8,128)(2,1)} %pad.12.own_ref, bf16[1024,384]{1,0:T(8,128)(2,1)} %pad.13.arr_ref, bf16[8,384,384]{2,1,0:T(8,128)(2,1)} %pad.14.fs_ref, f32[289,512]{1,0:T(8,128)} %copy.47.chain_ref), custom_call_target="tpu_custom_call" | custom-call | tf_op jit(solution)/shard_map/pallas_call | solution.py:73
  (10 shorter events, 0.1 us)
Async XLA Ops:
  0.0 3.5 %copy-start.1 = (bf16[8,289,289]{2,0,1:T(8,128)(2,1)S(1)}, bf16[8,289,289]{2,0,1:T(8,128)(2,1)}, u32[]{:S(2)}) copy-start(bf16[8,289,289]{2,0,1:T(8,128)(2,1)} %param.10) | copy-start | bytes 4009012
  3.5 17.0 %copy-start.4 = (s32[1,1,64,16]{2,3,1,0:T(8,128)S(1)}, s32[1,1,64,16]{2,3,1,0:T(8,128)}, u32[]{:S(2)}) copy-start(s32[1,1,64,16]{2,3,1,0:T(8,128)} %param.13) | copy-start | bytes 12292
  5.4 27.8 %all-to-all-start.1 = ((bf16[289,16,1]{0,2,1:T(2,128)(2,1)}), bf16[289,16,1]{0,2,1:T(2,128)(2,1)S(1)}, u32[]{:S(2)}, u32[]{:S(2)}) async-start(bf16[289,16,1]{0,2,1:T(2,128)(2,1)} %reshape.141), calls=%async_computation.1 | async-start | bytes 49152 | tf_op jit(solution)/shard_map/all_to_all | solution.py:97
  33.7 20.8 %copy-start = (bf16[8,289,289]{2,0,1:T(8,128)(2,1)S(1)}, bf16[8,289,289]{2,0,1:T(8,128)(2,1)}, u32[]{:S(2)}) copy-start(bf16[8,289,289]{2,0,1:T(8,128)(2,1)} %param.12) | copy-start | bytes 4009012
  34.4 13.7 %all-to-all-start.2 = ((bf16[289,32,2]{0,2,1:T(2,128)(2,1)}), bf16[289,32,2]{0,2,1:T(2,128)(2,1)S(1)}, u32[]{:S(2)}, u32[]{:S(2)}) async-start(bf16[289,32,2]{0,2,1:T(2,128)(2,1)} %broadcast_in_dim.45), calls=%async_computation.2 | async-start | bytes 98304 | tf_op jit(solution)/shard_map/all_to_all | solution.py:97
  48.1 48.9 %all-to-all-start = ((bf16[289,64,16]{0,2,1:T(8,128)(2,1)}), bf16[289,64,16]{0,2,1:T(8,128)(2,1)S(1)}, u32[]{:S(2)}, u32[]{:S(2)}) async-start(bf16[289,64,16]{0,2,1:T(8,128)(2,1)} %broadcast_select_fusion), calls=%async_computation | async-start | bytes 1572864 | tf_op jit(solution)/shard_map/all_to_all | solution.py:119
  54.5 2.8 %copy-start.5 = (s32[8,64]{1,0:T(8,128)S(1)}, s32[8,64]{1,0:T(8,128)}, u32[]{:S(2)}) copy-start(s32[8,64]{1,0:T(8,128)} %param.17) | copy-start | bytes 6148
  72.8 3.2 %copy-start.2 = (s32[16,512]{1,0:T(8,128)S(1)}, s32[16,512]{1,0:T(8,128)}, u32[]{:S(2)}) copy-start(s32[16,512]{1,0:T(8,128)} %param.14) | copy-start | bytes 98308
  72.8 3.2 %copy-start.3 = (s32[16,512]{1,0:T(8,128)S(1)}, s32[16,512]{1,0:T(8,128)}, u32[]{:S(2)}) copy-start(s32[16,512]{1,0:T(8,128)} %param.15) | copy-start | bytes 98308
  72.8 4.1 %copy-start.6 = (s32[8,64]{1,0:T(8,128)S(1)}, s32[8,64]{1,0:T(8,128)}, u32[]{:S(2)}) copy-start(s32[8,64]{1,0:T(8,128)} %param.16) | copy-start | bytes 6148

commit v14 on v13

--- a/solution.py
+++ b/solution.py
@@ -51,7 +51,7 @@
         acc_ref[pl.ds(t * CHUNKS, CHUNKS), :] = acc
         return carry
 
-    lax.fori_loop(0, targets, body, 0, unroll=8)
+    lax.fori_loop(0, targets, body, 0, unroll=16)
     coefs = out_ref.shape[0]
     for j in range(CHUNKS):
         block = acc_ref[pl.ds(j, targets, stride=CHUNKS), :].T

time: 115 us -> 114 us (level)
  no operation moved by 1% of the time
where the time goes in v14:
time: 114 us
  local copies, waits for them, and re-layouts  35.2 us (31%)
  starting transfers between devices  29.1 us (26%)
  waiting for transfers between devices  18.7 us (16%)
  Pallas kernels  15.7 us (14%)
  matrix products  9.99 us (9%)
  other arithmetic  4.84 us (4%)
    all_to_all x2, starting transfers between devices, gather_columns(): return lax.all_to_all(spread, axes, split_axis=1, concat_axis=1, tiled=True)  22.7 us
    pallas_call x1, Pallas kernels, far_field(): pl.pallas_call(far_kernel, out_shape=jax.ShapeDtypeStruct((coefs, targets...  15.7 us
    all_to_all x2, waiting for transfers between devices, gather_columns(): return lax.all_to_all(spread, axes, split_axis=1, concat_axis=1, tiled=True)  13.4 us
    unnamed x19, local copies, waits for them, and re-layouts  8.42 us
    gather x1, local copies, waits for them, and re-layouts, on_device(): jnp.take(far_shift, coarse_kinds, axis=0).transpose(1, 0, 2)  6.83 us
    all_to_all x1, starting transfers between devices, on_device(): lax.all_to_all(outgoing, ('gy', 'gz'), split_axis=1, concat_axis=1, tiled...  6.35 us
    all_to_all x1, waiting for transfers between devices, on_device(): lax.all_to_all(outgoing, ('gy', 'gz'), split_axis=1, concat_axis=1, tiled...  5.33 us
    dot_general x4, matrix products, lift_level(): lax.dot_general(up_shift, child_stack, (((2,), (1,)), ((0,), (0,))), pref...  3.99 us
  transfers between devices with their start and end apart: 3, of which 3 were waited for; matrix products, arithmetic and copies ran while one was open for 37% of the time, Pallas kernels for 0%

profile of v14, /device:TPU:8, one launch (start us, length us, event | category | flops | bytes accessed | tf_op | source)
XLA Modules:
  0.0 113.7 jit_solution(17102636378776766440)
XLA Ops:
  0.0 0.0 copy-start.1
  0.0 1.3 %copy.33 = bf16[289,512]{0,1:T(8,128)(2,1)S(1)} copy(bf16[289,512]{1,0:T(8,128)(2,1)} %param.9) | data formatting | bytes 591872 | tf_op args[0]
  1.3 2.2 %fusion.19 = bf16[289,8,8]{0,2,1:T(8,128)(2,1)S(1)} fusion(bf16[8,289,289]{2,0,1:T(8,128)(2,1)} %param.10, bf16[8,289,64]{1,0,2:T(8,128)(2,1)S(1)} %bitcast.96), kind=kOutput, calls=%fused_computation.21 | convolution fusion | flops 85544000 | bytes 1669264 | tf_op jit(solution)/shard_map/dot_general | solution.py:17
  3.5 0.0 copy-done.1
  3.5 0.0 copy-start.4
  3.6 0.6 fusion.28
  4.1 0.6 fusion.37
  4.8 0.6 reshape.141
  5.4 15.2 %all-to-all-start.1 = ((bf16[289,16,1]{0,2,1:T(2,128)(2,1)}), bf16[289,16,1]{0,2,1:T(2,128)(2,1)S(1)}, u32[]{:S(2)}, u32[]{:S(2)}) async-start(bf16[289,16,1]{0,2,1:T(2,128)(2,1)} %reshape.141), calls=%async_computation.1 | async-start | bytes 49152 | tf_op jit(solution)/shard_map/all_to_all | solution.py:97
  20.6 0.0 copy-done.4
  20.6 0.1 copy.35
  20.7 0.1 reshape.138
  20.8 3.9 %gather_fusion = bf16[1024,289]{1,0:T(8,128)(2,1)S(1)} fusion(bf16[289,512]{0,1:T(8,128)(2,1)S(1)} %copy.33, s32[1024]{0:T(1024)S(1)} %broadcast_clamp_fusion), kind=kCustom, calls=%fused_computation | custom fusion | bytes 1187840 | tf_op jit(solution)/shard_map/jit(_take)/gather | solution.py:118
  24.7 0.1 copy.34
  24.8 8.3 %all-to-all-done.1 = bf16[289,16,1]{0,2,1:T(2,128)(2,1)S(1)} async-done(((bf16[289,16,1]{0,2,1:T(2,128)(2,1)}), bf16[289,16,1]{0,2,1:T(2,128)(2,1)S(1)}, u32[]{:S(2)}, u32[]{:S(2)}) %all-to-all-start.1) | async-done | bytes 9280 | tf_op jit(solution)/shard_map/all_to_all | solution.py:97
  33.2 0.6 fusion.43
  33.7 0.0 copy-start
  33.8 0.7 broadcast_in_dim.45
  34.4 7.5 %all-to-all-start.2 = ((bf16[289,32,2]{0,2,1:T(2,128)(2,1)}), bf16[289,32,2]{0,2,1:T(2,128)(2,1)S(1)}, u32[]{:S(2)}, u32[]{:S(2)}) async-start(bf16[289,32,2]{0,2,1:T(2,128)(2,1)} %broadcast_in_dim.45), calls=%async_computation.2 | async-start | bytes 98304 | tf_op jit(solution)/shard_map/all_to_all | solution.py:97
  42.0 1.1 broadcast_select_fusion
  43.1 5.1 %all-to-all-done.2 = bf16[289,32,2]{0,2,1:T(2,128)(2,1)S(1)} async-done(((bf16[289,32,2]{0,2,1:T(2,128)(2,1)}), bf16[289,32,2]{0,2,1:T(2,128)(2,1)S(1)}, u32[]{:S(2)}, u32[]{:S(2)}) %all-to-all-start.2) | async-done | bytes 37024 | tf_op jit(solution)/shard_map/all_to_all | solution.py:97
  48.1 6.3 %all-to-all-start = ((bf16[289,64,16]{0,2,1:T(8,128)(2,1)}), bf16[289,64,16]{0,2,1:T(8,128)(2,1)S(1)}, u32[]{:S(2)}, u32[]{:S(2)}) async-start(bf16[289,64,16]{0,2,1:T(8,128)(2,1)} %broadcast_select_fusion), calls=%async_computation | async-start | bytes 1572864 | tf_op jit(solution)/shard_map/all_to_all | solution.py:119
  54.5 0.0 copy-done
  54.5 0.0 copy-start.5
  54.6 2.8 %copy.37 = bf16[8,289,289]{1,2,0:T(8,128)(2,1)} copy(bf16[8,289,289]{2,0,1:T(8,128)(2,1)S(1)} %copy-done) | data formatting | bytes 2672672 | tf_op args[3]
  57.3 0.0 copy-done.5
  57.3 0.2 fusion.56
  57.5 6.8 %gather_fusion.1 = bf16[8,289,289]{2,0,1:T(8,128)(2,1)} fusion(bf16[8,289,289]{2,0,1:T(8,128)(2,1)S(1)} %copy-done, s32[1024]{0:T(1024)S(1)} %pad_clamp_fusion.1), kind=kCustom, calls=%fused_computation.1 | custom fusion | bytes 2672704 | tf_op jit(solution)/shard_map/jit(_take)/gather | solution.py:131
  64.3 4.2 %copy.46 = bf16[8,289,289]{1,0,2:T(8,128)(2,1)} copy(bf16[8,289,289]{2,0,1:T(8,128)(2,1)} %param.11) | data formatting | bytes 2672672 | tf_op args[2]
  68.6 3.4 %reshape.143 = bf16[2312,289]{0,1:T(8,128)(2,1)S(1)} reshape(bf16[8,289,289]{1,0,2:T(8,128)(2,1)} %copy.46) | data formatting | bytes 2672672 | tf_op jit(solution)/shard_map/reshape | solution.py:27
  72.0 0.8 pad.12.own_ref
  72.8 0.0 copy-start.2
  72.8 0.0 copy-start.3
  72.8 0.0 copy-start.6
  72.8 3.2 %pad.14.fs_ref = bf16[8,384,384]{2,1,0:T(8,128)(2,1)} pad(bf16[8,289,289]{2,1,0:T(8,128)(2,1)} %bitcast.98, bf16[]{:T(256)} %constant.75.clone.1), padding=0_0x0_95x0_95 | pad | bytes 3695634 | tf_op jit(solution)/shard_map/jit(_pad)/pad | solution.py:71
  76.0 0.0 copy-done.2
  76.0 0.0 copy-done.3
  76.0 0.1 copy.32
  76.1 0.7 reshape.136.idx_ref
  76.9 0.0 copy-done.6
  76.9 0.2 fusion.57
  77.1 0.2 and_reduce_fusion
  77.3 1.9 %constant_dynamic-slice_fusion = bf16[1,289,289]{2,0,1:T(2,128)(2,1)S(1)} fusion(bf16[8,289,289]{2,0,1:T(8,128)(2,1)} %param.11, s32[]{:T(128)S(6)} %select_n.73), kind=kLoop, calls=%fused_computation.58 | loop fusion | bytes 334088 | tf_op jit(solution)/shard_map/dynamic_slice | solution.py:139
  79.3 3.0 %select_bitcast_fusion = bf16[289,8,289]{2,1,0:T(8,128)(2,1)} fusion(bf16[8,289,289]{2,0,1:T(8,128)(2,1)} %gather_fusion.1, pred[8]{0:T(512)(128)(4,1)S(1)} %get-tuple-element.6), kind=kLoop, calls=%fused_computation.10 | loop fusion | flops 668168 | bytes 2672680 | tf_op jit(solution)/shard_map/jit(_take)/select_n | solution.py:131
  82.3 0.6 gather_fusion.2
  82.9 0.1 select_bitcast_fusion.1
  83.0 2.1 %fusion.40 = bf16[289]{0:T(512)(128)(2,1)S(1)} fusion(bf16[289,8,289]{2,1,0:T(8,128)(2,1)} %select_bitcast_fusion, bf16[8,289,1]{1,0,2:T(8,128)(2,1)S(1)} %select_bitcast_fusion.1), kind=kOutput, calls=%fused_computation.28 | convolution fusion | flops 1336336 | bytes 1341538 | tf_op jit(solution)/shard_map/dot_general | solution.py:136
  85.1 0.2 convolution_reduce_fusion
  85.3 2.2 %fusion.1 = bf16[1,8,289]{2,0,1:T(2,128)(2,1)S(1)} fusion(bf16[289,1,1]{0,1,2:T(2,128)(2,1)S(1)} %reshape.179, bf16[8,289,289]{2,0,1:T(8,128)(2,1)} %param.11), kind=kOutput, calls=%fused_computation.6 | convolution fusion | flops 1336336 | bytes 1341538 | tf_op jit(solution)/shard_map/dot_general | solution.py:26
  87.5 0.3 fusion
  87.8 0.1 convert_element_type.74
  88.0 1.2 %convolution_bitcast_fusion = f32[2312,64]{0,1:T(8,128)} fusion(bf16[2312,289]{0,1:T(8,128)(2,1)S(1)} %reshape.143, bf16[8,289,8]{1,0,2:T(8,128)(2,1)S(1)} %convert_element_type.74), kind=kOutput, calls=%fused_computation.3 | convolution fusion | flops 85525504 | bytes 1965200 | tf_op jit(solution)/shard_map/dot_general | solution.py:26
  89.2 1.5 %reshape.144 = f32[8,289,64]{1,0,2:T(8,128)S(1)} reshape(f32[2312,64]{0,1:T(8,128)} %convolution_bitcast_fusion) | data formatting | bytes 1183744 | tf_op jit(solution)/shard_map/reshape | solution.py:29
  90.7 1.1 copy.47.chain_ref
  91.7 5.3 %all-to-all-done = bf16[289,64,16]{0,2,1:T(8,128)(2,1)S(1)} async-done(((bf16[289,64,16]{0,2,1:T(8,128)(2,1)}), bf16[289,64,16]{0,2,1:T(8,128)(2,1)S(1)}, u32[]{:S(2)}, u32[]{:S(2)}) %all-to-all-start) | async-done | bytes 591904 | tf_op jit(solution)/shard_map/all_to_all | solution.py:119
  97.1 1.0 pad.13.arr_ref
  98.1 15.7 %shard_map.91 = bf16[289,512]{1,0:T(8,128)(2,1)} custom-call(s32[8192]{0:T(1024)} %reshape.136.idx_ref, bf16[512,384]{1,0:T(8,128)(2,1)} %pad.12.own_ref, bf16[1024,384]{1,0:T(8,128)(2,1)} %pad.13.arr_ref, bf16[8,384,384]{2,1,0:T(8,128)(2,1)} %pad.14.fs_ref, f32[289,512]{1,0:T(8,128)} %copy.47.chain_ref), custom_call_target="tpu_custom_call" | custom-call | tf_op jit(solution)/shard_map/pallas_call | solution.py:73
  (10 shorter events, 0.1 us)
Async XLA Ops:
  0.0 3.5 %copy-start.1 = (bf16[8,289,289]{2,0,1:T(8,128)(2,1)S(1)}, bf16[8,289,289]{2,0,1:T(8,128)(2,1)}, u32[]{:S(2)}) copy-start(bf16[8,289,289]{2,0,1:T(8,128)(2,1)} %param.10) | copy-start | bytes 4009012
  3.5 17.0 %copy-start.4 = (s32[1,1,64,16]{2,3,1,0:T(8,128)S(1)}, s32[1,1,64,16]{2,3,1,0:T(8,128)}, u32[]{:S(2)}) copy-start(s32[1,1,64,16]{2,3,1,0:T(8,128)} %param.13) | copy-start | bytes 12292
  5.4 27.8 %all-to-all-start.1 = ((bf16[289,16,1]{0,2,1:T(2,128)(2,1)}), bf16[289,16,1]{0,2,1:T(2,128)(2,1)S(1)}, u32[]{:S(2)}, u32[]{:S(2)}) async-start(bf16[289,16,1]{0,2,1:T(2,128)(2,1)} %reshape.141), calls=%async_computation.1 | async-start | bytes 49152 | tf_op jit(solution)/shard_map/all_to_all | solution.py:97
  33.7 20.8 %copy-start = (bf16[8,289,289]{2,0,1:T(8,128)(2,1)S(1)}, bf16[8,289,289]{2,0,1:T(8,128)(2,1)}, u32[]{:S(2)}) copy-start(bf16[8,289,289]{2,0,1:T(8,128)(2,1)} %param.12) | copy-start | bytes 4009012
  34.4 13.7 %all-to-all-start.2 = ((bf16[289,32,2]{0,2,1:T(2,128)(2,1)}), bf16[289,32,2]{0,2,1:T(2,128)(2,1)S(1)}, u32[]{:S(2)}, u32[]{:S(2)}) async-start(bf16[289,32,2]{0,2,1:T(2,128)(2,1)} %broadcast_in_dim.45), calls=%async_computation.2 | async-start | bytes 98304 | tf_op jit(solution)/shard_map/all_to_all | solution.py:97
  48.1 48.9 %all-to-all-start = ((bf16[289,64,16]{0,2,1:T(8,128)(2,1)}), bf16[289,64,16]{0,2,1:T(8,128)(2,1)S(1)}, u32[]{:S(2)}, u32[]{:S(2)}) async-start(bf16[289,64,16]{0,2,1:T(8,128)(2,1)} %broadcast_select_fusion), calls=%async_computation | async-start | bytes 1572864 | tf_op jit(solution)/shard_map/all_to_all | solution.py:119
  54.5 2.8 %copy-start.5 = (s32[8,64]{1,0:T(8,128)S(1)}, s32[8,64]{1,0:T(8,128)}, u32[]{:S(2)}) copy-start(s32[8,64]{1,0:T(8,128)} %param.17) | copy-start | bytes 6148
  72.8 3.2 %copy-start.2 = (s32[16,512]{1,0:T(8,128)S(1)}, s32[16,512]{1,0:T(8,128)}, u32[]{:S(2)}) copy-start(s32[16,512]{1,0:T(8,128)} %param.14) | copy-start | bytes 98308
  72.8 3.2 %copy-start.3 = (s32[16,512]{1,0:T(8,128)S(1)}, s32[16,512]{1,0:T(8,128)}, u32[]{:S(2)}) copy-start(s32[16,512]{1,0:T(8,128)} %param.15) | copy-start | bytes 98308
  72.8 4.1 %copy-start.6 = (s32[8,64]{1,0:T(8,128)S(1)}, s32[8,64]{1,0:T(8,128)}, u32[]{:S(2)}) copy-start(s32[8,64]{1,0:T(8,128)} %param.16) | copy-start | bytes 6148

commit v15 on v14

--- a/solution.py
+++ b/solution.py
@@ -51,7 +51,7 @@
         acc_ref[pl.ds(t * CHUNKS, CHUNKS), :] = acc
         return carry
 
-    lax.fori_loop(0, targets, body, 0, unroll=16)
+    lax.fori_loop(0, targets, body, 0, unroll=32)
     coefs = out_ref.shape[0]
     for j in range(CHUNKS):
         block = acc_ref[pl.ds(j, targets, stride=CHUNKS), :].T

time: 114 us -> 114 us (level)
  no operation moved by 1% of the time
where the time goes in v15:
time: 114 us
  local copies, waits for them, and re-layouts  35.2 us (31%)
  starting transfers between devices  29.1 us (26%)
  waiting for transfers between devices  18.7 us (16%)
  Pallas kernels  15.6 us (14%)
  matrix products  9.99 us (9%)
  other arithmetic  4.84 us (4%)
    all_to_all x2, starting transfers between devices, gather_columns(): return lax.all_to_all(spread, axes, split_axis=1, concat_axis=1, tiled=True)  22.7 us
    pallas_call x1, Pallas kernels, far_field(): pl.pallas_call(far_kernel, out_shape=jax.ShapeDtypeStruct((coefs, targets...  15.6 us
    all_to_all x2, waiting for transfers between devices, gather_columns(): return lax.all_to_all(spread, axes, split_axis=1, concat_axis=1, tiled=True)  13.4 us
    unnamed x19, local copies, waits for them, and re-layouts  8.42 us
    gather x1, local copies, waits for them, and re-layouts, on_device(): jnp.take(far_shift, coarse_kinds, axis=0).transpose(1, 0, 2)  6.83 us
    all_to_all x1, starting transfers between devices, on_device(): lax.all_to_all(outgoing, ('gy', 'gz'), split_axis=1, concat_axis=1, tiled...  6.35 us
    all_to_all x1, waiting for transfers between devices, on_device(): lax.all_to_all(outgoing, ('gy', 'gz'), split_axis=1, concat_axis=1, tiled...  5.33 us
    dot_general x4, matrix products, lift_level(): lax.dot_general(up_shift, child_stack, (((2,), (1,)), ((0,), (0,))), pref...  3.99 us
  transfers between devices with their start and end apart: 3, of which 3 were waited for; matrix products, arithmetic and copies ran while one was open for 37% of the time, Pallas kernels for 0%

profile of v15, /device:TPU:8, one launch (start us, length us, event | category | flops | bytes accessed | tf_op | source)
XLA Modules:
  0.0 113.6 jit_solution(9727446782574550773)
XLA Ops:
  0.0 0.0 copy-start.1
  0.0 1.3 %copy.33 = bf16[289,512]{0,1:T(8,128)(2,1)S(1)} copy(bf16[289,512]{1,0:T(8,128)(2,1)} %param.9) | data formatting | bytes 591872 | tf_op args[0]
  1.3 2.2 %fusion.19 = bf16[289,8,8]{0,2,1:T(8,128)(2,1)S(1)} fusion(bf16[8,289,289]{2,0,1:T(8,128)(2,1)} %param.10, bf16[8,289,64]{1,0,2:T(8,128)(2,1)S(1)} %bitcast.96), kind=kOutput, calls=%fused_computation.21 | convolution fusion | flops 85544000 | bytes 1669264 | tf_op jit(solution)/shard_map/dot_general | solution.py:17
  3.5 0.0 copy-done.1
  3.5 0.0 copy-start.4
  3.6 0.6 fusion.28
  4.1 0.6 fusion.37
  4.8 0.6 reshape.141
  5.4 15.2 %all-to-all-start.1 = ((bf16[289,16,1]{0,2,1:T(2,128)(2,1)}), bf16[289,16,1]{0,2,1:T(2,128)(2,1)S(1)}, u32[]{:S(2)}, u32[]{:S(2)}) async-start(bf16[289,16,1]{0,2,1:T(2,128)(2,1)} %reshape.141), calls=%async_computation.1 | async-start | bytes 49152 | tf_op jit(solution)/shard_map/all_to_all | solution.py:97
  20.6 0.0 copy-done.4
  20.6 0.1 copy.35
  20.7 0.1 reshape.138
  20.8 3.9 %gather_fusion = bf16[1024,289]{1,0:T(8,128)(2,1)S(1)} fusion(bf16[289,512]{0,1:T(8,128)(2,1)S(1)} %copy.33, s32[1024]{0:T(1024)S(1)} %broadcast_clamp_fusion), kind=kCustom, calls=%fused_computation | custom fusion | bytes 1187840 | tf_op jit(solution)/shard_map/jit(_take)/gather | solution.py:118
  24.7 0.1 copy.34
  24.8 8.3 %all-to-all-done.1 = bf16[289,16,1]{0,2,1:T(2,128)(2,1)S(1)} async-done(((bf16[289,16,1]{0,2,1:T(2,128)(2,1)}), bf16[289,16,1]{0,2,1:T(2,128)(2,1)S(1)}, u32[]{:S(2)}, u32[]{:S(2)}) %all-to-all-start.1) | async-done | bytes 9280 | tf_op jit(solution)/shard_map/all_to_all | solution.py:97
  33.2 0.6 fusion.43
  33.7 0.0 copy-start
  33.8 0.7 broadcast_in_dim.45
  34.4 7.5 %all-to-all-start.2 = ((bf16[289,32,2]{0,2,1:T(2,128)(2,1)}), bf16[289,32,2]{0,2,1:T(2,128)(2,1)S(1)}, u32[]{:S(2)}, u32[]{:S(2)}) async-start(bf16[289,32,2]{0,2,1:T(2,128)(2,1)} %broadcast_in_dim.45), calls=%async_computation.2 | async-start | bytes 98304 | tf_op jit(solution)/shard_map/all_to_all | solution.py:97
  42.0 1.1 broadcast_select_fusion
  43.1 5.1 %all-to-all-done.2 = bf16[289,32,2]{0,2,1:T(2,128)(2,1)S(1)} async-done(((bf16[289,32,2]{0,2,1:T(2,128)(2,1)}), bf16[289,32,2]{0,2,1:T(2,128)(2,1)S(1)}, u32[]{:S(2)}, u32[]{:S(2)}) %all-to-all-start.2) | async-done | bytes 37024 | tf_op jit(solution)/shard_map/all_to_all | solution.py:97
  48.1 6.3 %all-to-all-start = ((bf16[289,64,16]{0,2,1:T(8,128)(2,1)}), bf16[289,64,16]{0,2,1:T(8,128)(2,1)S(1)}, u32[]{:S(2)}, u32[]{:S(2)}) async-start(bf16[289,64,16]{0,2,1:T(8,128)(2,1)} %broadcast_select_fusion), calls=%async_computation | async-start | bytes 1572864 | tf_op jit(solution)/shard_map/all_to_all | solution.py:119
  54.5 0.0 copy-done
  54.5 0.0 copy-start.5
  54.6 2.8 %copy.37 = bf16[8,289,289]{1,2,0:T(8,128)(2,1)} copy(bf16[8,289,289]{2,0,1:T(8,128)(2,1)S(1)} %copy-done) | data formatting | bytes 2672672 | tf_op args[3]
  57.3 0.0 copy-done.5
  57.3 0.2 fusion.56
  57.5 6.8 %gather_fusion.1 = bf16[8,289,289]{2,0,1:T(8,128)(2,1)} fusion(bf16[8,289,289]{2,0,1:T(8,128)(2,1)S(1)} %copy-done, s32[1024]{0:T(1024)S(1)} %pad_clamp_fusion.1), kind=kCustom, calls=%fused_computation.1 | custom fusion | bytes 2672704 | tf_op jit(solution)/shard_map/jit(_take)/gather | solution.py:131
  64.3 4.2 %copy.46 = bf16[8,289,289]{1,0,2:T(8,128)(2,1)} copy(bf16[8,289,289]{2,0,1:T(8,128)(2,1)} %param.11) | data formatting | bytes 2672672 | tf_op args[2]
  68.6 3.4 %reshape.143 = bf16[2312,289]{0,1:T(8,128)(2,1)S(1)} reshape(bf16[8,289,289]{1,0,2:T(8,128)(2,1)} %copy.46) | data formatting | bytes 2672672 | tf_op jit(solution)/shard_map/reshape | solution.py:27
  72.0 0.8 pad.12.own_ref
  72.8 0.0 copy-start.2
  72.8 0.0 copy-start.3
  72.8 0.0 copy-start.6
  72.8 3.2 %pad.14.fs_ref = bf16[8,384,384]{2,1,0:T(8,128)(2,1)} pad(bf16[8,289,289]{2,1,0:T(8,128)(2,1)} %bitcast.98, bf16[]{:T(256)} %constant.75.clone.1), padding=0_0x0_95x0_95 | pad | bytes 3695634 | tf_op jit(solution)/shard_map/jit(_pad)/pad | solution.py:71
  76.0 0.0 copy-done.2
  76.0 0.0 copy-done.3
  76.0 0.1 copy.32
  76.1 0.7 reshape.136.idx_ref
  76.9 0.0 copy-done.6
  76.9 0.2 fusion.57
  77.1 0.2 and_reduce_fusion
  77.3 1.9 %constant_dynamic-slice_fusion = bf16[1,289,289]{2,0,1:T(2,128)(2,1)S(1)} fusion(bf16[8,289,289]{2,0,1:T(8,128)(2,1)} %param.11, s32[]{:T(128)S(6)} %select_n.73), kind=kLoop, calls=%fused_computation.58 | loop fusion | bytes 334088 | tf_op jit(solution)/shard_map/dynamic_slice | solution.py:139
  79.3 3.0 %select_bitcast_fusion = bf16[289,8,289]{2,1,0:T(8,128)(2,1)} fusion(bf16[8,289,289]{2,0,1:T(8,128)(2,1)} %gather_fusion.1, pred[8]{0:T(512)(128)(4,1)S(1)} %get-tuple-element.6), kind=kLoop, calls=%fused_computation.10 | loop fusion | flops 668168 | bytes 2672680 | tf_op jit(solution)/shard_map/jit(_take)/select_n | solution.py:131
  82.3 0.6 gather_fusion.2
  82.9 0.1 select_bitcast_fusion.1
  83.0 2.1 %fusion.40 = bf16[289]{0:T(512)(128)(2,1)S(1)} fusion(bf16[289,8,289]{2,1,0:T(8,128)(2,1)} %select_bitcast_fusion, bf16[8,289,1]{1,0,2:T(8,128)(2,1)S(1)} %select_bitcast_fusion.1), kind=kOutput, calls=%fused_computation.28 | convolution fusion | flops 1336336 | bytes 1341538 | tf_op jit(solution)/shard_map/dot_general | solution.py:136
  85.1 0.2 convolution_reduce_fusion
  85.3 2.2 %fusion.1 = bf16[1,8,289]{2,0,1:T(2,128)(2,1)S(1)} fusion(bf16[289,1,1]{0,1,2:T(2,128)(2,1)S(1)} %reshape.179, bf16[8,289,289]{2,0,1:T(8,128)(2,1)} %param.11), kind=kOutput, calls=%fused_computation.6 | convolution fusion | flops 1336336 | bytes 1341538 | tf_op jit(solution)/shard_map/dot_general | solution.py:26
  87.5 0.3 fusion
  87.8 0.1 convert_element_type.74
  88.0 1.2 %convolution_bitcast_fusion = f32[2312,64]{0,1:T(8,128)} fusion(bf16[2312,289]{0,1:T(8,128)(2,1)S(1)} %reshape.143, bf16[8,289,8]{1,0,2:T(8,128)(2,1)S(1)} %convert_element_type.74), kind=kOutput, calls=%fused_computation.3 | convolution fusion | flops 85525504 | bytes 1965200 | tf_op jit(solution)/shard_map/dot_general | solution.py:26
  89.2 1.5 %reshape.144 = f32[8,289,64]{1,0,2:T(8,128)S(1)} reshape(f32[2312,64]{0,1:T(8,128)} %convolution_bitcast_fusion) | data formatting | bytes 1183744 | tf_op jit(solution)/shard_map/reshape | solution.py:29
  90.7 1.1 copy.47.chain_ref
  91.7 5.3 %all-to-all-done = bf16[289,64,16]{0,2,1:T(8,128)(2,1)S(1)} async-done(((bf16[289,64,16]{0,2,1:T(8,128)(2,1)}), bf16[289,64,16]{0,2,1:T(8,128)(2,1)S(1)}, u32[]{:S(2)}, u32[]{:S(2)}) %all-to-all-start) | async-done | bytes 591904 | tf_op jit(solution)/shard_map/all_to_all | solution.py:119
  97.1 1.0 pad.13.arr_ref
  98.1 15.6 %shard_map.91 = bf16[289,512]{1,0:T(8,128)(2,1)} custom-call(s32[8192]{0:T(1024)} %reshape.136.idx_ref, bf16[512,384]{1,0:T(8,128)(2,1)} %pad.12.own_ref, bf16[1024,384]{1,0:T(8,128)(2,1)} %pad.13.arr_ref, bf16[8,384,384]{2,1,0:T(8,128)(2,1)} %pad.14.fs_ref, f32[289,512]{1,0:T(8,128)} %copy.47.chain_ref), custom_call_target="tpu_custom_call" | custom-call | tf_op jit(solution)/shard_map/pallas_call | solution.py:73
  (10 shorter events, 0.1 us)
Async XLA Ops:
  0.0 3.5 %copy-start.1 = (bf16[8,289,289]{2,0,1:T(8,128)(2,1)S(1)}, bf16[8,289,289]{2,0,1:T(8,128)(2,1)}, u32[]{:S(2)}) copy-start(bf16[8,289,289]{2,0,1:T(8,128)(2,1)} %param.10) | copy-start | bytes 4009012
  3.5 17.0 %copy-start.4 = (s32[1,1,64,16]{2,3,1,0:T(8,128)S(1)}, s32[1,1,64,16]{2,3,1,0:T(8,128)}, u32[]{:S(2)}) copy-start(s32[1,1,64,16]{2,3,1,0:T(8,128)} %param.13) | copy-start | bytes 12292
  5.4 27.8 %all-to-all-start.1 = ((bf16[289,16,1]{0,2,1:T(2,128)(2,1)}), bf16[289,16,1]{0,2,1:T(2,128)(2,1)S(1)}, u32[]{:S(2)}, u32[]{:S(2)}) async-start(bf16[289,16,1]{0,2,1:T(2,128)(2,1)} %reshape.141), calls=%async_computation.1 | async-start | bytes 49152 | tf_op jit(solution)/shard_map/all_to_all | solution.py:97
  33.7 20.8 %copy-start = (bf16[8,289,289]{2,0,1:T(8,128)(2,1)S(1)}, bf16[8,289,289]{2,0,1:T(8,128)(2,1)}, u32[]{:S(2)}) copy-start(bf16[8,289,289]{2,0,1:T(8,128)(2,1)} %param.12) | copy-start | bytes 4009012
  34.4 13.7 %all-to-all-start.2 = ((bf16[289,32,2]{0,2,1:T(2,128)(2,1)}), bf16[289,32,2]{0,2,1:T(2,128)(2,1)S(1)}, u32[]{:S(2)}, u32[]{:S(2)}) async-start(bf16[289,32,2]{0,2,1:T(2,128)(2,1)} %broadcast_in_dim.45), calls=%async_computation.2 | async-start | bytes 98304 | tf_op jit(solution)/shard_map/all_to_all | solution.py:97
  48.1 48.9 %all-to-all-start = ((bf16[289,64,16]{0,2,1:T(8,128)(2,1)}), bf16[289,64,16]{0,2,1:T(8,128)(2,1)S(1)}, u32[]{:S(2)}, u32[]{:S(2)}) async-start(bf16[289,64,16]{0,2,1:T(8,128)(2,1)} %broadcast_select_fusion), calls=%async_computation | async-start | bytes 1572864 | tf_op jit(solution)/shard_map/all_to_all | solution.py:119
  54.5 2.8 %copy-start.5 = (s32[8,64]{1,0:T(8,128)S(1)}, s32[8,64]{1,0:T(8,128)}, u32[]{:S(2)}) copy-start(s32[8,64]{1,0:T(8,128)} %param.17) | copy-start | bytes 6148
  72.8 3.2 %copy-start.2 = (s32[16,512]{1,0:T(8,128)S(1)}, s32[16,512]{1,0:T(8,128)}, u32[]{:S(2)}) copy-start(s32[16,512]{1,0:T(8,128)} %param.14) | copy-start | bytes 98308
  72.8 3.2 %copy-start.3 = (s32[16,512]{1,0:T(8,128)S(1)}, s32[16,512]{1,0:T(8,128)}, u32[]{:S(2)}) copy-start(s32[16,512]{1,0:T(8,128)} %param.15) | copy-start | bytes 98308
  72.8 4.1 %copy-start.6 = (s32[8,64]{1,0:T(8,128)S(1)}, s32[8,64]{1,0:T(8,128)}, u32[]{:S(2)}) copy-start(s32[8,64]{1,0:T(8,128)} %param.16) | copy-start | bytes 6148

commit v16 on v14

--- a/solution.py
+++ b/solution.py
@@ -45,9 +45,13 @@
 
     def body(t, carry):
         base = t * lists
+        half = lists // 2
         acc = table_ref[pl.ds(idx_ref[base], CHUNKS), :]
-        for l in range(1, lists):
+        other = table_ref[pl.ds(idx_ref[base + half], CHUNKS), :]
+        for l in range(1, half):
             acc = acc + table_ref[pl.ds(idx_ref[base + l], CHUNKS), :]
+            other = other + table_ref[pl.ds(idx_ref[base + half + l], CHUNKS), :]
+        acc = acc + other
         acc_ref[pl.ds(t * CHUNKS, CHUNKS), :] = acc
         return carry
 

time: 114 us -> 114 us (level)
  no operation moved by 1% of the time
where the time goes in v16:
time: 114 us
  local copies, waits for them, and re-layouts  35.2 us (31%)
  starting transfers between devices  29.1 us (26%)
  waiting for transfers between devices  18.7 us (16%)
  Pallas kernels  15.6 us (14%)
  matrix products  9.99 us (9%)
  other arithmetic  4.84 us (4%)
    all_to_all x2, starting transfers between devices, gather_columns(): return lax.all_to_all(spread, axes, split_axis=1, concat_axis=1, tiled=True)  22.7 us
    pallas_call x1, Pallas kernels, far_field(): pl.pallas_call(far_kernel, out_shape=jax.ShapeDtypeStruct((coefs, targets...  15.6 us
    all_to_all x2, waiting for transfers between devices, gather_columns(): return lax.all_to_all(spread, axes, split_axis=1, concat_axis=1, tiled=True)  13.4 us
    unnamed x19, local copies, waits for them, and re-layouts  8.42 us
    gather x1, local copies, waits for them, and re-layouts, on_device(): jnp.take(far_shift, coarse_kinds, axis=0).transpose(1, 0, 2)  6.83 us
    all_to_all x1, starting transfers between devices, on_device(): lax.all_to_all(outgoing, ('gy', 'gz'), split_axis=1, concat_axis=1, tiled...  6.35 us
    all_to_all x1, waiting for transfers between devices, on_device(): lax.all_to_all(outgoing, ('gy', 'gz'), split_axis=1, concat_axis=1, tiled...  5.33 us
    dot_general x4, matrix products, lift_level(): lax.dot_general(up_shift, child_stack, (((2,), (1,)), ((0,), (0,))), pref...  3.99 us
  transfers between devices with their start and end apart: 3, of which 3 were waited for; matrix products, arithmetic and copies ran while one was open for 37% of the time, Pallas kernels for 0%

profile of v16, /device:TPU:8, one launch (start us, length us, event | category | flops | bytes accessed | tf_op | source)
XLA Modules:
  0.0 113.7 jit_solution(7429789425447150852)
XLA Ops:
  0.0 0.0 copy-start.1
  0.0 1.3 %copy.33 = bf16[289,512]{0,1:T(8,128)(2,1)S(1)} copy(bf16[289,512]{1,0:T(8,128)(2,1)} %param.9) | data formatting | bytes 591872 | tf_op args[0]
  1.3 2.2 %fusion.19 = bf16[289,8,8]{0,2,1:T(8,128)(2,1)S(1)} fusion(bf16[8,289,289]{2,0,1:T(8,128)(2,1)} %param.10, bf16[8,289,64]{1,0,2:T(8,128)(2,1)S(1)} %bitcast.96), kind=kOutput, calls=%fused_computation.21 | convolution fusion | flops 85544000 | bytes 1669264 | tf_op jit(solution)/shard_map/dot_general | solution.py:17
  3.5 0.0 copy-done.1
  3.5 0.0 copy-start.4
  3.6 0.6 fusion.28
  4.1 0.6 fusion.37
  4.8 0.6 reshape.141
  5.4 15.2 %all-to-all-start.1 = ((bf16[289,16,1]{0,2,1:T(2,128)(2,1)}), bf16[289,16,1]{0,2,1:T(2,128)(2,1)S(1)}, u32[]{:S(2)}, u32[]{:S(2)}) async-start(bf16[289,16,1]{0,2,1:T(2,128)(2,1)} %reshape.141), calls=%async_computation.1 | async-start | bytes 49152 | tf_op jit(solution)/shard_map/all_to_all | solution.py:101
  20.6 0.0 copy-done.4
  20.6 0.1 copy.35
  20.7 0.1 reshape.138
  20.8 3.9 %gather_fusion = bf16[1024,289]{1,0:T(8,128)(2,1)S(1)} fusion(bf16[289,512]{0,1:T(8,128)(2,1)S(1)} %copy.33, s32[1024]{0:T(1024)S(1)} %broadcast_clamp_fusion), kind=kCustom, calls=%fused_computation | custom fusion | bytes 1187840 | tf_op jit(solution)/shard_map/jit(_take)/gather | solution.py:122
  24.7 0.1 copy.34
  24.8 8.3 %all-to-all-done.1 = bf16[289,16,1]{0,2,1:T(2,128)(2,1)S(1)} async-done(((bf16[289,16,1]{0,2,1:T(2,128)(2,1)}), bf16[289,16,1]{0,2,1:T(2,128)(2,1)S(1)}, u32[]{:S(2)}, u32[]{:S(2)}) %all-to-all-start.1) | async-done | bytes 9280 | tf_op jit(solution)/shard_map/all_to_all | solution.py:101
  33.2 0.6 fusion.43
  33.7 0.0 copy-start
  33.8 0.7 broadcast_in_dim.45
  34.4 7.5 %all-to-all-start.2 = ((bf16[289,32,2]{0,2,1:T(2,128)(2,1)}), bf16[289,32,2]{0,2,1:T(2,128)(2,1)S(1)}, u32[]{:S(2)}, u32[]{:S(2)}) async-start(bf16[289,32,2]{0,2,1:T(2,128)(2,1)} %broadcast_in_dim.45), calls=%async_computation.2 | async-start | bytes 98304 | tf_op jit(solution)/shard_map/all_to_all | solution.py:101
  42.0 1.1 broadcast_select_fusion
  43.1 5.1 %all-to-all-done.2 = bf16[289,32,2]{0,2,1:T(2,128)(2,1)S(1)} async-done(((bf16[289,32,2]{0,2,1:T(2,128)(2,1)}), bf16[289,32,2]{0,2,1:T(2,128)(2,1)S(1)}, u32[]{:S(2)}, u32[]{:S(2)}) %all-to-all-start.2) | async-done | bytes 37024 | tf_op jit(solution)/shard_map/all_to_all | solution.py:101
  48.1 6.3 %all-to-all-start = ((bf16[289,64,16]{0,2,1:T(8,128)(2,1)}), bf16[289,64,16]{0,2,1:T(8,128)(2,1)S(1)}, u32[]{:S(2)}, u32[]{:S(2)}) async-start(bf16[289,64,16]{0,2,1:T(8,128)(2,1)} %broadcast_select_fusion), calls=%async_computation | async-start | bytes 1572864 | tf_op jit(solution)/shard_map/all_to_all | solution.py:123
  54.5 0.0 copy-done
  54.5 0.0 copy-start.5
  54.6 2.8 %copy.37 = bf16[8,289,289]{1,2,0:T(8,128)(2,1)} copy(bf16[8,289,289]{2,0,1:T(8,128)(2,1)S(1)} %copy-done) | data formatting | bytes 2672672 | tf_op args[3]
  57.3 0.0 copy-done.5
  57.3 0.2 fusion.56
  57.5 6.8 %gather_fusion.1 = bf16[8,289,289]{2,0,1:T(8,128)(2,1)} fusion(bf16[8,289,289]{2,0,1:T(8,128)(2,1)S(1)} %copy-done, s32[1024]{0:T(1024)S(1)} %pad_clamp_fusion.1), kind=kCustom, calls=%fused_computation.1 | custom fusion | bytes 2672704 | tf_op jit(solution)/shard_map/jit(_take)/gather | solution.py:135
  64.3 4.2 %copy.46 = bf16[8,289,289]{1,0,2:T(8,128)(2,1)} copy(bf16[8,289,289]{2,0,1:T(8,128)(2,1)} %param.11) | data formatting | bytes 2672672 | tf_op args[2]
  68.6 3.4 %reshape.143 = bf16[2312,289]{0,1:T(8,128)(2,1)S(1)} reshape(bf16[8,289,289]{1,0,2:T(8,128)(2,1)} %copy.46) | data formatting | bytes 2672672 | tf_op jit(solution)/shard_map/reshape | solution.py:27
  72.0 0.8 pad.12.own_ref
  72.8 0.0 copy-start.2
  72.8 0.0 copy-start.3
  72.8 0.0 copy-start.6
  72.8 3.2 %pad.14.fs_ref = bf16[8,384,384]{2,1,0:T(8,128)(2,1)} pad(bf16[8,289,289]{2,1,0:T(8,128)(2,1)} %bitcast.98, bf16[]{:T(256)} %constant.75.clone.1), padding=0_0x0_95x0_95 | pad | bytes 3695634 | tf_op jit(solution)/shard_map/jit(_pad)/pad | solution.py:75
  76.0 0.0 copy-done.2
  76.0 0.0 copy-done.3
  76.0 0.1 copy.32
  76.1 0.7 reshape.136.idx_ref
  76.9 0.0 copy-done.6
  76.9 0.2 fusion.57
  77.1 0.2 and_reduce_fusion
  77.3 1.9 %constant_dynamic-slice_fusion = bf16[1,289,289]{2,0,1:T(2,128)(2,1)S(1)} fusion(bf16[8,289,289]{2,0,1:T(8,128)(2,1)} %param.11, s32[]{:T(128)S(6)} %select_n.73), kind=kLoop, calls=%fused_computation.58 | loop fusion | bytes 334088 | tf_op jit(solution)/shard_map/dynamic_slice | solution.py:143
  79.3 3.0 %select_bitcast_fusion = bf16[289,8,289]{2,1,0:T(8,128)(2,1)} fusion(bf16[8,289,289]{2,0,1:T(8,128)(2,1)} %gather_fusion.1, pred[8]{0:T(512)(128)(4,1)S(1)} %get-tuple-element.6), kind=kLoop, calls=%fused_computation.10 | loop fusion | flops 668168 | bytes 2672680 | tf_op jit(solution)/shard_map/jit(_take)/select_n | solution.py:135
  82.3 0.6 gather_fusion.2
  82.9 0.1 select_bitcast_fusion.1
  83.0 2.1 %fusion.40 = bf16[289]{0:T(512)(128)(2,1)S(1)} fusion(bf16[289,8,289]{2,1,0:T(8,128)(2,1)} %select_bitcast_fusion, bf16[8,289,1]{1,0,2:T(8,128)(2,1)S(1)} %select_bitcast_fusion.1), kind=kOutput, calls=%fused_computation.28 | convolution fusion | flops 1336336 | bytes 1341538 | tf_op jit(solution)/shard_map/dot_general | solution.py:140
  85.1 0.2 convolution_reduce_fusion
  85.3 2.2 %fusion.1 = bf16[1,8,289]{2,0,1:T(2,128)(2,1)S(1)} fusion(bf16[289,1,1]{0,1,2:T(2,128)(2,1)S(1)} %reshape.179, bf16[8,289,289]{2,0,1:T(8,128)(2,1)} %param.11), kind=kOutput, calls=%fused_computation.6 | convolution fusion | flops 1336336 | bytes 1341538 | tf_op jit(solution)/shard_map/dot_general | solution.py:26
  87.5 0.3 fusion
  87.8 0.1 convert_element_type.74
  88.0 1.2 %convolution_bitcast_fusion = f32[2312,64]{0,1:T(8,128)} fusion(bf16[2312,289]{0,1:T(8,128)(2,1)S(1)} %reshape.143, bf16[8,289,8]{1,0,2:T(8,128)(2,1)S(1)} %convert_element_type.74), kind=kOutput, calls=%fused_computation.3 | convolution fusion | flops 85525504 | bytes 1965200 | tf_op jit(solution)/shard_map/dot_general | solution.py:26
  89.2 1.5 %reshape.144 = f32[8,289,64]{1,0,2:T(8,128)S(1)} reshape(f32[2312,64]{0,1:T(8,128)} %convolution_bitcast_fusion) | data formatting | bytes 1183744 | tf_op jit(solution)/shard_map/reshape | solution.py:29
  90.7 1.1 copy.47.chain_ref
  91.7 5.3 %all-to-all-done = bf16[289,64,16]{0,2,1:T(8,128)(2,1)S(1)} async-done(((bf16[289,64,16]{0,2,1:T(8,128)(2,1)}), bf16[289,64,16]{0,2,1:T(8,128)(2,1)S(1)}, u32[]{:S(2)}, u32[]{:S(2)}) %all-to-all-start) | async-done | bytes 591904 | tf_op jit(solution)/shard_map/all_to_all | solution.py:123
  97.1 1.0 pad.13.arr_ref
  98.1 15.6 %shard_map.91 = bf16[289,512]{1,0:T(8,128)(2,1)} custom-call(s32[8192]{0:T(1024)} %reshape.136.idx_ref, bf16[512,384]{1,0:T(8,128)(2,1)} %pad.12.own_ref, bf16[1024,384]{1,0:T(8,128)(2,1)} %pad.13.arr_ref, bf16[8,384,384]{2,1,0:T(8,128)(2,1)} %pad.14.fs_ref, f32[289,512]{1,0:T(8,128)} %copy.47.chain_ref), custom_call_target="tpu_custom_call" | custom-call | tf_op jit(solution)/shard_map/pallas_call | solution.py:77
  (10 shorter events, 0.1 us)
Async XLA Ops:
  0.0 3.5 %copy-start.1 = (bf16[8,289,289]{2,0,1:T(8,128)(2,1)S(1)}, bf16[8,289,289]{2,0,1:T(8,128)(2,1)}, u32[]{:S(2)}) copy-start(bf16[8,289,289]{2,0,1:T(8,128)(2,1)} %param.10) | copy-start | bytes 4009012
  3.5 17.0 %copy-start.4 = (s32[1,1,64,16]{2,3,1,0:T(8,128)S(1)}, s32[1,1,64,16]{2,3,1,0:T(8,128)}, u32[]{:S(2)}) copy-start(s32[1,1,64,16]{2,3,1,0:T(8,128)} %param.13) | copy-start | bytes 12292
  5.4 27.8 %all-to-all-start.1 = ((bf16[289,16,1]{0,2,1:T(2,128)(2,1)}), bf16[289,16,1]{0,2,1:T(2,128)(2,1)S(1)}, u32[]{:S(2)}, u32[]{:S(2)}) async-start(bf16[289,16,1]{0,2,1:T(2,128)(2,1)} %reshape.141), calls=%async_computation.1 | async-start | bytes 49152 | tf_op jit(solution)/shard_map/all_to_all | solution.py:101
  33.7 20.8 %copy-start = (bf16[8,289,289]{2,0,1:T(8,128)(2,1)S(1)}, bf16[8,289,289]{2,0,1:T(8,128)(2,1)}, u32[]{:S(2)}) copy-start(bf16[8,289,289]{2,0,1:T(8,128)(2,1)} %param.12) | copy-start | bytes 4009012
  34.4 13.7 %all-to-all-start.2 = ((bf16[289,32,2]{0,2,1:T(2,128)(2,1)}), bf16[289,32,2]{0,2,1:T(2,128)(2,1)S(1)}, u32[]{:S(2)}, u32[]{:S(2)}) async-start(bf16[289,32,2]{0,2,1:T(2,128)(2,1)} %broadcast_in_dim.45), calls=%async_computation.2 | async-start | bytes 98304 | tf_op jit(solution)/shard_map/all_to_all | solution.py:101
  48.1 48.9 %all-to-all-start = ((bf16[289,64,16]{0,2,1:T(8,128)(2,1)}), bf16[289,64,16]{0,2,1:T(8,128)(2,1)S(1)}, u32[]{:S(2)}, u32[]{:S(2)}) async-start(bf16[289,64,16]{0,2,1:T(8,128)(2,1)} %broadcast_select_fusion), calls=%async_computation | async-start | bytes 1572864 | tf_op jit(solution)/shard_map/all_to_all | solution.py:123
  54.5 2.8 %copy-start.5 = (s32[8,64]{1,0:T(8,128)S(1)}, s32[8,64]{1,0:T(8,128)}, u32[]{:S(2)}) copy-start(s32[8,64]{1,0:T(8,128)} %param.17) | copy-start | bytes 6148
  72.8 3.2 %copy-start.2 = (s32[16,512]{1,0:T(8,128)S(1)}, s32[16,512]{1,0:T(8,128)}, u32[]{:S(2)}) copy-start(s32[16,512]{1,0:T(8,128)} %param.14) | copy-start | bytes 98308
  72.8 3.2 %copy-start.3 = (s32[16,512]{1,0:T(8,128)S(1)}, s32[16,512]{1,0:T(8,128)}, u32[]{:S(2)}) copy-start(s32[16,512]{1,0:T(8,128)} %param.15) | copy-start | bytes 98308
  72.8 4.1 %copy-start.6 = (s32[8,64]{1,0:T(8,128)S(1)}, s32[8,64]{1,0:T(8,128)}, u32[]{:S(2)}) copy-start(s32[8,64]{1,0:T(8,128)} %param.16) | copy-start | bytes 6148
